TPU v7x, 256 devices: a whole 4x4x8 slice. The times are simulated.
256 devices in a mesh: wide: 32 (over y, z), deep: 8 (over x, core).
Axes of the slice: x: 4, y: 4, z: 8, core: 2. Of those that a mesh axis runs over, the one named last changes fastest.
Arguments:
- rhs_local: float32 [512, 128, 256], P('wide', 'deep'), may hold values from -6 to 6
- metric: float32 [3, 512, 128, 256], P(None, 'wide', 'deep'), may hold values from 0.005 to 0.05
- helm: float32 [512, 128, 256], P('wide', 'deep'), may hold values from 0.5 to 4
- columns: int32 [32, 16, 8, 8], P('wide', 'deep'), may hold values from 0 to 47
- live_blocks: int32 [32, 16, 8], P('wide', 'deep'), may hold values from 1 to 8
- block_values: float32 [32, 16, 8, 512], P('wide', 'deep'), may hold values from -0.0234375 to 0.0234375
Outputs:
- smoothed: float32 [512, 128, 256], P('wide', 'deep')
- coarse_product: float32 [32, 16, 64], P('wide', 'deep')
All inputs are finite; a program needn't handle non-finite values.
Results may differ from a plain program's by a relative error of at most 0.00013.
Values sent between devices are 32-bit elements; how exact they have to be, the bound alone decides.
No kernel may reach another device: no remote copies, remote signals or barrier semaphores. Data moves between devices by JAX's collectives and lax.ppermute only.
A program may use at most 64 MiB of HBM per device.

v0:
```python
import jax
import jax.numpy as jnp
import numpy as np
from jax import lax
from jax.sharding import PartitionSpec as P

NP = 8
K = 8
BS = 8


upper_bound = 6.0
lower_bound = 0.6
highest = lax.Precision.HIGHEST


def gll_tables(count):
    order = count - 1
    nodes = np.cos(np.pi * np.arange(count) / order)
    legendre = np.zeros((count, count))
    for sweep in range(101):
        legendre[:, 0] = 1.0
        legendre[:, 1] = nodes
        for degree in range(2, count):
            legendre[:, degree] = (
                (2 * degree - 1) * nodes * legendre[:, degree - 1]
                - (degree - 1) * legendre[:, degree - 2]
            ) / degree
        if sweep < 100:
            nodes = nodes - (nodes * legendre[:, order] - legendre[:, order - 1]) / (
                count * legendre[:, order]
            )
    nodes = nodes[::-1].copy()
    values = legendre[::-1, order].copy()
    identity_table = np.eye(count)
    spacing = nodes[:, None] - nodes[None, :] + identity_table
    derivative = values[:, None] / values[None, :] / spacing
    derivative = derivative * (1.0 - identity_table)
    derivative[0, 0] = -order * (order + 1) / 4.0
    derivative[-1, -1] = order * (order + 1) / 4.0
    linear = np.stack([(1.0 - nodes) / 2.0, (1.0 + nodes) / 2.0], axis=1)
    return (np.asarray(derivative, np.float32), np.asarray(linear, np.float32))


def block_extent():
    return 128


def repeat_table(small, copies):
    return jnp.asarray(np.kron(np.eye(copies, dtype=np.float32), small))


def contract(field, table, axis):
    if axis == 0:
        return jnp.einsum("mi,iyz->myz", table, field, precision=highest)
    if axis == 1:
        return jnp.einsum("mj,xjz->xmz", table, field, precision=highest)
    shape = field.shape
    blocked = table.shape[1]
    grid = field.reshape(shape[0], shape[1], shape[2] // blocked, blocked)
    result = jnp.einsum("mk,xynk->xynm", table, grid, precision=highest)
    return result.reshape(shape[0], shape[1], -1)


def shift(value, dw, dd):
    nw = lax.axis_size("wide")
    nd = lax.axis_size("deep")
    if dd == 0:
        pairs = [((w + dw) % nw, w) for w in range(nw)]
        return lax.ppermute(value, "wide", pairs)
    if dw == 0:
        pairs = [((d + dd) % nd, d) for d in range(nd)]
        return lax.ppermute(value, "deep", pairs)
    pairs = []
    for w in range(nw):
        for d in range(nd):
            src = ((w + dw) % nw) * nd + (d + dd) % nd
            pairs.append((src, w * nd + d))
    return lax.ppermute(value, ("wide", "deep"), pairs)


def node_mask(length, count, node, axis, ndim):
    index = lax.broadcasted_iota(jnp.int32, (length,), 0) % count == node
    shape = [1] * ndim
    shape[axis] = length
    return index.reshape(shape)


def assemble(field, count, carry=None):
    nd = field.ndim
    X, Y, Z = field.shape[-3:]
    lx = shift(field[..., -1, :, :], -1, 0)
    rx = shift(field[..., 0, :, :], 1, 0)
    ext = jnp.concatenate([lx[..., None, :, :], field, rx[..., None, :, :]], axis=-3)
    hi = node_mask(X, count, count - 1, nd - 3, nd)
    lo = node_mask(X, count, 0, nd - 3, nd)
    field = (
        ext[..., 1 : X + 1, :, :]
        + jnp.where(hi, ext[..., 2 : X + 2, :, :], 0.0)
        + jnp.where(lo, ext[..., 0:X, :, :], 0.0)
    )
    ly = shift(field[..., :, -1, :], 0, -1)
    face = field[..., :, 0, :]
    carried = None
    if carry is None:
        ry = shift(face, 0, 1)
    else:
        packed = shift(jnp.concatenate([face.reshape(-1), carry]), 0, 1)
        ry = packed[: face.size].reshape(face.shape)
        carried = packed[face.size :]
    ext = jnp.concatenate([ly[..., :, None, :], field, ry[..., :, None, :]], axis=-2)
    hi = node_mask(Y, count, count - 1, nd - 2, nd)
    lo = node_mask(Y, count, 0, nd - 2, nd)
    field = (
        ext[..., :, 1 : Y + 1, :]
        + jnp.where(hi, ext[..., :, 2 : Y + 2, :], 0.0)
        + jnp.where(lo, ext[..., :, 0:Y, :], 0.0)
    )
    hi = node_mask(Z, count, count - 1, nd - 1, nd)
    lo = node_mask(Z, count, 0, nd - 1, nd)
    field = (
        field
        + jnp.where(hi, jnp.roll(field, -1, axis=-1), 0.0)
        + jnp.where(lo, jnp.roll(field, 1, axis=-1), 0.0)
    )
    if carry is None:
        return field
    return field, carried


def apply_operator(field, metric, helm, tables):
    total = helm * field
    for axis in range(3):
        slope = contract(field, tables[axis], axis)
        total = total + contract(metric[axis] * slope, tables[axis].T, axis)
    return total


def chebyshev(solution, rhs_local, metric, helm, tables, inverse, first_residual):
    centre = (upper_bound + lower_bound) / 2.0
    half_width = (upper_bound - lower_bound) / 2.0
    aspect = centre / half_width
    weight_prev = 1.0 / aspect
    if first_residual is not None:
        residual = first_residual
    else:
        residual = assemble(rhs_local - apply_operator(solution, metric, helm, tables), NP)
    update = inverse * residual / centre
    solution = solution + update
    residual = assemble(rhs_local - apply_operator(solution, metric, helm, tables), NP)
    weight_next = 1.0 / (2.0 * aspect - weight_prev)
    update = (
        weight_next * weight_prev * update + 2.0 * weight_next / half_width * inverse * residual
    )
    solution = solution + update
    return solution


def local(rhs_local, metric, helm, columns, live_blocks, block_values):
    derivative, linear = gll_tables(NP)
    shape = rhs_local.shape
    nw = lax.axis_size("wide")
    copies = (shape[0] // NP, shape[1] // NP, block_extent() // NP)
    tables = tuple((repeat_table(derivative, copies[axis]) for axis in range(3)))
    square_tables = tuple(
        (repeat_table(derivative * derivative, copies[axis]) for axis in range(3))
    )
    down_tables = tuple((repeat_table(linear.T, copies[axis]) for axis in range(3)))
    up_tables = tuple((repeat_table(linear, copies[axis]) for axis in range(3)))

    diagonal = helm
    for axis in range(3):
        diagonal = diagonal + contract(metric[axis], square_tables[axis].T, axis)
    mats = jnp.concatenate(
        [
            block_values[0, 0].reshape(-1),
            columns[0, 0].astype(jnp.float32).reshape(-1),
            live_blocks[0, 0].astype(jnp.float32),
        ]
    )
    both, mats = assemble(jnp.stack([diagonal, rhs_local]), NP, mats)
    nvals = block_values.shape[2] * block_values.shape[3]
    ncols = columns.shape[2] * columns.shape[3]
    next_values = mats[:nvals].reshape(block_values.shape[2:])
    next_columns = mats[nvals : nvals + ncols].astype(jnp.int32).reshape(columns.shape[2:])
    next_live = mats[nvals + ncols :].astype(jnp.int32)
    inverse = 1.0 / both[0]
    first = chebyshev(
        jnp.zeros_like(rhs_local), rhs_local, metric, helm, tables, inverse, both[1]
    )
    local_res = rhs_local - apply_operator(first, metric, helm, tables)
    corners = local_res
    for axis in range(3):
        corners = contract(corners, down_tables[axis], axis)

    cx, cy, cz = corners.shape
    ext = jnp.concatenate([shift(corners, 0, -1), corners, shift(corners, 0, 1)], axis=1)
    qz = ext[:, :, 0::2] + jnp.roll(ext, 1, axis=2)[:, :, 0::2]
    qy = qz[:, cy : cy + 7 : 2] + qz[:, cy - 1 : cy + 6 : 2]
    zero = jnp.zeros_like(qy[:1])
    qx = jnp.concatenate([zero, qy, zero], axis=0)
    partial = qx[1 : cx + 2 : 2] + qx[0 : cx + 1 : 2]

    sent = jnp.stack(
        [jnp.roll(partial, 1, axis=2), partial, jnp.roll(partial, -1, axis=2)], axis=-1
    )
    sent = jnp.transpose(sent, (2, 0, 1, 3))
    got = lax.all_to_all(sent, "wide", 0, 0, tiled=True)
    even = got[:, 0] + jnp.roll(got[:, 2], 1, axis=0)
    got = jnp.stack([even, got[:, 1]], axis=1)
    frame = jnp.transpose(got, (3, 2, 0, 1)).reshape(3, 4, -1)
    span = frame.shape[2]
    nxb = span // BS
    frame_rows = frame.reshape(-1, BS)

    cols = jnp.concatenate([columns[0], next_columns[None]], axis=0)
    lives = jnp.concatenate([live_blocks[0], next_live[None]], axis=0)
    vals = jnp.concatenate([block_values[0], next_values[None]], axis=0)
    y_off = jnp.array([0, 0, 2], jnp.int32)[:, None, None]
    layer = cols // (2 * nxb)
    block = cols % (2 * nxb)
    index = (layer * 4 + y_off + block // nxb) * nxb + block % nxb
    picked = jnp.take(frame_rows, index.reshape(-1), axis=0).reshape(index.shape + (BS,))
    live = (jnp.arange(K, dtype=jnp.int32)[None, None, :] < lives[:, :, None]).astype(
        jnp.float32
    )
    values = vals.reshape(vals.shape[:2] + (K, BS, BS))
    product = jnp.einsum("yxkij,yxkj,yxk->yxi", values, picked, live, precision=highest)
    product = product.reshape(3, span)
    coarse_product = product[:2].reshape(1, 2, span)

    pick = (2 * np.arange(nw)[:, None] + np.arange(3)[None, :]) % span
    back = jnp.transpose(product[:, pick], (1, 0, 2))
    got = lax.all_to_all(back, "wide", 0, 0, tiled=True)
    hx = jnp.stack([got[:, :, 0:2], got[:, :, 1:3]], axis=-1).reshape(nw, 3, 4)
    hy = jnp.stack([hx[:, 0:2], hx[:, 1:3]], axis=2).reshape(nw, 4, 4)
    hz = jnp.stack([hy, jnp.roll(hy, -1, axis=0)], axis=1).reshape(2 * nw, 4, 4)
    correction = jnp.transpose(hz, (2, 1, 0))
    for axis in range(3):
        correction = contract(correction, up_tables[axis], axis)
    second = first + correction
    smoothed = chebyshev(second, rhs_local, metric, helm, tables, inverse, None)
    return (smoothed, coarse_product)


def solution(mesh):
    placed = (
        P("wide", "deep", None),
        P(None, "wide", "deep", None),
        P("wide", "deep", None),
        P("wide", "deep", None, None),
        P("wide", "deep", None),
        P("wide", "deep", None, None),
    )
    return jax.shard_map(
        local,
        mesh=mesh,
        in_specs=placed,
        out_specs=(P("wide", "deep", None), P("wide", "deep", None)),
        check_vma=False,
    )
```

profile of v0, /device:TPU:7, one launch (start us, length us, event | category | flops | bytes accessed | tf_op | source)
XLA Modules:
  0.0 133.8 jit_solution(12215007336732400334)
XLA Ops:
  0.6 1.1 fusion.111
  4.9 0.8 copy-done.1
  5.7 0.7 fusion.10
  6.5 8.1 %collective-permute-start = (f32[2,16,256]{2,1,0:T(8,128)S(1)}, f32[2,16,256]{2,1,0:T(8,128)S(1)}, u32[]{:S(2)}, u32[]{:S(2)}) collective-permute-start(f32[2,16,256]{2,1,0:T(8,128)S(1)} %bitcast.317), channel_id=1, source_target_pairs={{8,0},{16,8},{24,16},{32,24},{40,32},{48,40},{56,48},{64,56},{72,6... | collective-permute-start | bytes 98312 | tf_op jit(solution)/shard_map/ppermute | solution.py:70
  16.9 3.9 %collective-permute-done.1 = f32[2,16,256]{2,1,0:T(8,128)S(1)} collective-permute-done((f32[2,16,256]{2,1,0:T(8,128)S(1)}, f32[2,16,256]{2,1,0:T(8,128)S(1)}, u32[]{:S(2)}, u32[]{:S(2)}) %collective-permute-start.1) | collective-permute-done | bytes 32800 | tf_op jit(solution)/shard_map/ppermute | solution.py:70
  21.2 2.1 %collective-permute-start.2 = (f32[12360]{0:T(1024)S(1)}, f32[12360]{0:T(1024)S(1)}, u32[]{:S(2)}, u32[]{:S(2)}) collective-permute-start(f32[12360]{0:T(1024)S(1)} %concatenate.132), channel_id=1, source_target_pairs={{1,0},{2,1},{3,2},{4,3},{5,4},{6,5},{7,6},{0,7},{9,8},{10,9},{11,1... | collective-permute-start | bytes 148328 | tf_op jit(solution)/shard_map/ppermute | solution.py:73
  23.3 0.8 collective-permute-start.3
  24.2 1.1 concatenate.143
  28.7 0.8 div.64
  29.5 1.4 %convolution_multiply_fusion.6 = f32[16,16,2,128]{3,1,2,0:T(8,128)S(1)} fusion(f32[128,128,1,1]{1,0,3,2:T(8,128)S(1)} %copy-done.3, f32[16,16,2,128]{3,2,0,1:T(2,128)} %div.64, f32[16,16,2,128]{3,2,1,0:T(2,128)S(1)} %reshape_squeeze.9), kind=kOutput, calls=%fused_computation.17 | convolution fusion | flops 100728832 | bytes 851968 | tf_op jit(solution)/shard_map/mk,xynk->xynm/dot_general | solution.py:61
  31.3 0.8 copy.259
  32.1 1.2 reshape.420
  33.7 0.8 fusion.15
  34.9 1.3 collective-permute-start.5
  37.8 3.1 %collective-permute-done.5 = f32[16,256]{1,0:T(8,128)S(1)} collective-permute-done((f32[16,256]{1,0:T(8,128)S(1)}, f32[16,256]{1,0:T(8,128)S(1)}, u32[]{:S(2)}, u32[]{:S(2)}) %collective-permute-start.5) | collective-permute-done | bytes 16416 | tf_op jit(solution)/shard_map/ppermute | solution.py:70
  41.1 1.7 %collective-permute-start.6 = (f32[16,256]{1,0:T(8,128)S(1)}, f32[16,256]{1,0:T(8,128)S(1)}, u32[]{:S(2)}, u32[]{:S(2)}) collective-permute-start(f32[16,256]{1,0:T(8,128)S(1)} %get-tuple-element.44), channel_id=1, source_target_pairs={{1,0},{2,1},{3,2},{4,3},{5,4},{6,5},{7,6},{0,7},{9,8},{10,9},{11,1... | collective-permute-start | bytes 49160 | tf_op jit(solution)/shard_map/ppermute | solution.py:73
  42.8 2.3 %collective-permute-start.7 = (f32[16,256]{1,0:T(8,128)S(1)}, f32[16,256]{1,0:T(8,128)S(1)}, u32[]{:S(2)}, u32[]{:S(2)}) collective-permute-start(f32[16,256]{1,0:T(8,128)S(1)} %get-tuple-element.45), channel_id=1, source_target_pairs={{7,0},{0,1},{1,2},{2,3},{3,4},{4,5},{5,6},{6,7},{15,8},{8,9},{9,10... | collective-permute-start | bytes 49160 | tf_op jit(solution)/shard_map/ppermute | solution.py:73
  45.2 1.3 collective-permute-done.6
  49.7 0.8 copy.270
  50.6 1.2 reshape.422
  52.2 0.8 fusion.16
  54.3 3.0 %collective-permute-start.8 = (f32[4,4,64]{2,1,0:T(4,128)S(1)}, f32[4,4,64]{2,1,0:T(4,128)S(1)}, u32[]{:S(2)}, u32[]{:S(2)}) collective-permute-start(f32[4,4,64]{2,1,0:T(4,128)S(1)} %reshape.424), channel_id=1, source_target_pairs={{7,0},{0,1},{1,2},{2,3},{3,4},{4,5},{5,6},{6,7},{15,8},{8,9},{9,10... | collective-permute-start | bytes 12296 | tf_op jit(solution)/shard_map/ppermute | solution.py:73
  57.3 0.8 collective-permute-done.8
  58.1 3.5 %collective-permute-done.9 = f32[4,4,64]{2,1,0:T(4,128)S(1)} collective-permute-done((f32[4,4,64]{2,1,0:T(4,128)S(1)}, f32[4,4,64]{2,1,0:T(4,128)S(1)}, u32[]{:S(2)}, u32[]{:S(2)}) %collective-permute-start.9) | collective-permute-done | bytes 4128 | tf_op jit(solution)/shard_map/ppermute | solution.py:73
  62.7 0.8 copy.275
  63.5 3.9 %all-to-all-start = ((f32[32,3,4,3]{2,1,3,0:T(4,128)}), f32[32,3,4,3]{2,1,3,0:T(4,128)S(1)}, u32[]{:S(2)}, u32[]{:S(2)}) async-start(f32[32,3,4,3]{2,1,3,0:T(4,128)} %copy.275), calls=%async_computation | async-start | bytes 393216 | tf_op jit(solution)/shard_map/all_to_all | solution.py:208
  67.4 0.7 slice.424
  68.1 0.9 concatenate.144
  69.0 8.2 %all-to-all-done = f32[32,3,4,3]{2,1,3,0:T(4,128)S(1)} async-done(((f32[32,3,4,3]{2,1,3,0:T(4,128)}), f32[32,3,4,3]{2,1,3,0:T(4,128)S(1)}, u32[]{:S(2)}, u32[]{:S(2)}) %all-to-all-start) | async-done | bytes 4640 | tf_op jit(solution)/shard_map/all_to_all | solution.py:208
  78.1 0.7 gather_fusion
  79.2 2.6 %fusion.19 = f32[3,8,1,8,1]{3,2,4,1,0:T(1,128)S(1)} fusion(f32[3,8,8,8,1]{3,4,2,1,0:T(1,128)S(1)} %bitcast.297, f32[1,8,8,8,8]{4,3,2,1,0:T(8,128)} %concatenate.144, f32[2,8,8,8,8]{4,3,2,1,0:T(8,128)S(1)} %copy-done.5), kind=kOutput, calls=%fused_computation.41 | convolution fusion | flops 159744 | bytes 56064 | tf_op jit(solution)/shard_map/yxkij,yxkj,yxk->yxi/dot_general | solution.py:228
  82.8 12.2 %all_to_all.10 = f32[32,3,3]{2,1,0:T(4,128)S(1)} all-to-all(f32[32,3,3]{2,1,0:T(4,128)S(1)} %copy.283), channel_id=1, replica_groups=mesh['wide'=32,'deep'=8] {'wide'}, dimensions={0} | all-to-all | bytes 2304 | tf_op jit(solution)/shard_map/all_to_all | solution.py:234
  100.5 0.8 copy.302
  101.4 1.2 reshape.431
  102.9 0.8 fusion.17
  103.8 0.9 collective-permute-start.10
  105.4 1.5 %collective-permute-done.10 = f32[16,256]{1,0:T(8,128)S(1)} collective-permute-done((f32[16,256]{1,0:T(8,128)S(1)}, f32[16,256]{1,0:T(8,128)S(1)}, u32[]{:S(2)}, u32[]{:S(2)}) %collective-permute-start.10) | collective-permute-done | bytes 16416 | tf_op jit(solution)/shard_map/ppermute | solution.py:70
  106.9 3.7 %collective-permute-done.11 = f32[16,256]{1,0:T(8,128)S(1)} collective-permute-done((f32[16,256]{1,0:T(8,128)S(1)}, f32[16,256]{1,0:T(8,128)S(1)}, u32[]{:S(2)}, u32[]{:S(2)}) %collective-permute-start.11) | collective-permute-done | bytes 16416 | tf_op jit(solution)/shard_map/ppermute | solution.py:70
  110.8 0.9 collective-permute-start.12
  111.7 3.2 %collective-permute-start.13 = (f32[16,256]{1,0:T(8,128)S(1)}, f32[16,256]{1,0:T(8,128)S(1)}, u32[]{:S(2)}, u32[]{:S(2)}) collective-permute-start(f32[16,256]{1,0:T(8,128)S(1)} %get-tuple-element.37), channel_id=1, source_target_pairs={{7,0},{0,1},{1,2},{2,3},{3,4},{4,5},{5,6},{6,7},{15,8},{8,9},{9,10... | collective-permute-start | bytes 49160 | tf_op jit(solution)/shard_map/ppermute | solution.py:73
  114.9 1.4 %collective-permute-done.12 = f32[16,256]{1,0:T(8,128)S(1)} collective-permute-done((f32[16,256]{1,0:T(8,128)S(1)}, f32[16,256]{1,0:T(8,128)S(1)}, u32[]{:S(2)}, u32[]{:S(2)}) %collective-permute-start.12) | collective-permute-done | bytes 16416 | tf_op jit(solution)/shard_map/ppermute | solution.py:73
  119.7 0.8 fusion.18
  120.6 1.4 %collective-permute-start.15 = (f32[16,256]{1,0:T(8,128)S(1)}, f32[16,256]{1,0:T(8,128)S(1)}, u32[]{:S(2)}, u32[]{:S(2)}) collective-permute-start(f32[16,256]{1,0:T(8,128)S(1)} %bitcast.326), channel_id=1, source_target_pairs={{248,0},{0,8},{8,16},{16,24},{24,32},{32,40},{40,48},{48,56},{56,6... | collective-permute-start | bytes 49160 | tf_op jit(solution)/shard_map/ppermute | solution.py:70
  122.1 1.1 collective-permute-done.14
  123.2 3.4 %collective-permute-done.15 = f32[16,256]{1,0:T(8,128)S(1)} collective-permute-done((f32[16,256]{1,0:T(8,128)S(1)}, f32[16,256]{1,0:T(8,128)S(1)}, u32[]{:S(2)}, u32[]{:S(2)}) %collective-permute-start.15) | collective-permute-done | bytes 16416 | tf_op jit(solution)/shard_map/ppermute | solution.py:70
  126.8 4.1 %collective-permute-start.17 = (f32[16,256]{1,0:T(8,128)S(1)}, f32[16,256]{1,0:T(8,128)S(1)}, u32[]{:S(2)}, u32[]{:S(2)}) collective-permute-start(f32[16,256]{1,0:T(8,128)S(1)} %get-tuple-element.29), channel_id=1, source_target_pairs={{7,0},{0,1},{1,2},{2,3},{3,4},{4,5},{5,6},{6,7},{15,8},{8,9},{9,10... | collective-permute-start | bytes 49160 | tf_op jit(solution)/shard_map/ppermute | solution.py:73
  131.6 0.8 collective-permute-done.16
  133.0 0.9 copy.317
  (226 shorter events, 31.7 us)
Async XLA Ops:
  1.7 0.8 copy-start.7
  2.5 1.1 copy-start.2
  3.1 0.8 copy-start.10
  3.8 0.9 copy-start
  4.8 0.9 copy-start.1
  6.5 10.3 %collective-permute-start = (f32[2,16,256]{2,1,0:T(8,128)S(1)}, f32[2,16,256]{2,1,0:T(8,128)S(1)}, u32[]{:S(2)}, u32[]{:S(2)}) collective-permute-start(f32[2,16,256]{2,1,0:T(8,128)S(1)} %bitcast.317), channel_id=1, source_target_pairs={{8,0},{16,8},{24,16},{32,24},{40,32},{48,40},{56,48},{64,56},{72,6... | collective-permute-start | bytes 98312 | tf_op jit(solution)/shard_map/ppermute | solution.py:70
  14.6 0.8 copy-start.6
  14.6 0.8 copy-start.8
  14.6 6.2 %collective-permute-start.1 = (f32[2,16,256]{2,1,0:T(8,128)S(1)}, f32[2,16,256]{2,1,0:T(8,128)S(1)}, u32[]{:S(2)}, u32[]{:S(2)}) collective-permute-start(f32[2,16,256]{2,1,0:T(8,128)S(1)} %bitcast.318), channel_id=1, source_target_pairs={{248,0},{0,8},{8,16},{16,24},{24,32},{32,40},{40,48},{48,56},{56,6... | collective-permute-start | bytes 98312 | tf_op jit(solution)/shard_map/ppermute | solution.py:70
  15.4 0.7 copy-start.22
  16.1 0.7 copy-start.24
  21.2 4.8 %collective-permute-start.2 = (f32[12360]{0:T(1024)S(1)}, f32[12360]{0:T(1024)S(1)}, u32[]{:S(2)}, u32[]{:S(2)}) collective-permute-start(f32[12360]{0:T(1024)S(1)} %concatenate.132), channel_id=1, source_target_pairs={{1,0},{2,1},{3,2},{4,3},{5,4},{6,5},{7,6},{0,7},{9,8},{10,9},{11,1... | collective-permute-start | bytes 148328 | tf_op jit(solution)/shard_map/ppermute | solution.py:73
  23.3 2.8 %collective-permute-start.3 = (f32[2,16,256]{2,1,0:T(8,128)S(1)}, f32[2,16,256]{2,1,0:T(8,128)S(1)}, u32[]{:S(2)}, u32[]{:S(2)}) collective-permute-start(f32[2,16,256]{2,1,0:T(8,128)S(1)} %get-tuple-element.21), channel_id=1, source_target_pairs={{7,0},{0,1},{1,2},{2,3},{3,4},{4,5},{5,6},{6,7},{15,8},{8,9},{9,10... | collective-permute-start | bytes 98312 | tf_op jit(solution)/shard_map/ppermute | solution.py:73
  24.1 2.4 %copy-start.13 = (pred[256]{0:T(512)(128)(4,1)}, pred[256]{0:T(512)(128)(4,1)S(1)}, u32[]{:S(2)}) copy-start(pred[256]{0:T(512)(128)(4,1)S(1)} %get-tuple-element.60) | copy-start | bytes 772
  24.1 2.4 %copy-start.15 = (pred[256]{0:T(512)(128)(4,1)}, pred[256]{0:T(512)(128)(4,1)S(1)}, u32[]{:S(2)}) copy-start(pred[256]{0:T(512)(128)(4,1)S(1)} %get-tuple-element.61) | copy-start | bytes 772
  24.1 1.1 copy-start.20
  26.0 10.2 %copy-start.9 = (f32[12360]{0:T(1024)}, f32[12360]{0:T(1024)S(1)}, u32[]{:S(2)}) copy-start(f32[12360]{0:T(1024)S(1)} %collective-permute-done.2) | copy-start | bytes 148324
  27.0 0.7 copy-start.4
  28.7 0.8 copy-start.3
  34.6 6.3 %collective-permute-start.4 = (f32[16,256]{1,0:T(8,128)S(1)}, f32[16,256]{1,0:T(8,128)S(1)}, u32[]{:S(2)}, u32[]{:S(2)}) collective-permute-start(f32[16,256]{1,0:T(8,128)S(1)} %bitcast.320), channel_id=1, source_target_pairs={{8,0},{16,8},{24,16},{32,24},{40,32},{48,40},{56,48},{64,56},{72,6... | collective-permute-start | bytes 49160 | tf_op jit(solution)/shard_map/ppermute | solution.py:70
  34.9 6.0 %collective-permute-start.5 = (f32[16,256]{1,0:T(8,128)S(1)}, f32[16,256]{1,0:T(8,128)S(1)}, u32[]{:S(2)}, u32[]{:S(2)}) collective-permute-start(f32[16,256]{1,0:T(8,128)S(1)} %bitcast.321), channel_id=1, source_target_pairs={{248,0},{0,8},{8,16},{16,24},{24,32},{32,40},{40,48},{48,56},{56,6... | collective-permute-start | bytes 49160 | tf_op jit(solution)/shard_map/ppermute | solution.py:70
  36.3 0.7 copy-start.23
  37.1 0.7 copy-start.21
  41.1 5.4 %collective-permute-start.6 = (f32[16,256]{1,0:T(8,128)S(1)}, f32[16,256]{1,0:T(8,128)S(1)}, u32[]{:S(2)}, u32[]{:S(2)}) collective-permute-start(f32[16,256]{1,0:T(8,128)S(1)} %get-tuple-element.44), channel_id=1, source_target_pairs={{1,0},{2,1},{3,2},{4,3},{5,4},{6,5},{7,6},{0,7},{9,8},{10,9},{11,1... | collective-permute-start | bytes 49160 | tf_op jit(solution)/shard_map/ppermute | solution.py:73
  42.8 3.7 %collective-permute-start.7 = (f32[16,256]{1,0:T(8,128)S(1)}, f32[16,256]{1,0:T(8,128)S(1)}, u32[]{:S(2)}, u32[]{:S(2)}) collective-permute-start(f32[16,256]{1,0:T(8,128)S(1)} %get-tuple-element.45), channel_id=1, source_target_pairs={{7,0},{0,1},{1,2},{2,3},{3,4},{4,5},{5,6},{6,7},{15,8},{8,9},{9,10... | collective-permute-start | bytes 49160 | tf_op jit(solution)/shard_map/ppermute | solution.py:73
  46.8 0.6 copy-start.14
  46.8 0.7 copy-start.16
  52.2 0.8 copy-start.17
  53.3 0.7 copy-start.12
  54.2 3.1 %copy-start.19 = (s32[192,1]{0,1:T(1,128)S(1)}, s32[192,1]{0,1:T(1,128)}, u32[]{:S(2)}) copy-start(s32[192,1]{0,1:T(1,128)} %add.470) | copy-start | bytes 2308
  54.3 3.8 %collective-permute-start.8 = (f32[4,4,64]{2,1,0:T(4,128)S(1)}, f32[4,4,64]{2,1,0:T(4,128)S(1)}, u32[]{:S(2)}, u32[]{:S(2)}) collective-permute-start(f32[4,4,64]{2,1,0:T(4,128)S(1)} %reshape.424), channel_id=1, source_target_pairs={{7,0},{0,1},{1,2},{2,3},{3,4},{4,5},{5,6},{6,7},{15,8},{8,9},{9,10... | collective-permute-start | bytes 12296 | tf_op jit(solution)/shard_map/ppermute | solution.py:73
  57.3 4.3 %collective-permute-start.9 = (f32[4,4,64]{2,1,0:T(4,128)S(1)}, f32[4,4,64]{2,1,0:T(4,128)S(1)}, u32[]{:S(2)}, u32[]{:S(2)}) collective-permute-start(f32[4,4,64]{2,1,0:T(4,128)S(1)} %reshape.424), channel_id=1, source_target_pairs={{1,0},{2,1},{3,2},{4,3},{5,4},{6,5},{7,6},{0,7},{9,8},{10,9},{11,1... | collective-permute-start | bytes 12296 | tf_op jit(solution)/shard_map/ppermute | solution.py:73
  63.5 13.7 %all-to-all-start = ((f32[32,3,4,3]{2,1,3,0:T(4,128)}), f32[32,3,4,3]{2,1,3,0:T(4,128)S(1)}, u32[]{:S(2)}, u32[]{:S(2)}) async-start(f32[32,3,4,3]{2,1,3,0:T(4,128)} %copy.275), calls=%async_computation | async-start | bytes 393216 | tf_op jit(solution)/shard_map/all_to_all | solution.py:208
  78.1 1.0 copy-start.5
  95.8 0.7 copy-start.18
  97.1 0.7 copy-start.11
  103.8 3.1 %collective-permute-start.10 = (f32[16,256]{1,0:T(8,128)S(1)}, f32[16,256]{1,0:T(8,128)S(1)}, u32[]{:S(2)}, u32[]{:S(2)}) collective-permute-start(f32[16,256]{1,0:T(8,128)S(1)} %bitcast.323), channel_id=1, source_target_pairs={{8,0},{16,8},{24,16},{32,24},{40,32},{48,40},{56,48},{64,56},{72,6... | collective-permute-start | bytes 49160 | tf_op jit(solution)/shard_map/ppermute | solution.py:70
  104.7 5.9 %collective-permute-start.11 = (f32[16,256]{1,0:T(8,128)S(1)}, f32[16,256]{1,0:T(8,128)S(1)}, u32[]{:S(2)}, u32[]{:S(2)}) collective-permute-start(f32[16,256]{1,0:T(8,128)S(1)} %bitcast.325), channel_id=1, source_target_pairs={{248,0},{0,8},{8,16},{16,24},{24,32},{32,40},{40,48},{48,56},{56,6... | collective-permute-start | bytes 49160 | tf_op jit(solution)/shard_map/ppermute | solution.py:70
  110.8 5.5 %collective-permute-start.12 = (f32[16,256]{1,0:T(8,128)S(1)}, f32[16,256]{1,0:T(8,128)S(1)}, u32[]{:S(2)}, u32[]{:S(2)}) collective-permute-start(f32[16,256]{1,0:T(8,128)S(1)} %get-tuple-element.36), channel_id=1, source_target_pairs={{1,0},{2,1},{3,2},{4,3},{5,4},{6,5},{7,6},{0,7},{9,8},{10,9},{11,1... | collective-permute-start | bytes 49160 | tf_op jit(solution)/shard_map/ppermute | solution.py:73
  111.7 4.6 %collective-permute-start.13 = (f32[16,256]{1,0:T(8,128)S(1)}, f32[16,256]{1,0:T(8,128)S(1)}, u32[]{:S(2)}, u32[]{:S(2)}) collective-permute-start(f32[16,256]{1,0:T(8,128)S(1)} %get-tuple-element.37), channel_id=1, source_target_pairs={{7,0},{0,1},{1,2},{2,3},{3,4},{4,5},{5,6},{6,7},{15,8},{8,9},{9,10... | collective-permute-start | bytes 49160 | tf_op jit(solution)/shard_map/ppermute | solution.py:73
  120.5 2.7 %collective-permute-start.14 = (f32[16,256]{1,0:T(8,128)S(1)}, f32[16,256]{1,0:T(8,128)S(1)}, u32[]{:S(2)}, u32[]{:S(2)}) collective-permute-start(f32[16,256]{1,0:T(8,128)S(1)} %bitcast.324), channel_id=1, source_target_pairs={{8,0},{16,8},{24,16},{32,24},{40,32},{48,40},{56,48},{64,56},{72,6... | collective-permute-start | bytes 49160 | tf_op jit(solution)/shard_map/ppermute | solution.py:70
  120.6 6.0 %collective-permute-start.15 = (f32[16,256]{1,0:T(8,128)S(1)}, f32[16,256]{1,0:T(8,128)S(1)}, u32[]{:S(2)}, u32[]{:S(2)}) collective-permute-start(f32[16,256]{1,0:T(8,128)S(1)} %bitcast.326), channel_id=1, source_target_pairs={{248,0},{0,8},{8,16},{16,24},{24,32},{32,40},{40,48},{48,56},{56,6... | collective-permute-start | bytes 49160 | tf_op jit(solution)/shard_map/ppermute | solution.py:70
  126.8 5.6 %collective-permute-start.16 = (f32[16,256]{1,0:T(8,128)S(1)}, f32[16,256]{1,0:T(8,128)S(1)}, u32[]{:S(2)}, u32[]{:S(2)}) collective-permute-start(f32[16,256]{1,0:T(8,128)S(1)} %get-tuple-element.28), channel_id=1, source_target_pairs={{1,0},{2,1},{3,2},{4,3},{5,4},{6,5},{7,6},{0,7},{9,8},{10,9},{11,1... | collective-permute-start | bytes 49160 | tf_op jit(solution)/shard_map/ppermute | solution.py:73
  126.8 5.5 %collective-permute-start.17 = (f32[16,256]{1,0:T(8,128)S(1)}, f32[16,256]{1,0:T(8,128)S(1)}, u32[]{:S(2)}, u32[]{:S(2)}) collective-permute-start(f32[16,256]{1,0:T(8,128)S(1)} %get-tuple-element.29), channel_id=1, source_target_pairs={{7,0},{0,1},{1,2},{2,3},{3,4},{4,5},{5,6},{6,7},{15,8},{8,9},{9,10... | collective-permute-start | bytes 49160 | tf_op jit(solution)/shard_map/ppermute | solution.py:73
where the time goes:
time: 135 us; the launch traced here: 134 us
  starting transfers between devices  34.9 us (26%)
  waiting for transfers between devices  32.7 us (24%)
  local copies, waits for them, and re-layouts  30.5 us (23%)
  matrix products  18.6 us (14%)
  blocking collectives  12.2 us (9%)
  other arithmetic  3.38 us (3%)
  between operations  1.67 us (1%)
    ppermute x10, starting transfers between devices, shift(): return lax.ppermute(value, 'deep', pairs)  18.2 us
    ppermute x8, waiting for transfers between devices, shift(): return lax.ppermute(value, 'wide', pairs)  16.7 us
    ppermute x8, starting transfers between devices, shift(): return lax.ppermute(value, 'wide', pairs)  12.8 us
    all_to_all x1, blocking collectives, local(): got = lax.all_to_all(back, 'wide', 0, 0, tiled=True)  12.2 us
    unnamed x63, local copies, waits for them, and re-layouts  10.2 us
    all_to_all x1, waiting for transfers between devices, local(): got = lax.all_to_all(sent, 'wide', 0, 0, tiled=True)  8.21 us
    ppermute x10, waiting for transfers between devices, shift(): return lax.ppermute(value, 'deep', pairs)  7.72 us
    dot_general x11, matrix products, contract(): return jnp.einsum('mi,iyz->myz', table, field, precision=highest)  6.27 us
  transfers between devices with their start and end apart: 19, of which 12 were waited for; matrix products, arithmetic and copies ran while one was open for 4% of the time, Pallas kernels for 0%

commit v1 on v0

--- a/solution.py
+++ b/solution.py
@@ -156,7 +156,7 @@
     return solution
 
 
-def local(rhs_local, metric, helm, columns, live_blocks, block_values):
+def body(rhs_local, metric, helm, columns, live_blocks, block_values):
     derivative, linear = gll_tables(NP)
     shape = rhs_local.shape
     nw = lax.axis_size("wide")
@@ -171,19 +171,25 @@
     diagonal = helm
     for axis in range(3):
         diagonal = diagonal + contract(metric[axis], square_tables[axis].T, axis)
-    mats = jnp.concatenate(
+    nw_ = lax.axis_size("wide")
+    nxb_ = columns.shape[2]
+    xbs_ = np.stack([(2 * np.arange(nw_) + 2 * j) // BS % nxb_ for j in range(2)], axis=1)
+    packed = jnp.concatenate(
         [
-            block_values[0, 0].reshape(-1),
-            columns[0, 0].astype(jnp.float32).reshape(-1),
-            live_blocks[0, 0].astype(jnp.float32),
-        ]
-    )
-    both, mats = assemble(jnp.stack([diagonal, rhs_local]), NP, mats)
-    nvals = block_values.shape[2] * block_values.shape[3]
-    ncols = columns.shape[2] * columns.shape[3]
-    next_values = mats[:nvals].reshape(block_values.shape[2:])
-    next_columns = mats[nvals : nvals + ncols].astype(jnp.int32).reshape(columns.shape[2:])
-    next_live = mats[nvals + ncols :].astype(jnp.int32)
+            block_values[0],
+            columns[0].astype(jnp.float32),
+            live_blocks[0].astype(jnp.float32)[..., None],
+        ],
+        axis=-1,
+    )
+    packed = jnp.transpose(jnp.take(packed, jnp.asarray(xbs_), axis=1), (1, 0, 2, 3))
+    fetched = lax.all_to_all(packed, "wide", 0, 0, tiled=True)
+    fetched = jnp.concatenate([fetched, shift(fetched[:, :1], 0, 1)], axis=1)
+    nvals = block_values.shape[3]
+    fetched_vals = fetched[..., :nvals]
+    fetched_cols = fetched[..., nvals : nvals + K].astype(jnp.int32)
+    fetched_live = fetched[..., nvals + K].astype(jnp.int32)
+    both = assemble(jnp.stack([diagonal, rhs_local]), NP)
     inverse = 1.0 / both[0]
     first = chebyshev(
         jnp.zeros_like(rhs_local), rhs_local, metric, helm, tables, inverse, both[1]
@@ -193,7 +199,7 @@
     for axis in range(3):
         corners = contract(corners, down_tables[axis], axis)
 
-    cx, cy, cz = corners.shape
+    cx, cy, _ = corners.shape
     ext = jnp.concatenate([shift(corners, 0, -1), corners, shift(corners, 0, 1)], axis=1)
     qz = ext[:, :, 0::2] + jnp.roll(ext, 1, axis=2)[:, :, 0::2]
     qy = qz[:, cy : cy + 7 : 2] + qz[:, cy - 1 : cy + 6 : 2]
@@ -201,37 +207,43 @@
     qx = jnp.concatenate([zero, qy, zero], axis=0)
     partial = qx[1 : cx + 2 : 2] + qx[0 : cx + 1 : 2]
 
-    sent = jnp.stack(
-        [jnp.roll(partial, 1, axis=2), partial, jnp.roll(partial, -1, axis=2)], axis=-1
-    )
-    sent = jnp.transpose(sent, (2, 0, 1, 3))
-    got = lax.all_to_all(sent, "wide", 0, 0, tiled=True)
+    got = lax.all_to_all(
+        jnp.broadcast_to(partial[None], (nw,) + partial.shape), "wide", 0, 0, tiled=True
+    )
     even = got[:, 0] + jnp.roll(got[:, 2], 1, axis=0)
     got = jnp.stack([even, got[:, 1]], axis=1)
-    frame = jnp.transpose(got, (3, 2, 0, 1)).reshape(3, 4, -1)
+    layers = got.shape[-1]
+    frame = jnp.transpose(got, (3, 2, 0, 1)).reshape(layers, 4, -1)
     span = frame.shape[2]
     nxb = span // BS
     frame_rows = frame.reshape(-1, BS)
-
-    cols = jnp.concatenate([columns[0], next_columns[None]], axis=0)
-    lives = jnp.concatenate([live_blocks[0], next_live[None]], axis=0)
-    vals = jnp.concatenate([block_values[0], next_values[None]], axis=0)
-    y_off = jnp.array([0, 0, 2], jnp.int32)[:, None, None]
-    layer = cols // (2 * nxb)
-    block = cols % (2 * nxb)
-    index = (layer * 4 + y_off + block // nxb) * nxb + block % nxb
-    picked = jnp.take(frame_rows, index.reshape(-1), axis=0).reshape(index.shape + (BS,))
-    live = (jnp.arange(K, dtype=jnp.int32)[None, None, :] < lives[:, :, None]).astype(
-        jnp.float32
-    )
-    values = vals.reshape(vals.shape[:2] + (K, BS, BS))
-    product = jnp.einsum("yxkij,yxkj,yxk->yxi", values, picked, live, precision=highest)
-    product = product.reshape(3, span)
-    coarse_product = product[:2].reshape(1, 2, span)
-
-    pick = (2 * np.arange(nw)[:, None] + np.arange(3)[None, :]) % span
-    back = jnp.transpose(product[:, pick], (1, 0, 2))
-    got = lax.all_to_all(back, "wide", 0, 0, tiled=True)
+    w_index = lax.axis_index("wide")
+
+    def rows_of(cols, lives, vals, z, y_off):
+        layer = cols // (2 * nxb)
+        block = cols % (2 * nxb)
+        src = (z + layer - 1) % layers
+        index = ((src * 4 + y_off + block // nxb) * nxb + block % nxb)
+        picked = jnp.take(frame_rows, index.reshape(-1), axis=0).reshape(index.shape + (BS,))
+        live = (jnp.arange(K, dtype=jnp.int32) < lives[..., None]).astype(jnp.float32)
+        values = vals.reshape(vals.shape[:-1] + (K, BS, BS))
+        return jnp.einsum("...kij,...kj,...k->...i", values, picked, live, precision=highest)
+
+    own = rows_of(columns[0], live_blocks[0], block_values[0], w_index, 0)
+    coarse_product = own.reshape(1, 2, span)
+
+    corr = rows_of(
+        fetched_cols,
+        fetched_live,
+        fetched_vals,
+        jnp.arange(layers, dtype=jnp.int32)[:, None, None, None],
+        jnp.array([0, 0, 2], jnp.int32)[None, :, None, None],
+    )
+    corr = corr.reshape(layers, 3, 2 * BS)
+    x_need = (2 * w_index + jnp.arange(3, dtype=jnp.int32)) % span
+    first_block = (2 * w_index // BS) % nxb
+    virtual = jnp.where(x_need // BS == first_block, 0, BS) + x_need % BS
+    got = jnp.take(corr, virtual, axis=2)
     hx = jnp.stack([got[:, :, 0:2], got[:, :, 1:3]], axis=-1).reshape(nw, 3, 4)
     hy = jnp.stack([hx[:, 0:2], hx[:, 1:3]], axis=2).reshape(nw, 4, 4)
     hz = jnp.stack([hy, jnp.roll(hy, -1, axis=0)], axis=1).reshape(2 * nw, 4, 4)
@@ -253,7 +265,7 @@
         P("wide", "deep", None, None),
     )
     return jax.shard_map(
-        local,
+        body,
         mesh=mesh,
         in_specs=placed,
         out_specs=(P("wide", "deep", None), P("wide", "deep", None)),

time: 135 us -> 158 us (1.17)
  other arithmetic: 3.38 us -> 16 us
  blocking collectives: 12.2 us -> 0 us
  local copies, waits for them, and re-layouts: 30.5 us -> 38.3 us
  waiting for transfers between devices: 32.7 us -> 40.5 us
  starting transfers between devices: 34.9 us -> 39.1 us
  matrix products: 18.6 us -> 20.3 us
    all_to_all x1 -> x0, blocking collectives: 12.2 us -> none  [local(): got = lax.all_to_all(back, 'wide', 0, 0, tiled=True)]
    all_to_all x1 -> x2, waiting for transfers between devices: 8.21 us -> 17 us  [the longest x1 10 us: body(): fetched = lax.all_to_all(packed, 'wide', 0, 0, tiled=True)]
    gather x4 -> x5, local copies, waits for them, and re-layouts: 1.52 us -> 7.44 us  [the longest x2 4.91 us: rows_of(): jnp.take(frame_rows, index.reshape(-1), axis=0).reshape(index.shape + (BS,))]
    ppermute x10 -> x11, waiting for transfers between devices: 7.72 us -> 2.59 us  [shift(): return lax.ppermute(value, 'deep', pairs)]
    unnamed x63 -> x100, local copies, waits for them, and re-layouts: 10.2 us -> 5.42 us
    ppermute x8, waiting for transfers between devices: 16.7 us -> 20.9 us  [shift(): return lax.ppermute(value, 'wide', pairs)]
    all_to_all x1 -> x2, starting transfers between devices: 3.86 us -> 7.95 us  [the longest x1 4.1 us: body(): fetched = lax.all_to_all(packed, 'wide', 0, 0, tiled=True)]
    another operation x8 -> x7, local copies, waits for them, and re-layouts: 0.54 us -> 3.34 us  [the longest x1 2.04 us: body(): frame_rows = frame.reshape(-1, BS)]
  transfers between devices with their start and end apart: 19 -> 21, of which waited for: 12 -> 13; matrix products, arithmetic and copies ran while one was open for 4% -> 11% of each run, Pallas kernels for 0% -> 0%
where the time goes in v1:
time: 158 us; the launch traced here: 156 us
  waiting for transfers between devices  40.5 us (26%)
  starting transfers between devices  39.1 us (25%)
  local copies, waits for them, and re-layouts  38.3 us (24%)
  matrix products  20.3 us (13%)
  other arithmetic  16 us (10%)
  between operations  1.94 us (1%)
    ppermute x8, waiting for transfers between devices, shift(): return lax.ppermute(value, 'wide', pairs)  20.9 us
    ppermute x11, starting transfers between devices, shift(): return lax.ppermute(value, 'deep', pairs)  17.7 us
    ppermute x8, starting transfers between devices, shift(): return lax.ppermute(value, 'wide', pairs)  13.5 us
    all_to_all x1, waiting for transfers between devices, body(): fetched = lax.all_to_all(packed, 'wide', 0, 0, tiled=True)  10 us
    dot_general x11, matrix products, contract(): return jnp.einsum('mi,iyz->myz', table, field, precision=highest)  7.84 us
    all_to_all x1, waiting for transfers between devices, body(): lax.all_to_all(jnp.broadcast_to(partial[None], (nw,) + partial.shape), 'w...  6.93 us
    dot_general x11, matrix products, contract(): return jnp.einsum('mj,xjz->xmz', table, field, precision=highest)  6.15 us
    unnamed x100, local copies, waits for them, and re-layouts  5.42 us
  transfers between devices with their start and end apart: 21, of which 13 were waited for; matrix products, arithmetic and copies ran while one was open for 11% of the time, Pallas kernels for 0%

profile of v1, /device:TPU:7, one launch (start us, length us, event | category | flops | bytes accessed | tf_op | source)
XLA Modules:
  0.0 156.1 jit_solution(5641968280180059601)
XLA Ops:
  0.7 1.1 fusion.134
  4.1 8.1 %collective-permute-start = (f32[2,16,256]{2,1,0:T(8,128)S(1)}, f32[2,16,256]{2,1,0:T(8,128)S(1)}, u32[]{:S(2)}, u32[]{:S(2)}) collective-permute-start(f32[2,16,256]{2,1,0:T(8,128)S(1)} %bitcast.340), channel_id=1, source_target_pairs={{8,0},{16,8},{24,16},{32,24},{40,32},{48,40},{56,48},{64,56},{72,6... | collective-permute-start | bytes 98312 | tf_op jit(solution)/shard_map/ppermute | solution.py:70
  12.2 1.0 collective-permute-done
  13.2 5.0 %collective-permute-done.1 = f32[2,16,256]{2,1,0:T(8,128)S(1)} collective-permute-done((f32[2,16,256]{2,1,0:T(8,128)S(1)}, f32[2,16,256]{2,1,0:T(8,128)S(1)}, u32[]{:S(2)}, u32[]{:S(2)}) %collective-permute-start.1) | collective-permute-done | bytes 32800 | tf_op jit(solution)/shard_map/ppermute | solution.py:70
  18.6 2.1 %collective-permute-start.2 = (f32[2,16,256]{2,1,0:T(8,128)S(1)}, f32[2,16,256]{2,1,0:T(8,128)S(1)}, u32[]{:S(2)}, u32[]{:S(2)}) collective-permute-start(f32[2,16,256]{2,1,0:T(8,128)S(1)} %get-tuple-element.24), channel_id=1, source_target_pairs={{1,0},{2,1},{3,2},{4,3},{5,4},{6,5},{7,6},{0,7},{9,8},{10,9},{11,1... | collective-permute-start | bytes 98312 | tf_op jit(solution)/shard_map/ppermute | solution.py:73
  20.7 0.8 collective-permute-start.3
  21.5 1.6 %collective-permute-done.2 = f32[2,16,256]{2,1,0:T(8,128)S(1)} collective-permute-done((f32[2,16,256]{2,1,0:T(8,128)S(1)}, f32[2,16,256]{2,1,0:T(8,128)S(1)}, u32[]{:S(2)}, u32[]{:S(2)}) %collective-permute-start.2) | collective-permute-done | bytes 32800 | tf_op jit(solution)/shard_map/ppermute | solution.py:73
  26.2 1.4 convolution_multiply_fusion.6
  28.8 1.2 reshape.612
  31.4 1.4 collective-permute-start.5
  32.8 4.7 %collective-permute-done.5 = f32[16,256]{1,0:T(8,128)S(1)} collective-permute-done((f32[16,256]{1,0:T(8,128)S(1)}, f32[16,256]{1,0:T(8,128)S(1)}, u32[]{:S(2)}, u32[]{:S(2)}) %collective-permute-start.5) | collective-permute-done | bytes 16416 | tf_op jit(solution)/shard_map/ppermute | solution.py:70
  37.7 2.1 %collective-permute-start.6 = (f32[16,256]{1,0:T(8,128)S(1)}, f32[16,256]{1,0:T(8,128)S(1)}, u32[]{:S(2)}, u32[]{:S(2)}) collective-permute-start(f32[16,256]{1,0:T(8,128)S(1)} %get-tuple-element.48), channel_id=1, source_target_pairs={{1,0},{2,1},{3,2},{4,3},{5,4},{6,5},{7,6},{0,7},{9,8},{10,9},{11,1... | collective-permute-start | bytes 49160 | tf_op jit(solution)/shard_map/ppermute | solution.py:73
  39.8 2.1 %collective-permute-start.7 = (f32[16,256]{1,0:T(8,128)S(1)}, f32[16,256]{1,0:T(8,128)S(1)}, u32[]{:S(2)}, u32[]{:S(2)}) collective-permute-start(f32[16,256]{1,0:T(8,128)S(1)} %get-tuple-element.49), channel_id=1, source_target_pairs={{7,0},{0,1},{1,2},{2,3},{3,4},{4,5},{5,6},{6,7},{15,8},{8,9},{9,10... | collective-permute-start | bytes 49160 | tf_op jit(solution)/shard_map/ppermute | solution.py:73
  43.9 1.0 fusion.58
  49.2 3.0 %collective-permute-start.9 = (f32[4,4,64]{2,1,0:T(4,128)S(1)}, f32[4,4,64]{2,1,0:T(4,128)S(1)}, u32[]{:S(2)}, u32[]{:S(2)}) collective-permute-start(f32[4,4,64]{2,1,0:T(4,128)S(1)} %reshape.617), channel_id=1, source_target_pairs={{7,0},{0,1},{1,2},{2,3},{3,4},{4,5},{5,6},{6,7},{15,8},{8,9},{9,10... | collective-permute-start | bytes 12296 | tf_op jit(solution)/shard_map/ppermute | solution.py:73
  55.2 3.9 %all-to-all-start.1 = ((f32[32,1,384]{2,1,0:T(1,128)}), f32[32,1,384]{2,1,0:T(1,128)S(1)}, u32[]{:S(2)}, u32[]{:S(2)}) async-start(f32[32,1,384]{2,1,0:T(1,128)} %reshape.683), calls=%async_computation.1 | async-start | bytes 98304 | tf_op jit(solution)/shard_map/all_to_all | solution.py:210
  59.1 0.9 gather_fusion
  60.0 0.9 copy.551
  60.9 6.9 %all-to-all-done.1 = f32[32,1,384]{2,1,0:T(1,128)S(1)} async-done(((f32[32,1,384]{2,1,0:T(1,128)}), f32[32,1,384]{2,1,0:T(1,128)S(1)}, u32[]{:S(2)}, u32[]{:S(2)}) %all-to-all-start.1) | async-done | bytes 49184 | tf_op jit(solution)/shard_map/all_to_all | solution.py:210
  67.9 4.1 %all-to-all-start = ((f32[32,2,2,521]{3,2,1,0:T(2,128)}), f32[32,2,2,521]{3,2,1,0:T(2,128)S(1)}, u32[]{:S(2)}, u32[]{:S(2)}) async-start(f32[32,2,2,521]{3,2,1,0:T(2,128)} %bitcast.300), calls=%async_computation | async-start | bytes 655360 | tf_op jit(solution)/shard_map/all_to_all | solution.py:186
  75.3 10.0 %all-to-all-done = f32[32,2,2,521]{3,2,1,0:T(2,128)S(1)} async-done(((f32[32,2,2,521]{3,2,1,0:T(2,128)}), f32[32,2,2,521]{3,2,1,0:T(2,128)S(1)}, u32[]{:S(2)}, u32[]{:S(2)}) %all-to-all-start) | async-done | bytes 266784 | tf_op jit(solution)/shard_map/all_to_all | solution.py:186
  86.6 2.9 %copy.402 = f32[32,4,32,2]{3,2,1,0:T(8,128)} copy(f32[32,4,32,2]{0,2,1,3:T(8,128)S(1)} %maximum_bitcast_fusion) | data formatting | bytes 65536 | tf_op jit(solution)/shard_map/transpose | solution.py:216
  89.5 2.0 %reshape_reshape.3 = f32[1024,8]{1,0:T(8,128)S(1)} reshape(f32[32,4,32,2]{3,2,1,0:T(8,128)} %copy.402) | data formatting | bytes 65536 | tf_op jit(solution)/shard_map/reshape;reshape | solution.py:219
  92.3 1.1 copy.386
  94.0 1.3 fusion
  98.7 3.7 %gather_fusion.1 = f32[1536,8]{1,0:T(8,128)} fusion(f32[1024,8]{1,0:T(8,128)S(1)} %reshape_reshape.3, s32[2048]{0:T(1024)S(1)} %pad_clamp_fusion), kind=kCustom, calls=%fused_computation.1 | custom fusion | bytes 104448 | tf_op jit(solution)/shard_map/jit(_take)/gather | solution.py:227
  102.4 2.4 %multiply_bitcast_fusion = f32[32,3,2,8,8]{3,4,2,1,0:T(8,128)} fusion(f32[32,3,2,8,8]{4,3,2,1,0:T(8,128)} %bitcast.313, f32[32,3,2,8]{3,2,1,0:T(2,128)} %compare_convert_fusion, pred[32,3,2,8]{3,2,1,0:T(4,128)(4,1)S(1)} %copy.387), kind=kLoop, calls=%fused_computation.49 | loop fusion | flops 24576 | bytes 105984
  104.8 2.1 %copy.484 = f32[32,3,2,8,8]{0,3,4,2,1:T(8,128)} copy(f32[32,3,2,8,8]{3,4,2,1,0:T(8,128)} %multiply_bitcast_fusion) | data formatting | bytes 98304
  106.9 1.2 multiply_reduce_fusion
  112.5 1.2 fusion.13
  115.4 1.9 %reshape.625 = f32[16,16,256]{2,0,1:T(8,128)} reshape(f32[16,16,2,128]{3,2,0,1:T(2,128)} %copy.425) | data formatting | bytes 524288 | tf_op jit(solution)/shard_map/reshape | solution.py:62
  117.2 1.4 fusion.151
  118.6 1.8 %fusion.18 = f32[16,16,256]{2,0,1:T(8,128)S(1)} fusion(f32[16,16,256]{2,0,1:T(8,128)} %reshape.625, f32[16,16,1]{1,0,2:T(8,128)S(1)} %copy-done.9, f32[16,16,256]{2,0,1:T(8,128)S(1)} %convolution_multiply_fusion.3, f32[16,256,16]{1,2,0:T(8,128)S(1)} %fusion.151, f32[16,16,256]{2,0,1:T(8,128)S(1)} %add.675, f32[16,16,256]{2,1,0:T(8,128)S(1)} %copy-done.1, ...), kind=kOutput, calls=%fused_computation.45 | convolution fusion | flops 12910592 | bytes 1836032 | tf_op jit(solution)/shard_map/mi,iyz->myz/dot_general | solution.py:55
  120.5 2.3 %collective-permute-start.11 = (f32[16,256]{1,0:T(8,128)S(1)}, f32[16,256]{1,0:T(8,128)S(1)}, u32[]{:S(2)}, u32[]{:S(2)}) collective-permute-start(f32[16,256]{1,0:T(8,128)S(1)} %bitcast.346), channel_id=1, source_target_pairs={{8,0},{16,8},{24,16},{32,24},{40,32},{48,40},{56,48},{64,56},{72,6... | collective-permute-start | bytes 49160 | tf_op jit(solution)/shard_map/ppermute | solution.py:70
  122.8 0.9 collective-permute-done.11
  123.8 4.9 %collective-permute-done.12 = f32[16,256]{1,0:T(8,128)S(1)} collective-permute-done((f32[16,256]{1,0:T(8,128)S(1)}, f32[16,256]{1,0:T(8,128)S(1)}, u32[]{:S(2)}, u32[]{:S(2)}) %collective-permute-start.12) | collective-permute-done | bytes 16416 | tf_op jit(solution)/shard_map/ppermute | solution.py:70
  129.5 1.0 collective-permute-start.13
  130.4 2.6 %collective-permute-start.14 = (f32[16,256]{1,0:T(8,128)}, f32[16,256]{1,0:T(8,128)}, u32[]{:S(2)}, u32[]{:S(2)}) collective-permute-start(f32[16,256]{1,0:T(8,128)} %get-tuple-element.41), channel_id=1, source_target_pairs={{7,0},{0,1},{1,2},{2,3},{3,4},{4,5},{5,6},{6,7},{15,8},{8,9},{9,10... | collective-permute-start | bytes 49160 | tf_op jit(solution)/shard_map/ppermute | solution.py:73
  133.0 1.1 reshape_squeeze.7
  134.2 1.2 gather_fusion.3
  136.5 2.2 %multiply_add_fusion = (f32[16,16,256]{2,0,1:T(8,128)S(1)}, f32[16,16,256]{2,0,1:T(8,128)}) fusion(f32[16,16,256]{2,0,1:T(8,128)S(1)} %add.675, f32[16,16,255]{2,0,1:T(8,128)S(1)} %get-tuple-element.37, f32[16,16,1]{2,0,1:T(8,128)S(1)} %get-tuple-element.39, pred[256]{0:T(512)(128)(4,1)S(1)} %copy-done.31, f32[16,16,1]{2,0,1:T(8,128)S(1)} %get-tuple-element.38, ...), kind=kLoop, calls=%fused_computation.145 | loop fusion | flops 1048576 | bytes 1868320 | tf_op jit(solution)/shard_map/add | solution.py:149
  138.9 1.1 convolution_multiply_fusion.1
  143.2 1.4 collective-permute-start.16
  144.8 1.0 collective-permute-done.15
  145.8 3.4 %collective-permute-done.16 = f32[16,256]{1,0:T(8,128)S(1)} collective-permute-done((f32[16,256]{1,0:T(8,128)S(1)}, f32[16,256]{1,0:T(8,128)S(1)}, u32[]{:S(2)}, u32[]{:S(2)}) %collective-permute-start.16) | collective-permute-done | bytes 16416 | tf_op jit(solution)/shard_map/ppermute | solution.py:70
  149.4 3.5 %collective-permute-start.18 = (f32[16,256]{1,0:T(8,128)S(1)}, f32[16,256]{1,0:T(8,128)S(1)}, u32[]{:S(2)}, u32[]{:S(2)}) collective-permute-start(f32[16,256]{1,0:T(8,128)S(1)} %get-tuple-element.33), channel_id=1, source_target_pairs={{7,0},{0,1},{1,2},{2,3},{3,4},{4,5},{5,6},{6,7},{15,8},{8,9},{9,10... | collective-permute-start | bytes 49160 | tf_op jit(solution)/shard_map/ppermute | solution.py:73
  152.8 1.1 fusion.155
  155.2 0.9 copy.440
  (266 shorter events, 39.2 us)
Async XLA Ops:
  4.1 9.1 %collective-permute-start = (f32[2,16,256]{2,1,0:T(8,128)S(1)}, f32[2,16,256]{2,1,0:T(8,128)S(1)}, u32[]{:S(2)}, u32[]{:S(2)}) collective-permute-start(f32[2,16,256]{2,1,0:T(8,128)S(1)} %bitcast.340), channel_id=1, source_target_pairs={{8,0},{16,8},{24,16},{32,24},{40,32},{48,40},{56,48},{64,56},{72,6... | collective-permute-start | bytes 98312 | tf_op jit(solution)/shard_map/ppermute | solution.py:70
  12.2 6.1 %collective-permute-start.1 = (f32[2,16,256]{2,1,0:T(8,128)S(1)}, f32[2,16,256]{2,1,0:T(8,128)S(1)}, u32[]{:S(2)}, u32[]{:S(2)}) collective-permute-start(f32[2,16,256]{2,1,0:T(8,128)S(1)} %bitcast.341), channel_id=1, source_target_pairs={{248,0},{0,8},{8,16},{16,24},{24,32},{32,40},{40,48},{48,56},{56,6... | collective-permute-start | bytes 98312 | tf_op jit(solution)/shard_map/ppermute | solution.py:70
  12.2 31.7 %copy-start.19 = (pred[16]{0:T(512)(128)(4,1)}, pred[16]{0:T(512)(128)(4,1)S(1)}, u32[]{:S(2)}) copy-start(pred[16]{0:T(512)(128)(4,1)S(1)} %get-tuple-element.58) | copy-start | bytes 52
  12.2 31.7 %copy-start.21 = (pred[16]{0:T(512)(128)(4,1)}, pred[16]{0:T(512)(128)(4,1)S(1)}, u32[]{:S(2)}) copy-start(pred[16]{0:T(512)(128)(4,1)S(1)} %get-tuple-element.59) | copy-start | bytes 52
  18.6 4.6 %collective-permute-start.2 = (f32[2,16,256]{2,1,0:T(8,128)S(1)}, f32[2,16,256]{2,1,0:T(8,128)S(1)}, u32[]{:S(2)}, u32[]{:S(2)}) collective-permute-start(f32[2,16,256]{2,1,0:T(8,128)S(1)} %get-tuple-element.24), channel_id=1, source_target_pairs={{1,0},{2,1},{3,2},{4,3},{5,4},{6,5},{7,6},{0,7},{9,8},{10,9},{11,1... | collective-permute-start | bytes 98312 | tf_op jit(solution)/shard_map/ppermute | solution.py:73
  20.7 2.4 %collective-permute-start.3 = (f32[2,16,256]{2,1,0:T(8,128)S(1)}, f32[2,16,256]{2,1,0:T(8,128)S(1)}, u32[]{:S(2)}, u32[]{:S(2)}) collective-permute-start(f32[2,16,256]{2,1,0:T(8,128)S(1)} %get-tuple-element.25), channel_id=1, source_target_pairs={{7,0},{0,1},{1,2},{2,3},{3,4},{4,5},{5,6},{6,7},{15,8},{8,9},{9,10... | collective-permute-start | bytes 98312 | tf_op jit(solution)/shard_map/ppermute | solution.py:73
  28.8 4.0 %copy-start.18 = (s32[1,2,8,8]{3,2,1,0:T(8,128)S(1)}, s32[1,2,8,8]{3,2,1,0:T(8,128)}, u32[]{:S(2)}) copy-start(s32[1,2,8,8]{3,2,1,0:T(8,128)} %param.23) | copy-start | bytes 1540
  30.0 11.9 %copy-start.37 = (s32[1,2,8]{2,1,0:T(2,128)S(1)}, s32[1,2,8]{2,1,0:T(2,128)}, u32[]{:S(2)}) copy-start(s32[1,2,8]{2,1,0:T(2,128)} %param.24) | copy-start | bytes 196
  30.0 11.9 %copy-start.15 = (f32[1,2,8,512]{3,2,1,0:T(8,128)S(1)}, f32[1,2,8,512]{3,2,1,0:T(8,128)}, u32[]{:S(2)}) copy-start(f32[1,2,8,512]{3,2,1,0:T(8,128)} %param.25) | copy-start | bytes 98308
  31.3 6.3 %collective-permute-start.4 = (f32[16,256]{1,0:T(8,128)S(1)}, f32[16,256]{1,0:T(8,128)S(1)}, u32[]{:S(2)}, u32[]{:S(2)}) collective-permute-start(f32[16,256]{1,0:T(8,128)S(1)} %bitcast.343), channel_id=1, source_target_pairs={{8,0},{16,8},{24,16},{32,24},{40,32},{48,40},{56,48},{64,56},{72,6... | collective-permute-start | bytes 49160 | tf_op jit(solution)/shard_map/ppermute | solution.py:70
  31.4 6.2 %collective-permute-start.5 = (f32[16,256]{1,0:T(8,128)S(1)}, f32[16,256]{1,0:T(8,128)S(1)}, u32[]{:S(2)}, u32[]{:S(2)}) collective-permute-start(f32[16,256]{1,0:T(8,128)S(1)} %bitcast.348), channel_id=1, source_target_pairs={{248,0},{0,8},{8,16},{16,24},{24,32},{32,40},{40,48},{48,56},{56,6... | collective-permute-start | bytes 49160 | tf_op jit(solution)/shard_map/ppermute | solution.py:70
  37.7 5.6 %collective-permute-start.6 = (f32[16,256]{1,0:T(8,128)S(1)}, f32[16,256]{1,0:T(8,128)S(1)}, u32[]{:S(2)}, u32[]{:S(2)}) collective-permute-start(f32[16,256]{1,0:T(8,128)S(1)} %get-tuple-element.48), channel_id=1, source_target_pairs={{1,0},{2,1},{3,2},{4,3},{5,4},{6,5},{7,6},{0,7},{9,8},{10,9},{11,1... | collective-permute-start | bytes 49160 | tf_op jit(solution)/shard_map/ppermute | solution.py:73
  39.8 3.5 %collective-permute-start.7 = (f32[16,256]{1,0:T(8,128)S(1)}, f32[16,256]{1,0:T(8,128)S(1)}, u32[]{:S(2)}, u32[]{:S(2)}) collective-permute-start(f32[16,256]{1,0:T(8,128)S(1)} %get-tuple-element.49), channel_id=1, source_target_pairs={{7,0},{0,1},{1,2},{2,3},{3,4},{4,5},{5,6},{6,7},{15,8},{8,9},{9,10... | collective-permute-start | bytes 49160 | tf_op jit(solution)/shard_map/ppermute | solution.py:73
  47.0 5.2 %copy-start.17 = (f32[1,2,8,512]{3,1,2,0:T(2,128)S(1)}, f32[1,2,8,512]{3,1,2,0:T(2,128)}, u32[]{:S(2)}) copy-start(f32[1,2,8,512]{3,1,2,0:T(2,128)} %copy.555) | copy-start | bytes 98308
  47.0 5.2 %copy-start.27 = (f32[2,8,1]{2,0,1:T(2,128)S(1)}, f32[2,8,1]{2,0,1:T(2,128)}, u32[]{:S(2)}) copy-start(f32[2,8,1]{2,0,1:T(2,128)} %copy.382) | copy-start | bytes 196
  47.7 11.4 %copy-start.40 = (s32[64]{0:T(128)S(1)}, s32[64]{0:T(128)}, u32[]{:S(2)}) copy-start(s32[64]{0:T(128)} %constant.373) | copy-start | bytes 772
  49.2 4.3 %collective-permute-start.10 = (f32[4,4,64]{2,1,0:T(4,128)S(1)}, f32[4,4,64]{2,1,0:T(4,128)S(1)}, u32[]{:S(2)}, u32[]{:S(2)}) collective-permute-start(f32[4,4,64]{2,1,0:T(4,128)S(1)} %reshape.617), channel_id=1, source_target_pairs={{1,0},{2,1},{3,2},{4,3},{5,4},{6,5},{7,6},{0,7},{9,8},{10,9},{11,1... | collective-permute-start | bytes 12296 | tf_op jit(solution)/shard_map/ppermute | solution.py:73
  49.2 4.3 %collective-permute-start.9 = (f32[4,4,64]{2,1,0:T(4,128)S(1)}, f32[4,4,64]{2,1,0:T(4,128)S(1)}, u32[]{:S(2)}, u32[]{:S(2)}) collective-permute-start(f32[4,4,64]{2,1,0:T(4,128)S(1)} %reshape.617), channel_id=1, source_target_pairs={{7,0},{0,1},{1,2},{2,3},{3,4},{4,5},{5,6},{6,7},{15,8},{8,9},{9,10... | collective-permute-start | bytes 12296 | tf_op jit(solution)/shard_map/ppermute | solution.py:73
  52.3 20.8 %copy-start.38 = (s32[1,2,8]{2,1,0:T(2,128)S(1)}, s32[1,2,8]{2,1,0:T(2,128)}, u32[]{:S(2)}) copy-start(s32[1,2,8]{2,1,0:T(2,128)} %param.24) | copy-start | bytes 196
  55.2 12.7 %all-to-all-start.1 = ((f32[32,1,384]{2,1,0:T(1,128)}), f32[32,1,384]{2,1,0:T(1,128)S(1)}, u32[]{:S(2)}, u32[]{:S(2)}) async-start(f32[32,1,384]{2,1,0:T(1,128)} %reshape.683), calls=%async_computation.1 | async-start | bytes 98304 | tf_op jit(solution)/shard_map/all_to_all | solution.py:210
  67.9 17.4 %all-to-all-start = ((f32[32,2,2,521]{3,2,1,0:T(2,128)}), f32[32,2,2,521]{3,2,1,0:T(2,128)S(1)}, u32[]{:S(2)}, u32[]{:S(2)}) async-start(f32[32,2,2,521]{3,2,1,0:T(2,128)} %bitcast.300), calls=%async_computation | async-start | bytes 655360 | tf_op jit(solution)/shard_map/all_to_all | solution.py:186
  86.0 6.3 %collective-permute-start.8 = (f32[32,1,2,521]{3,0,2,1:T(8,128)}, f32[32,1,2,521]{3,0,2,1:T(8,128)}, u32[]{:S(2)}, u32[]{:S(2)}) collective-permute-start(f32[32,1,2,521]{3,0,2,1:T(8,128)} %copy.384), channel_id=1, source_target_pairs={{1,0},{2,1},{3,2},{4,3},{5,4},{6,5},{7,6},{0,7},{9,8},{10,9},{11,1... | collective-permute-start | bytes 400136 | tf_op jit(solution)/shard_map/ppermute | solution.py:73
  102.4 4.6 %copy-start.4 = (f32[32,3,2,512]{0,3,2,1:T(8,128)S(1)}, f32[32,3,2,512]{0,3,2,1:T(8,128)}, u32[]{:S(2)}) copy-start(f32[32,3,2,512]{0,3,2,1:T(8,128)} %fusion) | copy-start | bytes 1179652
  104.8 4.0 %copy-start.42 = (pred[3]{0:T(512)(128)(4,1)S(1)}, pred[3]{0:T(512)(128)(4,1)}, u32[]{:S(2)}) copy-start(pred[3]{0:T(512)(128)(4,1)} %compare_and_fusion.2) | copy-start | bytes 13
  104.8 4.8 %copy-start.36 = (f32[16,4,1]{0,1,2:T(4,128)S(1)}, f32[16,4,1]{0,1,2:T(4,128)}, u32[]{:S(2)}) copy-start(f32[16,4,1]{0,1,2:T(4,128)} %constant.379) | copy-start | bytes 772
  106.9 3.4 %copy-start.28 = (f32[128,32,1,1]{0,1,3,2:T(8,128)S(1)}, f32[128,32,1,1]{0,1,3,2:T(8,128)}, u32[]{:S(2)}) copy-start(f32[128,32,1,1]{0,1,3,2:T(8,128)} %constant.382) | copy-start | bytes 49156
  113.7 5.0 %copy-start.1 = (f32[16,16,256]{2,1,0:T(8,128)S(1)}, f32[16,16,256]{2,1,0:T(8,128)}, u32[]{:S(2)}) copy-start(f32[16,16,256]{2,1,0:T(8,128)} %param.20) | copy-start | bytes 786436
  113.7 5.0 %copy-start.3 = (f32[16,16,256]{2,1,0:T(8,128)S(1)}, f32[16,16,256]{2,1,0:T(8,128)}, u32[]{:S(2)}) copy-start(f32[16,16,256]{2,1,0:T(8,128)} %param.22) | copy-start | bytes 786436
  115.4 7.4 %copy-start.41 = (s32[128,1]{0,1:T(1,128)S(1)}, s32[128,1]{0,1:T(1,128)}, u32[]{:S(2)}) copy-start(s32[128,1]{0,1:T(1,128)} %squeeze.104) | copy-start | bytes 1540
  115.4 13.3 %copy-start.20 = (pred[16]{0:T(512)(128)(4,1)S(1)}, pred[16]{0:T(512)(128)(4,1)}, u32[]{:S(2)}) copy-start(pred[16]{0:T(512)(128)(4,1)} %copy-done.19) | copy-start | bytes 52
  115.4 13.3 %copy-start.22 = (pred[16]{0:T(512)(128)(4,1)S(1)}, pred[16]{0:T(512)(128)(4,1)}, u32[]{:S(2)}) copy-start(pred[16]{0:T(512)(128)(4,1)} %copy-done.21) | copy-start | bytes 52
  117.2 15.8 %copy-start.16 = (f32[1,2,8,512]{3,2,1,0:T(8,128)S(1)}, f32[1,2,8,512]{3,2,1,0:T(8,128)}, u32[]{:S(2)}) copy-start(f32[1,2,8,512]{3,2,1,0:T(8,128)} %param.25) | copy-start | bytes 98308
  120.5 3.3 %collective-permute-start.11 = (f32[16,256]{1,0:T(8,128)S(1)}, f32[16,256]{1,0:T(8,128)S(1)}, u32[]{:S(2)}, u32[]{:S(2)}) collective-permute-start(f32[16,256]{1,0:T(8,128)S(1)} %bitcast.346), channel_id=1, source_target_pairs={{8,0},{16,8},{24,16},{32,24},{40,32},{48,40},{56,48},{64,56},{72,6... | collective-permute-start | bytes 49160 | tf_op jit(solution)/shard_map/ppermute | solution.py:70
  122.7 5.9 %collective-permute-start.12 = (f32[16,256]{1,0:T(8,128)S(1)}, f32[16,256]{1,0:T(8,128)S(1)}, u32[]{:S(2)}, u32[]{:S(2)}) collective-permute-start(f32[16,256]{1,0:T(8,128)S(1)} %bitcast.347), channel_id=1, source_target_pairs={{248,0},{0,8},{8,16},{16,24},{24,32},{32,40},{40,48},{48,56},{56,6... | collective-permute-start | bytes 49160 | tf_op jit(solution)/shard_map/ppermute | solution.py:70
  128.8 7.7 %copy-start.8 = (f32[16,16,256]{2,0,1:T(8,128)}, f32[16,16,256]{2,0,1:T(8,128)S(1)}, u32[]{:S(2)}) copy-start(f32[16,16,256]{2,0,1:T(8,128)S(1)} %fusion.43) | copy-start | bytes 786436
  129.5 6.0 %collective-permute-start.13 = (f32[16,256]{1,0:T(8,128)}, f32[16,256]{1,0:T(8,128)S(1)}, u32[]{:S(2)}, u32[]{:S(2)}) collective-permute-start(f32[16,256]{1,0:T(8,128)} %get-tuple-element.40), channel_id=1, source_target_pairs={{1,0},{2,1},{3,2},{4,3},{5,4},{6,5},{7,6},{0,7},{9,8},{10,9},{11,1... | collective-permute-start | bytes 49160 | tf_op jit(solution)/shard_map/ppermute | solution.py:73
  130.4 5.0 %collective-permute-start.14 = (f32[16,256]{1,0:T(8,128)}, f32[16,256]{1,0:T(8,128)}, u32[]{:S(2)}, u32[]{:S(2)}) collective-permute-start(f32[16,256]{1,0:T(8,128)} %get-tuple-element.41), channel_id=1, source_target_pairs={{7,0},{0,1},{1,2},{2,3},{3,4},{4,5},{5,6},{6,7},{15,8},{8,9},{9,10... | collective-permute-start | bytes 49160 | tf_op jit(solution)/shard_map/ppermute | solution.py:73
  133.0 3.5 %copy-start.31 = (pred[256]{0:T(512)(128)(4,1)S(1)}, pred[256]{0:T(512)(128)(4,1)}, u32[]{:S(2)}) copy-start(pred[256]{0:T(512)(128)(4,1)} %copy-done.30) | copy-start | bytes 772
  133.0 3.5 %copy-start.33 = (pred[256]{0:T(512)(128)(4,1)S(1)}, pred[256]{0:T(512)(128)(4,1)}, u32[]{:S(2)}) copy-start(pred[256]{0:T(512)(128)(4,1)} %copy-done.32) | copy-start | bytes 772
  141.5 3.1 %copy-start.14 = (f32[128,8]{1,0:T(8,128)S(1)}, f32[128,8]{1,0:T(8,128)}, u32[]{:S(2)}) copy-start(f32[128,8]{1,0:T(8,128)} %gather_fusion.3) | copy-start | bytes 12292
  141.6 3.1 %copy-start.26 = (f32[2,8,8]{2,1,0:T(8,128)S(1)}, f32[2,8,8]{2,1,0:T(8,128)}, u32[]{:S(2)}) copy-start(f32[2,8,8]{2,1,0:T(8,128)} %get-tuple-element.62) | copy-start | bytes 1540
  141.6 3.1 %copy-start.34 = (pred[2,8,8]{2,1,0:T(8,128)(4,1)S(1)}, pred[2,8,8]{2,1,0:T(8,128)(4,1)}, u32[]{:S(2)}) copy-start(pred[2,8,8]{2,1,0:T(8,128)(4,1)} %get-tuple-element.63) | copy-start | bytes 388
  141.8 11.0 %copy-start.10 = (f32[2,8,8,8,8]{4,3,2,1,0:T(8,128)S(1)}, f32[2,8,8,8,8]{4,3,2,1,0:T(8,128)}, u32[]{:S(2)}) copy-start(f32[2,8,8,8,8]{4,3,2,1,0:T(8,128)} %reshape_squeeze.7) | copy-start | bytes 98308
  143.1 2.7 %collective-permute-start.15 = (f32[16,256]{1,0:T(8,128)S(1)}, f32[16,256]{1,0:T(8,128)S(1)}, u32[]{:S(2)}, u32[]{:S(2)}) collective-permute-start(f32[16,256]{1,0:T(8,128)S(1)} %bitcast.344), channel_id=1, source_target_pairs={{8,0},{16,8},{24,16},{32,24},{40,32},{48,40},{56,48},{64,56},{72,6... | collective-permute-start | bytes 49160 | tf_op jit(solution)/shard_map/ppermute | solution.py:70
  143.2 6.0 %collective-permute-start.16 = (f32[16,256]{1,0:T(8,128)S(1)}, f32[16,256]{1,0:T(8,128)S(1)}, u32[]{:S(2)}, u32[]{:S(2)}) collective-permute-start(f32[16,256]{1,0:T(8,128)S(1)} %bitcast.345), channel_id=1, source_target_pairs={{248,0},{0,8},{8,16},{16,24},{24,32},{32,40},{40,48},{48,56},{56,6... | collective-permute-start | bytes 49160 | tf_op jit(solution)/shard_map/ppermute | solution.py:70
  149.2 5.8 %copy-start.11 = (f32[16,16,256]{2,0,1:T(8,128)S(1)}, f32[16,16,256]{2,0,1:T(8,128)}, u32[]{:S(2)}) copy-start(f32[16,16,256]{2,0,1:T(8,128)} %get-tuple-element.15) | copy-start | bytes 786436
  149.3 5.3 %collective-permute-start.17 = (f32[16,256]{1,0:T(8,128)S(1)}, f32[16,256]{1,0:T(8,128)S(1)}, u32[]{:S(2)}, u32[]{:S(2)}) collective-permute-start(f32[16,256]{1,0:T(8,128)S(1)} %get-tuple-element.32), channel_id=1, source_target_pairs={{1,0},{2,1},{3,2},{4,3},{5,4},{6,5},{7,6},{0,7},{9,8},{10,9},{11,1... | collective-permute-start | bytes 49160 | tf_op jit(solution)/shard_map/ppermute | solution.py:73
  149.4 5.3 %collective-permute-start.18 = (f32[16,256]{1,0:T(8,128)S(1)}, f32[16,256]{1,0:T(8,128)S(1)}, u32[]{:S(2)}, u32[]{:S(2)}) collective-permute-start(f32[16,256]{1,0:T(8,128)S(1)} %get-tuple-element.33), channel_id=1, source_target_pairs={{7,0},{0,1},{1,2},{2,3},{3,4},{4,5},{5,6},{6,7},{15,8},{8,9},{9,10... | collective-permute-start | bytes 49160 | tf_op jit(solution)/shard_map/ppermute | solution.py:73
  (16 other events, 25.6 us)

commit v2 on v0

--- a/solution.py
+++ b/solution.py
@@ -129,11 +129,27 @@
 
 
 def apply_operator(field, metric, helm, tables):
-    total = helm * field
-    for axis in range(3):
-        slope = contract(field, tables[axis], axis)
-        total = total + contract(metric[axis] * slope, tables[axis].T, axis)
-    return total
+    shape = field.shape
+    flat = field.reshape(-1, shape[-1])
+    total = helm.reshape(flat.shape) * flat
+    tx, ty, tz = tables
+    for axis, table in ((0, tx), (1, ty)):
+        slope = jnp.dot(table, flat, precision=highest)
+        weighted = metric[axis].reshape(flat.shape) * slope
+        total = total + jnp.dot(table.T, weighted, precision=highest)
+    slope = jnp.dot(flat, tz.T, precision=highest)
+    weighted = metric[2].reshape(flat.shape) * slope
+    total = total + jnp.dot(weighted, tz, precision=highest)
+    return total.reshape(shape)
+
+
+def big_tables(small, shape):
+    X, Y, Z = shape
+    n = small.shape[0]
+    px = np.kron(np.kron(np.eye(X // n, dtype=np.float32), small), np.eye(Y, dtype=np.float32))
+    py = np.kron(np.eye(X, dtype=np.float32), np.kron(np.eye(Y // n, dtype=np.float32), small))
+    pz = np.kron(np.eye(Z // n, dtype=np.float32), small)
+    return tuple(jnp.asarray(t) for t in (px, py, pz))
 
 
 def chebyshev(solution, rhs_local, metric, helm, tables, inverse, first_residual):
@@ -161,16 +177,18 @@
     shape = rhs_local.shape
     nw = lax.axis_size("wide")
     copies = (shape[0] // NP, shape[1] // NP, block_extent() // NP)
-    tables = tuple((repeat_table(derivative, copies[axis]) for axis in range(3)))
-    square_tables = tuple(
-        (repeat_table(derivative * derivative, copies[axis]) for axis in range(3))
-    )
+    tables = big_tables(derivative, shape)
+    sx, sy, sz = big_tables(derivative * derivative, shape)
     down_tables = tuple((repeat_table(linear.T, copies[axis]) for axis in range(3)))
     up_tables = tuple((repeat_table(linear, copies[axis]) for axis in range(3)))
 
-    diagonal = helm
-    for axis in range(3):
-        diagonal = diagonal + contract(metric[axis], square_tables[axis].T, axis)
+    rows = shape[0] * shape[1]
+    diagonal = (
+        helm.reshape(rows, -1)
+        + jnp.dot(sx.T, metric[0].reshape(rows, -1), precision=highest)
+        + jnp.dot(sy.T, metric[1].reshape(rows, -1), precision=highest)
+        + jnp.dot(metric[2].reshape(rows, -1), sz, precision=highest)
+    ).reshape(shape)
     mats = jnp.concatenate(
         [
             block_values[0, 0].reshape(-1),

time: 135 us -> 126 us (0.933)
  local copies, waits for them, and re-layouts: 30.5 us -> 18.1 us
  other arithmetic: 3.38 us -> 7.55 us
  starting transfers between devices: 34.9 us -> 38 us
  matrix products: 18.6 us -> 15.9 us
  waiting for transfers between devices: 32.7 us -> 31.3 us
    dot_general x0 -> x27, matrix products: none -> 12.6 us  [the longest x8 4.79 us: apply_operator(): total = total + jnp.dot(table.T, weighted, precision=highest)]
    dot_general x11 -> x2, matrix products: 6.27 us -> 0.63 us  [contract(): return jnp.einsum('mi,iyz->myz', table, field, precision=highest)]
    dot_general x11 -> x2, matrix products: 5.2 us -> 0.54 us  [contract(): result = jnp.einsum('mk,xynk->xynm', table, grid, precision=highest)]
    reshape x7 -> x1, local copies, waits for them, and re-layouts: 4.2 us -> 0.09 us  [contract(): return result.reshape(shape[0], shape[1], -1)]
    dot_general x11 -> x2, matrix products: 4.49 us -> 0.48 us  [contract(): return jnp.einsum('mj,xjz->xmz', table, field, precision=highest)]
    dot_general x6 -> x0, local copies, waits for them, and re-layouts: 2.92 us -> none  [contract(): result = jnp.einsum('mk,xynk->xynm', table, grid, precision=highest)]
    ppermute x8, starting transfers between devices: 12.8 us -> 15.6 us  [shift(): return lax.ppermute(value, 'wide', pairs)]
    ppermute x8, waiting for transfers between devices: 16.7 us -> 14.2 us  [shift(): return lax.ppermute(value, 'wide', pairs)]
  transfers between devices with their start and end apart: 19 -> 19, of which waited for: 12 -> 13; matrix products, arithmetic and copies ran while one was open for 4% -> 4% of each run, Pallas kernels for 0% -> 0%
where the time goes in v2:
time: 126 us; the launch traced here: 125 us
  starting transfers between devices  38 us (30%)
  waiting for transfers between devices  31.3 us (25%)
  local copies, waits for them, and re-layouts  18.1 us (14%)
  matrix products  15.9 us (13%)
  blocking collectives  12.2 us (10%)
  other arithmetic  7.55 us (6%)
  between operations  1.64 us (1%)
    ppermute x10, starting transfers between devices, shift(): return lax.ppermute(value, 'deep', pairs)  18.5 us
    ppermute x8, starting transfers between devices, shift(): return lax.ppermute(value, 'wide', pairs)  15.6 us
    ppermute x8, waiting for transfers between devices, shift(): return lax.ppermute(value, 'wide', pairs)  14.2 us
    all_to_all x1, blocking collectives, local(): got = lax.all_to_all(back, 'wide', 0, 0, tiled=True)  12.2 us
    all_to_all x1, waiting for transfers between devices, local(): got = lax.all_to_all(sent, 'wide', 0, 0, tiled=True)  9.05 us
    ppermute x10, waiting for transfers between devices, shift(): return lax.ppermute(value, 'deep', pairs)  8.11 us
    unnamed x59, local copies, waits for them, and re-layouts  7.85 us
    dot_general x8, matrix products, apply_operator(): total = total + jnp.dot(table.T, weighted, precision=highest)  4.79 us
  transfers between devices with their start and end apart: 19, of which 13 were waited for; matrix products, arithmetic and copies ran while one was open for 4% of the time, Pallas kernels for 0%

profile of v2, /device:TPU:7, one launch (start us, length us, event | category | flops | bytes accessed | tf_op | source)
XLA Modules:
  0.0 124.7 jit_solution(9727802122933822347)
XLA Ops:
  0.7 1.2 fusion.83
  4.4 1.7 %collective-permute-start.1 = (f32[2,16,256]{2,1,0:T(8,128)S(1)}, f32[2,16,256]{2,1,0:T(8,128)S(1)}, u32[]{:S(2)}, u32[]{:S(2)}) collective-permute-start(f32[2,16,256]{2,1,0:T(8,128)S(1)} %get-tuple-element.14), channel_id=1, source_target_pairs={{248,0},{0,8},{8,16},{16,24},{24,32},{32,40},{40,48},{48,56},{56,6... | collective-permute-start | bytes 98312 | tf_op jit(solution)/shard_map/ppermute | solution.py:70
  6.1 6.5 %collective-permute-start = (f32[2,16,256]{2,1,0:T(8,128)S(1)}, f32[2,16,256]{2,1,0:T(8,128)S(1)}, u32[]{:S(2)}, u32[]{:S(2)}) collective-permute-start(f32[2,16,256]{2,1,0:T(8,128)S(1)} %get-tuple-element.13), channel_id=1, source_target_pairs={{8,0},{16,8},{24,16},{32,24},{40,32},{48,40},{56,48},{64,56},{72,6... | collective-permute-start | bytes 98312 | tf_op jit(solution)/shard_map/ppermute | solution.py:70
  12.6 0.7 copy-done.23
  13.3 0.7 copy-done.24
  15.0 1.0 collective-permute-start.2
  15.9 2.0 %collective-permute-start.3 = (f32[2,16,256]{2,1,0:T(8,128)S(1)}, f32[2,16,256]{2,1,0:T(8,128)S(1)}, u32[]{:S(2)}, u32[]{:S(2)}) collective-permute-start(f32[2,16,256]{2,1,0:T(8,128)S(1)} %bitcast.284), channel_id=1, source_target_pairs={{7,0},{0,1},{1,2},{2,3},{3,4},{4,5},{5,6},{6,7},{15,8},{8,9},{9,10... | collective-permute-start | bytes 98312 | tf_op jit(solution)/shard_map/ppermute | solution.py:73
  18.0 1.1 concatenate.143
  20.9 0.9 copy-done
  23.5 0.6 convolution_add_fusion.11
  24.1 0.6 convolution_add_fusion.10
  25.2 4.1 %collective-permute-start.4 = (f32[16,256]{1,0:T(8,128)S(1)}, f32[16,256]{1,0:T(8,128)S(1)}, u32[]{:S(2)}, u32[]{:S(2)}) collective-permute-start(f32[16,256]{1,0:T(8,128)S(1)} %get-tuple-element.37), channel_id=1, source_target_pairs={{8,0},{16,8},{24,16},{32,24},{40,32},{48,40},{56,48},{64,56},{72,6... | collective-permute-start | bytes 49160 | tf_op jit(solution)/shard_map/ppermute | solution.py:70
  29.4 0.7 fusion.73
  30.1 0.7 compare_and_fusion
  30.8 4.4 %collective-permute-done.5 = f32[16,256]{1,0:T(8,128)S(1)} collective-permute-done((f32[16,256]{1,0:T(8,128)S(1)}, f32[16,256]{1,0:T(8,128)S(1)}, u32[]{:S(2)}, u32[]{:S(2)}) %collective-permute-start.5) | collective-permute-done | bytes 16416 | tf_op jit(solution)/shard_map/ppermute | solution.py:70
  35.3 1.9 %collective-permute-start.6 = (f32[16,256]{1,0:T(8,128)S(1)}, f32[16,256]{1,0:T(8,128)S(1)}, u32[]{:S(2)}, u32[]{:S(2)}) collective-permute-start(f32[16,256]{1,0:T(8,128)S(1)} %bitcast.293), channel_id=1, source_target_pairs={{1,0},{2,1},{3,2},{4,3},{5,4},{6,5},{7,6},{0,7},{9,8},{10,9},{11,1... | collective-permute-start | bytes 49160 | tf_op jit(solution)/shard_map/ppermute | solution.py:73
  37.2 2.4 %collective-permute-start.7 = (f32[16,256]{1,0:T(8,128)S(1)}, f32[16,256]{1,0:T(8,128)S(1)}, u32[]{:S(2)}, u32[]{:S(2)}) collective-permute-start(f32[16,256]{1,0:T(8,128)S(1)} %bitcast.299), channel_id=1, source_target_pairs={{7,0},{0,1},{1,2},{2,3},{3,4},{4,5},{5,6},{6,7},{15,8},{8,9},{9,10... | collective-permute-start | bytes 49160 | tf_op jit(solution)/shard_map/ppermute | solution.py:73
  39.7 0.8 collective-permute-done.7
  43.0 0.6 convolution_add_fusion.8
  43.6 0.6 convolution_add_fusion.7
  44.6 0.6 copy-done.20
  46.7 3.0 %collective-permute-start.8 = (f32[4,4,64]{2,1,0:T(4,128)S(1)}, f32[4,4,64]{2,1,0:T(4,128)S(1)}, u32[]{:S(2)}, u32[]{:S(2)}) collective-permute-start(f32[4,4,64]{2,1,0:T(4,128)S(1)} %reshape.416), channel_id=1, source_target_pairs={{7,0},{0,1},{1,2},{2,3},{3,4},{4,5},{5,6},{6,7},{15,8},{8,9},{9,10... | collective-permute-start | bytes 12296 | tf_op jit(solution)/shard_map/ppermute | solution.py:73
  49.7 0.8 collective-permute-done.8
  50.5 3.5 %collective-permute-done.9 = f32[4,4,64]{2,1,0:T(4,128)S(1)} collective-permute-done((f32[4,4,64]{2,1,0:T(4,128)S(1)}, f32[4,4,64]{2,1,0:T(4,128)S(1)}, u32[]{:S(2)}, u32[]{:S(2)}) %collective-permute-start.9) | collective-permute-done | bytes 4128 | tf_op jit(solution)/shard_map/ppermute | solution.py:73
  55.1 0.8 copy.117
  56.0 3.9 %all-to-all-start = ((f32[32,3,4,3]{2,1,3,0:T(4,128)}), f32[32,3,4,3]{2,1,3,0:T(4,128)S(1)}, u32[]{:S(2)}, u32[]{:S(2)}) async-start(f32[32,3,4,3]{2,1,3,0:T(4,128)} %copy.117), calls=%async_computation | async-start | bytes 393216 | tf_op jit(solution)/shard_map/all_to_all | solution.py:226
  60.6 9.0 %all-to-all-done = f32[32,3,4,3]{2,1,3,0:T(4,128)S(1)} async-done(((f32[32,3,4,3]{2,1,3,0:T(4,128)}), f32[32,3,4,3]{2,1,3,0:T(4,128)S(1)}, u32[]{:S(2)}, u32[]{:S(2)}) %all-to-all-start) | async-done | bytes 4640 | tf_op jit(solution)/shard_map/all_to_all | solution.py:226
  70.6 1.0 gather_fusion
  71.5 0.8 select_multiply_fusion
  72.4 1.7 %fusion.1 = f32[3,8,1,8,1]{3,2,4,1,0:T(1,128)S(1)} fusion(f32[3,8,8,8,1]{3,4,2,1,0:T(1,128)S(1)} %bitcast.274, f32[1,8,8,8,8]{4,3,2,1,0:T(8,128)S(1)} %concatenate.144, f32[2,8,8,8,8]{4,3,2,1,0:T(8,128)S(1)} %copy-done.5), kind=kOutput, calls=%fused_computation.33 | convolution fusion | flops 159744 | bytes 56064 | tf_op jit(solution)/shard_map/yxkij,yxkj,yxk->yxi/dot_general | solution.py:246
  74.7 0.6 gather_fusion.1
  75.6 12.2 %all_to_all.10 = f32[32,3,3]{2,1,0:T(4,128)S(1)} all-to-all(f32[32,3,3]{2,1,0:T(4,128)S(1)} %copy.125), channel_id=1, replica_groups=mesh['wide'=32,'deep'=8] {'wide'}, dimensions={0} | all-to-all | bytes 2304 | tf_op jit(solution)/shard_map/all_to_all | solution.py:252
  92.2 0.6 convolution_add_fusion.5
  93.9 1.1 collective-permute-start.10
  95.0 0.7 collective-permute-start.11
  95.7 1.5 %collective-permute-done.10 = f32[16,256]{1,0:T(8,128)S(1)} collective-permute-done((f32[16,256]{1,0:T(8,128)S(1)}, f32[16,256]{1,0:T(8,128)S(1)}, u32[]{:S(2)}, u32[]{:S(2)}) %collective-permute-start.10) | collective-permute-done | bytes 16416 | tf_op jit(solution)/shard_map/ppermute | solution.py:70
  97.2 3.8 %collective-permute-done.11 = f32[16,256]{1,0:T(8,128)S(1)} collective-permute-done((f32[16,256]{1,0:T(8,128)S(1)}, f32[16,256]{1,0:T(8,128)S(1)}, u32[]{:S(2)}, u32[]{:S(2)}) %collective-permute-start.11) | collective-permute-done | bytes 16416 | tf_op jit(solution)/shard_map/ppermute | solution.py:70
  100.9 0.7 copy-done.10
  101.8 1.0 collective-permute-start.12
  102.7 3.2 %collective-permute-start.13 = (f32[16,256]{1,0:T(8,128)S(1)}, f32[16,256]{1,0:T(8,128)S(1)}, u32[]{:S(2)}, u32[]{:S(2)}) collective-permute-start(f32[16,256]{1,0:T(8,128)S(1)} %bitcast.298), channel_id=1, source_target_pairs={{7,0},{0,1},{1,2},{2,3},{3,4},{4,5},{5,6},{6,7},{15,8},{8,9},{9,10... | collective-permute-start | bytes 49160 | tf_op jit(solution)/shard_map/ppermute | solution.py:73
  105.9 1.4 %collective-permute-done.12 = f32[16,256]{1,0:T(8,128)S(1)} collective-permute-done((f32[16,256]{1,0:T(8,128)S(1)}, f32[16,256]{1,0:T(8,128)S(1)}, u32[]{:S(2)}, u32[]{:S(2)}) %collective-permute-start.12) | collective-permute-done | bytes 16416 | tf_op jit(solution)/shard_map/ppermute | solution.py:73
  111.6 1.5 %collective-permute-start.15 = (f32[16,256]{1,0:T(8,128)S(1)}, f32[16,256]{1,0:T(8,128)S(1)}, u32[]{:S(2)}, u32[]{:S(2)}) collective-permute-start(f32[16,256]{1,0:T(8,128)S(1)} %get-tuple-element.22), channel_id=1, source_target_pairs={{248,0},{0,8},{8,16},{16,24},{24,32},{32,40},{40,48},{48,56},{56,6... | collective-permute-start | bytes 49160 | tf_op jit(solution)/shard_map/ppermute | solution.py:70
  113.0 1.1 collective-permute-done.14
  114.2 3.4 %collective-permute-done.15 = f32[16,256]{1,0:T(8,128)S(1)} collective-permute-done((f32[16,256]{1,0:T(8,128)S(1)}, f32[16,256]{1,0:T(8,128)S(1)}, u32[]{:S(2)}, u32[]{:S(2)}) %collective-permute-start.15) | collective-permute-done | bytes 16416 | tf_op jit(solution)/shard_map/ppermute | solution.py:70
  117.8 4.1 %collective-permute-start.17 = (f32[16,256]{1,0:T(8,128)S(1)}, f32[16,256]{1,0:T(8,128)S(1)}, u32[]{:S(2)}, u32[]{:S(2)}) collective-permute-start(f32[16,256]{1,0:T(8,128)S(1)} %bitcast.296), channel_id=1, source_target_pairs={{7,0},{0,1},{1,2},{2,3},{3,4},{4,5},{5,6},{6,7},{15,8},{8,9},{9,10... | collective-permute-start | bytes 49160 | tf_op jit(solution)/shard_map/ppermute | solution.py:73
  121.9 0.6 reshape.426
  122.5 0.7 collective-permute-done.16
  123.7 1.0 fusion.51
  (210 shorter events, 25.9 us)
Async XLA Ops:
  0.6 1.2 copy-start.6
  0.6 1.3 %copy-start.3 = (f32[16,16,256]{2,1,0:T(8,128)S(1)}, f32[16,16,256]{2,1,0:T(8,128)}, u32[]{:S(2)}) copy-start(f32[16,16,256]{2,1,0:T(8,128)} %param.23) | copy-start | bytes 786436
  1.9 0.9 copy-start.4
  3.5 1.0 copy-start.2
  4.4 8.2 %copy-start.8 = (f32[1,2,8,512]{3,2,1,0:T(8,128)S(1)}, f32[1,2,8,512]{3,2,1,0:T(8,128)}, u32[]{:S(2)}) copy-start(f32[1,2,8,512]{3,2,1,0:T(8,128)} %param.26) | copy-start | bytes 98308
  4.4 10.2 %collective-permute-start.1 = (f32[2,16,256]{2,1,0:T(8,128)S(1)}, f32[2,16,256]{2,1,0:T(8,128)S(1)}, u32[]{:S(2)}, u32[]{:S(2)}) collective-permute-start(f32[2,16,256]{2,1,0:T(8,128)S(1)} %get-tuple-element.14), channel_id=1, source_target_pairs={{248,0},{0,8},{8,16},{16,24},{24,32},{32,40},{40,48},{48,56},{56,6... | collective-permute-start | bytes 98312 | tf_op jit(solution)/shard_map/ppermute | solution.py:70
  6.1 6.5 %copy-start.13 = (s32[1,2,8,8]{3,2,1,0:T(8,128)S(1)}, s32[1,2,8,8]{3,2,1,0:T(8,128)}, u32[]{:S(2)}) copy-start(s32[1,2,8,8]{3,2,1,0:T(8,128)} %param.24) | copy-start | bytes 1540
  6.1 8.5 %collective-permute-start = (f32[2,16,256]{2,1,0:T(8,128)S(1)}, f32[2,16,256]{2,1,0:T(8,128)S(1)}, u32[]{:S(2)}, u32[]{:S(2)}) collective-permute-start(f32[2,16,256]{2,1,0:T(8,128)S(1)} %get-tuple-element.13), channel_id=1, source_target_pairs={{8,0},{16,8},{24,16},{32,24},{40,32},{48,40},{56,48},{64,56},{72,6... | collective-permute-start | bytes 98312 | tf_op jit(solution)/shard_map/ppermute | solution.py:70
  12.6 0.7 copy-start.23
  13.3 0.7 copy-start.24
  14.6 26.8 %copy-start.9 = (pred[16]{0:T(512)(128)(4,1)}, pred[16]{0:T(512)(128)(4,1)S(1)}, u32[]{:S(2)}) copy-start(pred[16]{0:T(512)(128)(4,1)S(1)} %get-tuple-element.49) | copy-start | bytes 52
  14.6 26.8 %copy-start.11 = (pred[16]{0:T(512)(128)(4,1)}, pred[16]{0:T(512)(128)(4,1)S(1)}, u32[]{:S(2)}) copy-start(pred[16]{0:T(512)(128)(4,1)S(1)} %get-tuple-element.50) | copy-start | bytes 52
  15.0 4.8 %collective-permute-start.2 = (f32[12360]{0:T(1024)S(1)}, f32[12360]{0:T(1024)S(1)}, u32[]{:S(2)}, u32[]{:S(2)}) collective-permute-start(f32[12360]{0:T(1024)S(1)} %concatenate.132), channel_id=1, source_target_pairs={{1,0},{2,1},{3,2},{4,3},{5,4},{6,5},{7,6},{0,7},{9,8},{10,9},{11,1... | collective-permute-start | bytes 148328 | tf_op jit(solution)/shard_map/ppermute | solution.py:73
  15.9 3.3 %collective-permute-start.3 = (f32[2,16,256]{2,1,0:T(8,128)S(1)}, f32[2,16,256]{2,1,0:T(8,128)S(1)}, u32[]{:S(2)}, u32[]{:S(2)}) collective-permute-start(f32[2,16,256]{2,1,0:T(8,128)S(1)} %bitcast.284), channel_id=1, source_target_pairs={{7,0},{0,1},{1,2},{2,3},{3,4},{4,5},{5,6},{6,7},{15,8},{8,9},{9,10... | collective-permute-start | bytes 98312 | tf_op jit(solution)/shard_map/ppermute | solution.py:73
  17.9 23.5 %copy-start.16 = (pred[256]{0:T(512)(128)(4,1)}, pred[256]{0:T(512)(128)(4,1)S(1)}, u32[]{:S(2)}) copy-start(pred[256]{0:T(512)(128)(4,1)S(1)} %get-tuple-element.51) | copy-start | bytes 772
  17.9 23.5 %copy-start.18 = (pred[256]{0:T(512)(128)(4,1)}, pred[256]{0:T(512)(128)(4,1)S(1)}, u32[]{:S(2)}) copy-start(pred[256]{0:T(512)(128)(4,1)S(1)} %get-tuple-element.52) | copy-start | bytes 772
  17.9 1.1 copy-start.22
  20.8 1.0 copy-start
  22.2 1.0 copy-start.1
  25.2 5.6 %collective-permute-start.4 = (f32[16,256]{1,0:T(8,128)S(1)}, f32[16,256]{1,0:T(8,128)S(1)}, u32[]{:S(2)}, u32[]{:S(2)}) collective-permute-start(f32[16,256]{1,0:T(8,128)S(1)} %get-tuple-element.37), channel_id=1, source_target_pairs={{8,0},{16,8},{24,16},{32,24},{40,32},{48,40},{56,48},{64,56},{72,6... | collective-permute-start | bytes 49160 | tf_op jit(solution)/shard_map/ppermute | solution.py:70
  29.3 5.9 %collective-permute-start.5 = (f32[16,256]{1,0:T(8,128)S(1)}, f32[16,256]{1,0:T(8,128)S(1)}, u32[]{:S(2)}, u32[]{:S(2)}) collective-permute-start(f32[16,256]{1,0:T(8,128)S(1)} %get-tuple-element.38), channel_id=1, source_target_pairs={{248,0},{0,8},{8,16},{16,24},{24,32},{32,40},{40,48},{48,56},{56,6... | collective-permute-start | bytes 49160 | tf_op jit(solution)/shard_map/ppermute | solution.py:70
  35.3 5.7 %collective-permute-start.6 = (f32[16,256]{1,0:T(8,128)S(1)}, f32[16,256]{1,0:T(8,128)S(1)}, u32[]{:S(2)}, u32[]{:S(2)}) collective-permute-start(f32[16,256]{1,0:T(8,128)S(1)} %bitcast.293), channel_id=1, source_target_pairs={{1,0},{2,1},{3,2},{4,3},{5,4},{6,5},{7,6},{0,7},{9,8},{10,9},{11,1... | collective-permute-start | bytes 49160 | tf_op jit(solution)/shard_map/ppermute | solution.py:73
  37.2 3.2 %collective-permute-start.7 = (f32[16,256]{1,0:T(8,128)S(1)}, f32[16,256]{1,0:T(8,128)S(1)}, u32[]{:S(2)}, u32[]{:S(2)}) collective-permute-start(f32[16,256]{1,0:T(8,128)S(1)} %bitcast.299), channel_id=1, source_target_pairs={{7,0},{0,1},{1,2},{2,3},{3,4},{4,5},{5,6},{6,7},{15,8},{8,9},{9,10... | collective-permute-start | bytes 49160 | tf_op jit(solution)/shard_map/ppermute | solution.py:73
  44.6 0.7 copy-start.20
  45.7 0.7 copy-start.15
  46.7 3.8 %collective-permute-start.8 = (f32[4,4,64]{2,1,0:T(4,128)S(1)}, f32[4,4,64]{2,1,0:T(4,128)S(1)}, u32[]{:S(2)}, u32[]{:S(2)}) collective-permute-start(f32[4,4,64]{2,1,0:T(4,128)S(1)} %reshape.416), channel_id=1, source_target_pairs={{7,0},{0,1},{1,2},{2,3},{3,4},{4,5},{5,6},{6,7},{15,8},{8,9},{9,10... | collective-permute-start | bytes 12296 | tf_op jit(solution)/shard_map/ppermute | solution.py:73
  49.7 4.3 %collective-permute-start.9 = (f32[4,4,64]{2,1,0:T(4,128)S(1)}, f32[4,4,64]{2,1,0:T(4,128)S(1)}, u32[]{:S(2)}, u32[]{:S(2)}) collective-permute-start(f32[4,4,64]{2,1,0:T(4,128)S(1)} %reshape.416), channel_id=1, source_target_pairs={{1,0},{2,1},{3,2},{4,3},{5,4},{6,5},{7,6},{0,7},{9,8},{10,9},{11,1... | collective-permute-start | bytes 12296 | tf_op jit(solution)/shard_map/ppermute | solution.py:73
  56.0 13.7 %all-to-all-start = ((f32[32,3,4,3]{2,1,3,0:T(4,128)}), f32[32,3,4,3]{2,1,3,0:T(4,128)S(1)}, u32[]{:S(2)}, u32[]{:S(2)}) async-start(f32[32,3,4,3]{2,1,3,0:T(4,128)} %copy.117), calls=%async_computation | async-start | bytes 393216 | tf_op jit(solution)/shard_map/all_to_all | solution.py:226
  70.5 1.8 %copy-start.5 = (f32[2,8,8,8,8]{4,3,2,1,0:T(8,128)S(1)}, f32[2,8,8,8,8]{4,3,2,1,0:T(8,128)}, u32[]{:S(2)}) copy-start(f32[2,8,8,8,8]{4,3,2,1,0:T(8,128)} %concatenate.143) | copy-start | bytes 98308
  74.0 0.7 copy-start.7
  88.6 0.7 copy-start.21
  89.9 0.7 copy-start.14
  93.9 3.2 %collective-permute-start.10 = (f32[16,256]{1,0:T(8,128)S(1)}, f32[16,256]{1,0:T(8,128)S(1)}, u32[]{:S(2)}, u32[]{:S(2)}) collective-permute-start(f32[16,256]{1,0:T(8,128)S(1)} %get-tuple-element.29), channel_id=1, source_target_pairs={{8,0},{16,8},{24,16},{32,24},{40,32},{48,40},{56,48},{64,56},{72,6... | collective-permute-start | bytes 49160 | tf_op jit(solution)/shard_map/ppermute | solution.py:70
  95.0 5.9 %collective-permute-start.11 = (f32[16,256]{1,0:T(8,128)S(1)}, f32[16,256]{1,0:T(8,128)S(1)}, u32[]{:S(2)}, u32[]{:S(2)}) collective-permute-start(f32[16,256]{1,0:T(8,128)S(1)} %get-tuple-element.30), channel_id=1, source_target_pairs={{248,0},{0,8},{8,16},{16,24},{24,32},{32,40},{40,48},{48,56},{56,6... | collective-permute-start | bytes 49160 | tf_op jit(solution)/shard_map/ppermute | solution.py:70
  100.9 0.7 copy-start.10
  100.9 0.7 copy-start.12
  101.8 5.5 %collective-permute-start.12 = (f32[16,256]{1,0:T(8,128)S(1)}, f32[16,256]{1,0:T(8,128)S(1)}, u32[]{:S(2)}, u32[]{:S(2)}) collective-permute-start(f32[16,256]{1,0:T(8,128)S(1)} %bitcast.297), channel_id=1, source_target_pairs={{1,0},{2,1},{3,2},{4,3},{5,4},{6,5},{7,6},{0,7},{9,8},{10,9},{11,1... | collective-permute-start | bytes 49160 | tf_op jit(solution)/shard_map/ppermute | solution.py:73
  102.7 4.6 %collective-permute-start.13 = (f32[16,256]{1,0:T(8,128)S(1)}, f32[16,256]{1,0:T(8,128)S(1)}, u32[]{:S(2)}, u32[]{:S(2)}) collective-permute-start(f32[16,256]{1,0:T(8,128)S(1)} %bitcast.298), channel_id=1, source_target_pairs={{7,0},{0,1},{1,2},{2,3},{3,4},{4,5},{5,6},{6,7},{15,8},{8,9},{9,10... | collective-permute-start | bytes 49160 | tf_op jit(solution)/shard_map/ppermute | solution.py:73
  107.7 0.6 copy-start.17
  107.7 0.6 copy-start.19
  111.5 2.7 %collective-permute-start.14 = (f32[16,256]{1,0:T(8,128)S(1)}, f32[16,256]{1,0:T(8,128)S(1)}, u32[]{:S(2)}, u32[]{:S(2)}) collective-permute-start(f32[16,256]{1,0:T(8,128)S(1)} %get-tuple-element.21), channel_id=1, source_target_pairs={{8,0},{16,8},{24,16},{32,24},{40,32},{48,40},{56,48},{64,56},{72,6... | collective-permute-start | bytes 49160 | tf_op jit(solution)/shard_map/ppermute | solution.py:70
  111.6 6.0 %collective-permute-start.15 = (f32[16,256]{1,0:T(8,128)S(1)}, f32[16,256]{1,0:T(8,128)S(1)}, u32[]{:S(2)}, u32[]{:S(2)}) collective-permute-start(f32[16,256]{1,0:T(8,128)S(1)} %get-tuple-element.22), channel_id=1, source_target_pairs={{248,0},{0,8},{8,16},{16,24},{24,32},{32,40},{40,48},{48,56},{56,6... | collective-permute-start | bytes 49160 | tf_op jit(solution)/shard_map/ppermute | solution.py:70
  117.7 5.5 %collective-permute-start.16 = (f32[16,256]{1,0:T(8,128)S(1)}, f32[16,256]{1,0:T(8,128)S(1)}, u32[]{:S(2)}, u32[]{:S(2)}) collective-permute-start(f32[16,256]{1,0:T(8,128)S(1)} %bitcast.294), channel_id=1, source_target_pairs={{1,0},{2,1},{3,2},{4,3},{5,4},{6,5},{7,6},{0,7},{9,8},{10,9},{11,1... | collective-permute-start | bytes 49160 | tf_op jit(solution)/shard_map/ppermute | solution.py:73
  117.8 5.5 %collective-permute-start.17 = (f32[16,256]{1,0:T(8,128)S(1)}, f32[16,256]{1,0:T(8,128)S(1)}, u32[]{:S(2)}, u32[]{:S(2)}) collective-permute-start(f32[16,256]{1,0:T(8,128)S(1)} %bitcast.296), channel_id=1, source_target_pairs={{7,0},{0,1},{1,2},{2,3},{3,4},{4,5},{5,6},{6,7},{15,8},{8,9},{9,10... | collective-permute-start | bytes 49160 | tf_op jit(solution)/shard_map/ppermute | solution.py:73

commit v3 on v2

--- a/solution.py
+++ b/solution.py
@@ -12,6 +12,7 @@
 upper_bound = 6.0
 lower_bound = 0.6
 highest = lax.Precision.HIGHEST
+fast = lax.Precision.HIGH
 
 
 def gll_tables(count):
@@ -134,12 +135,12 @@
     total = helm.reshape(flat.shape) * flat
     tx, ty, tz = tables
     for axis, table in ((0, tx), (1, ty)):
-        slope = jnp.dot(table, flat, precision=highest)
+        slope = jnp.dot(table, flat, precision=fast)
         weighted = metric[axis].reshape(flat.shape) * slope
-        total = total + jnp.dot(table.T, weighted, precision=highest)
-    slope = jnp.dot(flat, tz.T, precision=highest)
+        total = total + jnp.dot(table.T, weighted, precision=fast)
+    slope = jnp.dot(flat, tz.T, precision=fast)
     weighted = metric[2].reshape(flat.shape) * slope
-    total = total + jnp.dot(weighted, tz, precision=highest)
+    total = total + jnp.dot(weighted, tz, precision=fast)
     return total.reshape(shape)
 
 
@@ -185,9 +186,9 @@
     rows = shape[0] * shape[1]
     diagonal = (
         helm.reshape(rows, -1)
-        + jnp.dot(sx.T, metric[0].reshape(rows, -1), precision=highest)
-        + jnp.dot(sy.T, metric[1].reshape(rows, -1), precision=highest)
-        + jnp.dot(metric[2].reshape(rows, -1), sz, precision=highest)
+        + jnp.dot(sx.T, metric[0].reshape(rows, -1), precision=fast)
+        + jnp.dot(sy.T, metric[1].reshape(rows, -1), precision=fast)
+        + jnp.dot(metric[2].reshape(rows, -1), sz, precision=fast)
     ).reshape(shape)
     mats = jnp.concatenate(
         [

time: 126 us -> 122 us (0.968)
  matrix products: 15.9 us -> 12.1 us
    dot_general x27, matrix products: 12.6 us -> 8.81 us  [the longest x8 3.13 us: apply_operator(): total = total + jnp.dot(table.T, weighted, precision=fast)]
where the time goes in v3:
time: 122 us; the launch traced here: 121 us
  starting transfers between devices  37.9 us (31%)
  waiting for transfers between devices  31.2 us (26%)
  local copies, waits for them, and re-layouts  18.5 us (15%)
  blocking collectives  12.2 us (10%)
  matrix products  12.1 us (10%)
  other arithmetic  7.55 us (6%)
  between operations  1.64 us (1%)
    ppermute x10, starting transfers between devices, shift(): return lax.ppermute(value, 'deep', pairs)  18.5 us
    ppermute x8, starting transfers between devices, shift(): return lax.ppermute(value, 'wide', pairs)  15.4 us
    ppermute x8, waiting for transfers between devices, shift(): return lax.ppermute(value, 'wide', pairs)  14.2 us
    all_to_all x1, blocking collectives, local(): got = lax.all_to_all(back, 'wide', 0, 0, tiled=True)  12.2 us
    all_to_all x1, waiting for transfers between devices, local(): got = lax.all_to_all(sent, 'wide', 0, 0, tiled=True)  8.87 us
    unnamed x59, local copies, waits for them, and re-layouts  8.25 us
    ppermute x10, waiting for transfers between devices, shift(): return lax.ppermute(value, 'deep', pairs)  8.11 us
    all_to_all x1, starting transfers between devices, local(): got = lax.all_to_all(sent, 'wide', 0, 0, tiled=True)  4.05 us
  transfers between devices with their start and end apart: 19, of which 13 were waited for; matrix products, arithmetic and copies ran while one was open for 4% of the time, Pallas kernels for 0%

profile of v3, /device:TPU:7, one launch (start us, length us, event | category | flops | bytes accessed | tf_op | source)
XLA Modules:
  0.0 121.1 jit_solution(1516136361653982621)
XLA Ops:
  0.7 1.2 %fusion.83 = (f32[1,16,16,256]{3,2,1,0:T(8,128)S(1)}, f32[1,16,16,256]{3,2,1,0:T(8,128)S(1)}, f32[1,16,16,256]{3,2,1,0:T(8,128)S(1)}) fusion(f32[3,16,16,256]{3,2,1,0:T(8,128)} %param.22), kind=kLoop, calls=%fused_computation.231 | loop fusion | bytes 1572864 | tf_op jit(solution)/shard_map/slice | solution.py:191
  3.5 0.6 copy-done.2
  4.2 1.7 %collective-permute-start.1 = (f32[2,16,256]{2,1,0:T(8,128)S(1)}, f32[2,16,256]{2,1,0:T(8,128)S(1)}, u32[]{:S(2)}, u32[]{:S(2)}) collective-permute-start(f32[2,16,256]{2,1,0:T(8,128)S(1)} %get-tuple-element.14), channel_id=1, source_target_pairs={{248,0},{0,8},{8,16},{16,24},{24,32},{32,40},{40,48},{48,56},{56,6... | collective-permute-start | bytes 98312 | tf_op jit(solution)/shard_map/ppermute | solution.py:71
  5.9 6.5 %collective-permute-start = (f32[2,16,256]{2,1,0:T(8,128)S(1)}, f32[2,16,256]{2,1,0:T(8,128)S(1)}, u32[]{:S(2)}, u32[]{:S(2)}) collective-permute-start(f32[2,16,256]{2,1,0:T(8,128)S(1)} %get-tuple-element.13), channel_id=1, source_target_pairs={{8,0},{16,8},{24,16},{32,24},{40,32},{48,40},{56,48},{64,56},{72,6... | collective-permute-start | bytes 98312 | tf_op jit(solution)/shard_map/ppermute | solution.py:71
  12.4 0.7 copy-done.23
  13.1 0.7 copy-done.24
  13.7 0.6 pad_clamp_fusion
  14.8 1.0 collective-permute-start.2
  15.7 2.0 %collective-permute-start.3 = (f32[2,16,256]{2,1,0:T(8,128)S(1)}, f32[2,16,256]{2,1,0:T(8,128)S(1)}, u32[]{:S(2)}, u32[]{:S(2)}) collective-permute-start(f32[2,16,256]{2,1,0:T(8,128)S(1)} %bitcast.284), channel_id=1, source_target_pairs={{7,0},{0,1},{1,2},{2,3},{3,4},{4,5},{5,6},{6,7},{15,8},{8,9},{9,10... | collective-permute-start | bytes 98312 | tf_op jit(solution)/shard_map/ppermute | solution.py:74
  17.7 1.1 concatenate.143
  20.7 0.9 copy-done
  22.2 0.6 copy-done.1
  24.2 4.1 %collective-permute-start.4 = (f32[16,256]{1,0:T(8,128)S(1)}, f32[16,256]{1,0:T(8,128)S(1)}, u32[]{:S(2)}, u32[]{:S(2)}) collective-permute-start(f32[16,256]{1,0:T(8,128)S(1)} %get-tuple-element.37), channel_id=1, source_target_pairs={{8,0},{16,8},{24,16},{32,24},{40,32},{48,40},{56,48},{64,56},{72,6... | collective-permute-start | bytes 49160 | tf_op jit(solution)/shard_map/ppermute | solution.py:71
  28.5 0.7 fusion.73
  29.2 0.7 compare_and_fusion
  29.8 4.4 %collective-permute-done.5 = f32[16,256]{1,0:T(8,128)S(1)} collective-permute-done((f32[16,256]{1,0:T(8,128)S(1)}, f32[16,256]{1,0:T(8,128)S(1)}, u32[]{:S(2)}, u32[]{:S(2)}) %collective-permute-start.5) | collective-permute-done | bytes 16416 | tf_op jit(solution)/shard_map/ppermute | solution.py:71
  34.4 1.9 %collective-permute-start.6 = (f32[16,256]{1,0:T(8,128)S(1)}, f32[16,256]{1,0:T(8,128)S(1)}, u32[]{:S(2)}, u32[]{:S(2)}) collective-permute-start(f32[16,256]{1,0:T(8,128)S(1)} %bitcast.293), channel_id=1, source_target_pairs={{1,0},{2,1},{3,2},{4,3},{5,4},{6,5},{7,6},{0,7},{9,8},{10,9},{11,1... | collective-permute-start | bytes 49160 | tf_op jit(solution)/shard_map/ppermute | solution.py:74
  36.3 2.4 %collective-permute-start.7 = (f32[16,256]{1,0:T(8,128)S(1)}, f32[16,256]{1,0:T(8,128)S(1)}, u32[]{:S(2)}, u32[]{:S(2)}) collective-permute-start(f32[16,256]{1,0:T(8,128)S(1)} %bitcast.299), channel_id=1, source_target_pairs={{7,0},{0,1},{1,2},{2,3},{3,4},{4,5},{5,6},{6,7},{15,8},{8,9},{9,10... | collective-permute-start | bytes 49160 | tf_op jit(solution)/shard_map/ppermute | solution.py:74
  38.8 0.8 collective-permute-done.7
  42.9 0.6 copy-done.20
  44.9 3.0 %collective-permute-start.8 = (f32[4,4,64]{2,1,0:T(4,128)S(1)}, f32[4,4,64]{2,1,0:T(4,128)S(1)}, u32[]{:S(2)}, u32[]{:S(2)}) collective-permute-start(f32[4,4,64]{2,1,0:T(4,128)S(1)} %reshape.416), channel_id=1, source_target_pairs={{7,0},{0,1},{1,2},{2,3},{3,4},{4,5},{5,6},{6,7},{15,8},{8,9},{9,10... | collective-permute-start | bytes 12296 | tf_op jit(solution)/shard_map/ppermute | solution.py:74
  48.0 0.8 collective-permute-done.8
  48.7 3.5 %collective-permute-done.9 = f32[4,4,64]{2,1,0:T(4,128)S(1)} collective-permute-done((f32[4,4,64]{2,1,0:T(4,128)S(1)}, f32[4,4,64]{2,1,0:T(4,128)S(1)}, u32[]{:S(2)}, u32[]{:S(2)}) %collective-permute-start.9) | collective-permute-done | bytes 4128 | tf_op jit(solution)/shard_map/ppermute | solution.py:74
  53.4 0.8 copy.117
  54.2 4.0 %all-to-all-start = ((f32[32,3,4,3]{2,1,3,0:T(4,128)}), f32[32,3,4,3]{2,1,3,0:T(4,128)S(1)}, u32[]{:S(2)}, u32[]{:S(2)}) async-start(f32[32,3,4,3]{2,1,3,0:T(4,128)} %copy.117), calls=%async_computation | async-start | bytes 393216 | tf_op jit(solution)/shard_map/all_to_all | solution.py:227
  58.3 0.6 pad_clamp_fusion.1
  59.0 8.9 %all-to-all-done = f32[32,3,4,3]{2,1,3,0:T(4,128)S(1)} async-done(((f32[32,3,4,3]{2,1,3,0:T(4,128)}), f32[32,3,4,3]{2,1,3,0:T(4,128)S(1)}, u32[]{:S(2)}, u32[]{:S(2)}) %all-to-all-start) | async-done | bytes 4640 | tf_op jit(solution)/shard_map/all_to_all | solution.py:227
  68.8 1.0 gather_fusion
  69.8 0.8 select_multiply_fusion
  70.6 1.7 %fusion.1 = f32[3,8,1,8,1]{3,2,4,1,0:T(1,128)S(1)} fusion(f32[3,8,8,8,1]{3,4,2,1,0:T(1,128)S(1)} %bitcast.274, f32[1,8,8,8,8]{4,3,2,1,0:T(8,128)S(1)} %concatenate.144, f32[2,8,8,8,8]{4,3,2,1,0:T(8,128)S(1)} %copy-done.5), kind=kOutput, calls=%fused_computation.33 | convolution fusion | flops 159744 | bytes 56064 | tf_op jit(solution)/shard_map/yxkij,yxkj,yxk->yxi/dot_general | solution.py:247
  72.9 0.6 gather_fusion.1
  73.8 12.2 %all_to_all.10 = f32[32,3,3]{2,1,0:T(4,128)S(1)} all-to-all(f32[32,3,3]{2,1,0:T(4,128)S(1)} %copy.125), channel_id=1, replica_groups=mesh['wide'=32,'deep'=8] {'wide'}, dimensions={0} | all-to-all | bytes 2304 | tf_op jit(solution)/shard_map/all_to_all | solution.py:253
  87.0 0.6 copy-done.21
  91.3 0.9 collective-permute-start.10
  92.2 0.7 collective-permute-start.11
  92.9 1.5 %collective-permute-done.10 = f32[16,256]{1,0:T(8,128)S(1)} collective-permute-done((f32[16,256]{1,0:T(8,128)S(1)}, f32[16,256]{1,0:T(8,128)S(1)}, u32[]{:S(2)}, u32[]{:S(2)}) %collective-permute-start.10) | collective-permute-done | bytes 16416 | tf_op jit(solution)/shard_map/ppermute | solution.py:71
  94.4 3.8 %collective-permute-done.11 = f32[16,256]{1,0:T(8,128)S(1)} collective-permute-done((f32[16,256]{1,0:T(8,128)S(1)}, f32[16,256]{1,0:T(8,128)S(1)}, u32[]{:S(2)}, u32[]{:S(2)}) %collective-permute-start.11) | collective-permute-done | bytes 16416 | tf_op jit(solution)/shard_map/ppermute | solution.py:71
  98.1 0.7 copy-done.10
  99.0 0.9 collective-permute-start.12
  99.9 3.2 %collective-permute-start.13 = (f32[16,256]{1,0:T(8,128)S(1)}, f32[16,256]{1,0:T(8,128)S(1)}, u32[]{:S(2)}, u32[]{:S(2)}) collective-permute-start(f32[16,256]{1,0:T(8,128)S(1)} %bitcast.298), channel_id=1, source_target_pairs={{7,0},{0,1},{1,2},{2,3},{3,4},{4,5},{5,6},{6,7},{15,8},{8,9},{9,10... | collective-permute-start | bytes 49160 | tf_op jit(solution)/shard_map/ppermute | solution.py:74
  103.1 1.4 %collective-permute-done.12 = f32[16,256]{1,0:T(8,128)S(1)} collective-permute-done((f32[16,256]{1,0:T(8,128)S(1)}, f32[16,256]{1,0:T(8,128)S(1)}, u32[]{:S(2)}, u32[]{:S(2)}) %collective-permute-start.12) | collective-permute-done | bytes 16416 | tf_op jit(solution)/shard_map/ppermute | solution.py:74
  108.0 1.5 %collective-permute-start.15 = (f32[16,256]{1,0:T(8,128)S(1)}, f32[16,256]{1,0:T(8,128)S(1)}, u32[]{:S(2)}, u32[]{:S(2)}) collective-permute-start(f32[16,256]{1,0:T(8,128)S(1)} %get-tuple-element.22), channel_id=1, source_target_pairs={{248,0},{0,8},{8,16},{16,24},{24,32},{32,40},{40,48},{48,56},{56,6... | collective-permute-start | bytes 49160 | tf_op jit(solution)/shard_map/ppermute | solution.py:71
  109.4 1.1 collective-permute-done.14
  110.6 3.4 %collective-permute-done.15 = f32[16,256]{1,0:T(8,128)S(1)} collective-permute-done((f32[16,256]{1,0:T(8,128)S(1)}, f32[16,256]{1,0:T(8,128)S(1)}, u32[]{:S(2)}, u32[]{:S(2)}) %collective-permute-start.15) | collective-permute-done | bytes 16416 | tf_op jit(solution)/shard_map/ppermute | solution.py:71
  114.2 4.1 %collective-permute-start.17 = (f32[16,256]{1,0:T(8,128)S(1)}, f32[16,256]{1,0:T(8,128)S(1)}, u32[]{:S(2)}, u32[]{:S(2)}) collective-permute-start(f32[16,256]{1,0:T(8,128)S(1)} %bitcast.296), channel_id=1, source_target_pairs={{7,0},{0,1},{1,2},{2,3},{3,4},{4,5},{5,6},{6,7},{15,8},{8,9},{9,10... | collective-permute-start | bytes 49160 | tf_op jit(solution)/shard_map/ppermute | solution.py:74
  118.3 0.6 reshape.426
  118.9 0.7 collective-permute-done.16
  120.1 1.0 fusion.51
  (210 shorter events, 22.5 us)
Async XLA Ops:
  0.6 1.2 %copy-start.6 = (f32[256,256]{1,0:T(8,128)S(1)}, f32[256,256]{1,0:T(8,128)}, u32[]{:S(2)}) copy-start(f32[256,256]{1,0:T(8,128)} %constant.210.clone) | copy-start | bytes 786436
  0.6 1.3 %copy-start.3 = (f32[16,16,256]{2,1,0:T(8,128)S(1)}, f32[16,16,256]{2,1,0:T(8,128)}, u32[]{:S(2)}) copy-start(f32[16,16,256]{2,1,0:T(8,128)} %param.23) | copy-start | bytes 786436
  1.9 0.9 copy-start.4
  3.2 1.0 copy-start.2
  4.2 8.2 %copy-start.8 = (f32[1,2,8,512]{3,2,1,0:T(8,128)S(1)}, f32[1,2,8,512]{3,2,1,0:T(8,128)}, u32[]{:S(2)}) copy-start(f32[1,2,8,512]{3,2,1,0:T(8,128)} %param.26) | copy-start | bytes 98308
  4.2 10.2 %collective-permute-start.1 = (f32[2,16,256]{2,1,0:T(8,128)S(1)}, f32[2,16,256]{2,1,0:T(8,128)S(1)}, u32[]{:S(2)}, u32[]{:S(2)}) collective-permute-start(f32[2,16,256]{2,1,0:T(8,128)S(1)} %get-tuple-element.14), channel_id=1, source_target_pairs={{248,0},{0,8},{8,16},{16,24},{24,32},{32,40},{40,48},{48,56},{56,6... | collective-permute-start | bytes 98312 | tf_op jit(solution)/shard_map/ppermute | solution.py:71
  5.9 6.5 %copy-start.13 = (s32[1,2,8,8]{3,2,1,0:T(8,128)S(1)}, s32[1,2,8,8]{3,2,1,0:T(8,128)}, u32[]{:S(2)}) copy-start(s32[1,2,8,8]{3,2,1,0:T(8,128)} %param.24) | copy-start | bytes 1540
  5.9 8.5 %collective-permute-start = (f32[2,16,256]{2,1,0:T(8,128)S(1)}, f32[2,16,256]{2,1,0:T(8,128)S(1)}, u32[]{:S(2)}, u32[]{:S(2)}) collective-permute-start(f32[2,16,256]{2,1,0:T(8,128)S(1)} %get-tuple-element.13), channel_id=1, source_target_pairs={{8,0},{16,8},{24,16},{32,24},{40,32},{48,40},{56,48},{64,56},{72,6... | collective-permute-start | bytes 98312 | tf_op jit(solution)/shard_map/ppermute | solution.py:71
  12.4 0.7 copy-start.23
  13.1 0.7 copy-start.24
  14.4 26.1 %copy-start.9 = (pred[16]{0:T(512)(128)(4,1)}, pred[16]{0:T(512)(128)(4,1)S(1)}, u32[]{:S(2)}) copy-start(pred[16]{0:T(512)(128)(4,1)S(1)} %get-tuple-element.49) | copy-start | bytes 52
  14.4 26.1 %copy-start.11 = (pred[16]{0:T(512)(128)(4,1)}, pred[16]{0:T(512)(128)(4,1)S(1)}, u32[]{:S(2)}) copy-start(pred[16]{0:T(512)(128)(4,1)S(1)} %get-tuple-element.50) | copy-start | bytes 52
  14.8 4.8 %collective-permute-start.2 = (f32[12360]{0:T(1024)S(1)}, f32[12360]{0:T(1024)S(1)}, u32[]{:S(2)}, u32[]{:S(2)}) collective-permute-start(f32[12360]{0:T(1024)S(1)} %concatenate.132), channel_id=1, source_target_pairs={{1,0},{2,1},{3,2},{4,3},{5,4},{6,5},{7,6},{0,7},{9,8},{10,9},{11,1... | collective-permute-start | bytes 148328 | tf_op jit(solution)/shard_map/ppermute | solution.py:74
  15.7 3.3 %collective-permute-start.3 = (f32[2,16,256]{2,1,0:T(8,128)S(1)}, f32[2,16,256]{2,1,0:T(8,128)S(1)}, u32[]{:S(2)}, u32[]{:S(2)}) collective-permute-start(f32[2,16,256]{2,1,0:T(8,128)S(1)} %bitcast.284), channel_id=1, source_target_pairs={{7,0},{0,1},{1,2},{2,3},{3,4},{4,5},{5,6},{6,7},{15,8},{8,9},{9,10... | collective-permute-start | bytes 98312 | tf_op jit(solution)/shard_map/ppermute | solution.py:74
  17.7 22.7 %copy-start.16 = (pred[256]{0:T(512)(128)(4,1)}, pred[256]{0:T(512)(128)(4,1)S(1)}, u32[]{:S(2)}) copy-start(pred[256]{0:T(512)(128)(4,1)S(1)} %get-tuple-element.51) | copy-start | bytes 772
  17.7 22.7 %copy-start.18 = (pred[256]{0:T(512)(128)(4,1)}, pred[256]{0:T(512)(128)(4,1)S(1)}, u32[]{:S(2)}) copy-start(pred[256]{0:T(512)(128)(4,1)S(1)} %get-tuple-element.52) | copy-start | bytes 772
  17.7 1.1 copy-start.22
  20.6 1.0 copy-start
  21.8 1.0 copy-start.1
  24.2 5.6 %collective-permute-start.4 = (f32[16,256]{1,0:T(8,128)S(1)}, f32[16,256]{1,0:T(8,128)S(1)}, u32[]{:S(2)}, u32[]{:S(2)}) collective-permute-start(f32[16,256]{1,0:T(8,128)S(1)} %get-tuple-element.37), channel_id=1, source_target_pairs={{8,0},{16,8},{24,16},{32,24},{40,32},{48,40},{56,48},{64,56},{72,6... | collective-permute-start | bytes 49160 | tf_op jit(solution)/shard_map/ppermute | solution.py:71
  28.3 5.9 %collective-permute-start.5 = (f32[16,256]{1,0:T(8,128)S(1)}, f32[16,256]{1,0:T(8,128)S(1)}, u32[]{:S(2)}, u32[]{:S(2)}) collective-permute-start(f32[16,256]{1,0:T(8,128)S(1)} %get-tuple-element.38), channel_id=1, source_target_pairs={{248,0},{0,8},{8,16},{16,24},{24,32},{32,40},{40,48},{48,56},{56,6... | collective-permute-start | bytes 49160 | tf_op jit(solution)/shard_map/ppermute | solution.py:71
  34.4 5.7 %collective-permute-start.6 = (f32[16,256]{1,0:T(8,128)S(1)}, f32[16,256]{1,0:T(8,128)S(1)}, u32[]{:S(2)}, u32[]{:S(2)}) collective-permute-start(f32[16,256]{1,0:T(8,128)S(1)} %bitcast.293), channel_id=1, source_target_pairs={{1,0},{2,1},{3,2},{4,3},{5,4},{6,5},{7,6},{0,7},{9,8},{10,9},{11,1... | collective-permute-start | bytes 49160 | tf_op jit(solution)/shard_map/ppermute | solution.py:74
  36.3 3.2 %collective-permute-start.7 = (f32[16,256]{1,0:T(8,128)S(1)}, f32[16,256]{1,0:T(8,128)S(1)}, u32[]{:S(2)}, u32[]{:S(2)}) collective-permute-start(f32[16,256]{1,0:T(8,128)S(1)} %bitcast.299), channel_id=1, source_target_pairs={{7,0},{0,1},{1,2},{2,3},{3,4},{4,5},{5,6},{6,7},{15,8},{8,9},{9,10... | collective-permute-start | bytes 49160 | tf_op jit(solution)/shard_map/ppermute | solution.py:74
  42.8 0.7 copy-start.20
  43.9 0.7 copy-start.15
  44.9 3.8 %collective-permute-start.8 = (f32[4,4,64]{2,1,0:T(4,128)S(1)}, f32[4,4,64]{2,1,0:T(4,128)S(1)}, u32[]{:S(2)}, u32[]{:S(2)}) collective-permute-start(f32[4,4,64]{2,1,0:T(4,128)S(1)} %reshape.416), channel_id=1, source_target_pairs={{7,0},{0,1},{1,2},{2,3},{3,4},{4,5},{5,6},{6,7},{15,8},{8,9},{9,10... | collective-permute-start | bytes 12296 | tf_op jit(solution)/shard_map/ppermute | solution.py:74
  47.9 4.3 %collective-permute-start.9 = (f32[4,4,64]{2,1,0:T(4,128)S(1)}, f32[4,4,64]{2,1,0:T(4,128)S(1)}, u32[]{:S(2)}, u32[]{:S(2)}) collective-permute-start(f32[4,4,64]{2,1,0:T(4,128)S(1)} %reshape.416), channel_id=1, source_target_pairs={{1,0},{2,1},{3,2},{4,3},{5,4},{6,5},{7,6},{0,7},{9,8},{10,9},{11,1... | collective-permute-start | bytes 12296 | tf_op jit(solution)/shard_map/ppermute | solution.py:74
  54.2 13.7 %all-to-all-start = ((f32[32,3,4,3]{2,1,3,0:T(4,128)}), f32[32,3,4,3]{2,1,3,0:T(4,128)S(1)}, u32[]{:S(2)}, u32[]{:S(2)}) async-start(f32[32,3,4,3]{2,1,3,0:T(4,128)} %copy.117), calls=%async_computation | async-start | bytes 393216 | tf_op jit(solution)/shard_map/all_to_all | solution.py:227
  68.8 1.8 %copy-start.5 = (f32[2,8,8,8,8]{4,3,2,1,0:T(8,128)S(1)}, f32[2,8,8,8,8]{4,3,2,1,0:T(8,128)}, u32[]{:S(2)}) copy-start(f32[2,8,8,8,8]{4,3,2,1,0:T(8,128)} %concatenate.143) | copy-start | bytes 98308
  72.3 0.7 copy-start.7
  86.9 0.7 copy-start.21
  88.1 0.7 copy-start.14
  91.3 3.0 %collective-permute-start.10 = (f32[16,256]{1,0:T(8,128)S(1)}, f32[16,256]{1,0:T(8,128)S(1)}, u32[]{:S(2)}, u32[]{:S(2)}) collective-permute-start(f32[16,256]{1,0:T(8,128)S(1)} %get-tuple-element.29), channel_id=1, source_target_pairs={{8,0},{16,8},{24,16},{32,24},{40,32},{48,40},{56,48},{64,56},{72,6... | collective-permute-start | bytes 49160 | tf_op jit(solution)/shard_map/ppermute | solution.py:71
  92.2 5.9 %collective-permute-start.11 = (f32[16,256]{1,0:T(8,128)S(1)}, f32[16,256]{1,0:T(8,128)S(1)}, u32[]{:S(2)}, u32[]{:S(2)}) collective-permute-start(f32[16,256]{1,0:T(8,128)S(1)} %get-tuple-element.30), channel_id=1, source_target_pairs={{248,0},{0,8},{8,16},{16,24},{24,32},{32,40},{40,48},{48,56},{56,6... | collective-permute-start | bytes 49160 | tf_op jit(solution)/shard_map/ppermute | solution.py:71
  98.1 0.7 copy-start.10
  98.1 0.7 copy-start.12
  99.0 5.5 %collective-permute-start.12 = (f32[16,256]{1,0:T(8,128)S(1)}, f32[16,256]{1,0:T(8,128)S(1)}, u32[]{:S(2)}, u32[]{:S(2)}) collective-permute-start(f32[16,256]{1,0:T(8,128)S(1)} %bitcast.297), channel_id=1, source_target_pairs={{1,0},{2,1},{3,2},{4,3},{5,4},{6,5},{7,6},{0,7},{9,8},{10,9},{11,1... | collective-permute-start | bytes 49160 | tf_op jit(solution)/shard_map/ppermute | solution.py:74
  99.9 4.6 %collective-permute-start.13 = (f32[16,256]{1,0:T(8,128)S(1)}, f32[16,256]{1,0:T(8,128)S(1)}, u32[]{:S(2)}, u32[]{:S(2)}) collective-permute-start(f32[16,256]{1,0:T(8,128)S(1)} %bitcast.298), channel_id=1, source_target_pairs={{7,0},{0,1},{1,2},{2,3},{3,4},{4,5},{5,6},{6,7},{15,8},{8,9},{9,10... | collective-permute-start | bytes 49160 | tf_op jit(solution)/shard_map/ppermute | solution.py:74
  104.9 0.6 copy-start.17
  104.9 0.6 copy-start.19
  107.9 2.7 %collective-permute-start.14 = (f32[16,256]{1,0:T(8,128)S(1)}, f32[16,256]{1,0:T(8,128)S(1)}, u32[]{:S(2)}, u32[]{:S(2)}) collective-permute-start(f32[16,256]{1,0:T(8,128)S(1)} %get-tuple-element.21), channel_id=1, source_target_pairs={{8,0},{16,8},{24,16},{32,24},{40,32},{48,40},{56,48},{64,56},{72,6... | collective-permute-start | bytes 49160 | tf_op jit(solution)/shard_map/ppermute | solution.py:71
  108.0 6.0 %collective-permute-start.15 = (f32[16,256]{1,0:T(8,128)S(1)}, f32[16,256]{1,0:T(8,128)S(1)}, u32[]{:S(2)}, u32[]{:S(2)}) collective-permute-start(f32[16,256]{1,0:T(8,128)S(1)} %get-tuple-element.22), channel_id=1, source_target_pairs={{248,0},{0,8},{8,16},{16,24},{24,32},{32,40},{40,48},{48,56},{56,6... | collective-permute-start | bytes 49160 | tf_op jit(solution)/shard_map/ppermute | solution.py:71
  114.1 5.5 %collective-permute-start.16 = (f32[16,256]{1,0:T(8,128)S(1)}, f32[16,256]{1,0:T(8,128)S(1)}, u32[]{:S(2)}, u32[]{:S(2)}) collective-permute-start(f32[16,256]{1,0:T(8,128)S(1)} %bitcast.294), channel_id=1, source_target_pairs={{1,0},{2,1},{3,2},{4,3},{5,4},{6,5},{7,6},{0,7},{9,8},{10,9},{11,1... | collective-permute-start | bytes 49160 | tf_op jit(solution)/shard_map/ppermute | solution.py:74
  114.2 5.5 %collective-permute-start.17 = (f32[16,256]{1,0:T(8,128)S(1)}, f32[16,256]{1,0:T(8,128)S(1)}, u32[]{:S(2)}, u32[]{:S(2)}) collective-permute-start(f32[16,256]{1,0:T(8,128)S(1)} %bitcast.296), channel_id=1, source_target_pairs={{7,0},{0,1},{1,2},{2,3},{3,4},{4,5},{5,6},{6,7},{15,8},{8,9},{9,10... | collective-permute-start | bytes 49160 | tf_op jit(solution)/shard_map/ppermute | solution.py:74

commit v4 on v3

--- a/solution.py
+++ b/solution.py
@@ -87,11 +87,12 @@
     return index.reshape(shape)
 
 
-def assemble(field, count, carry=None):
+def assemble(field, count, carry=None, faces=None):
     nd = field.ndim
     X, Y, Z = field.shape[-3:]
-    lx = shift(field[..., -1, :, :], -1, 0)
-    rx = shift(field[..., 0, :, :], 1, 0)
+    low, high = (field[..., 0, :, :], field[..., -1, :, :]) if faces is None else faces
+    lx = shift(high, -1, 0)
+    rx = shift(low, 1, 0)
     ext = jnp.concatenate([lx[..., None, :, :], field, rx[..., None, :, :]], axis=-3)
     hi = node_mask(X, count, count - 1, nd - 3, nd)
     lo = node_mask(X, count, 0, nd - 3, nd)
@@ -133,7 +134,7 @@
     shape = field.shape
     flat = field.reshape(-1, shape[-1])
     total = helm.reshape(flat.shape) * flat
-    tx, ty, tz = tables
+    tx, ty, tz = tables[:3]
     for axis, table in ((0, tx), (1, ty)):
         slope = jnp.dot(table, flat, precision=fast)
         weighted = metric[axis].reshape(flat.shape) * slope
@@ -144,6 +145,27 @@
     return total.reshape(shape)
 
 
+def operator_faces(field, metric, helm, tables, face_y):
+    X, Y, Z = field.shape
+    flat = field.reshape(X * Y, Z)
+    tx, ty, tz = tables
+
+    def planes(a):
+        a = a.reshape(X * Y, -1)
+        return jnp.concatenate([a[:Y], a[-Y:]], axis=0)
+
+    slope = jnp.dot(tx, flat, precision=fast)
+    weighted = metric[0].reshape(flat.shape) * slope
+    total = jnp.dot(planes(tx.T), weighted, precision=fast)
+    face = planes(field)
+    total = total + planes(helm) * face
+    slope = jnp.dot(face_y, face, precision=fast)
+    total = total + jnp.dot(face_y.T, planes(metric[1]) * slope, precision=fast)
+    slope = jnp.dot(face, tz.T, precision=fast)
+    total = total + jnp.dot(planes(metric[2]) * slope, tz, precision=fast)
+    return total
+
+
 def big_tables(small, shape):
     X, Y, Z = shape
     n = small.shape[0]
@@ -151,6 +173,15 @@
     py = np.kron(np.eye(X, dtype=np.float32), np.kron(np.eye(Y // n, dtype=np.float32), small))
     pz = np.kron(np.eye(Z // n, dtype=np.float32), small)
     return tuple(jnp.asarray(t) for t in (px, py, pz))
+
+
+def residual_of(solution, rhs_local, metric, helm, tables):
+    X, Y, Z = solution.shape
+    full = rhs_local - apply_operator(solution, metric, helm, tables)
+    rhs_flat = rhs_local.reshape(X * Y, Z)
+    rhs_faces = jnp.concatenate([rhs_flat[:Y], rhs_flat[-Y:]], axis=0)
+    faces = rhs_faces - operator_faces(solution, metric, helm, tables[:3], tables[3])
+    return assemble(full, NP, faces=(faces[:Y], faces[Y:]))
 
 
 def chebyshev(solution, rhs_local, metric, helm, tables, inverse, first_residual):
@@ -161,10 +192,10 @@
     if first_residual is not None:
         residual = first_residual
     else:
-        residual = assemble(rhs_local - apply_operator(solution, metric, helm, tables), NP)
+        residual = residual_of(solution, rhs_local, metric, helm, tables)
     update = inverse * residual / centre
     solution = solution + update
-    residual = assemble(rhs_local - apply_operator(solution, metric, helm, tables), NP)
+    residual = residual_of(solution, rhs_local, metric, helm, tables)
     weight_next = 1.0 / (2.0 * aspect - weight_prev)
     update = (
         weight_next * weight_prev * update + 2.0 * weight_next / half_width * inverse * residual
@@ -179,6 +210,8 @@
     nw = lax.axis_size("wide")
     copies = (shape[0] // NP, shape[1] // NP, block_extent() // NP)
     tables = big_tables(derivative, shape)
+    face_y = jnp.asarray(np.kron(np.eye(2 * shape[1] // NP, dtype=np.float32), derivative))
+    tables = tables + (face_y,)
     sx, sy, sz = big_tables(derivative * derivative, shape)
     down_tables = tuple((repeat_table(linear.T, copies[axis]) for axis in range(3)))
     up_tables = tuple((repeat_table(linear, copies[axis]) for axis in range(3)))

time: 122 us -> 125 us (1.025)
  matrix products: 12.1 us -> 16.5 us
  other arithmetic: 7.55 us -> 4.46 us
  local copies, waits for them, and re-layouts: 18.5 us -> 21.2 us
  starting transfers between devices: 37.9 us -> 36.2 us
    dot_general x0 -> x18, matrix products: none -> 3.42 us  [the longest x6 0.81 us: operator_faces(): slope = jnp.dot(face_y, face, precision=fast)]
    ppermute x10, waiting for transfers between devices: 8.11 us -> 11.1 us  [shift(): return lax.ppermute(value, 'deep', pairs)]
    ppermute x8, waiting for transfers between devices: 14.2 us -> 12 us  [shift(): return lax.ppermute(value, 'wide', pairs)]
    ppermute x8, starting transfers between devices: 15.4 us -> 13.7 us  [shift(): return lax.ppermute(value, 'wide', pairs)]
    unnamed x59 -> x49, local copies, waits for them, and re-layouts: 8.25 us -> 9.69 us
  transfers between devices with their start and end apart: 19 -> 19, of which waited for: 13 -> 13; matrix products, arithmetic and copies ran while one was open for 4% -> 6% of each run, Pallas kernels for 0% -> 0%
where the time goes in v4:
time: 125 us; the launch traced here: 124 us
  starting transfers between devices  36.2 us (29%)
  waiting for transfers between devices  32 us (26%)
  local copies, waits for them, and re-layouts  21.2 us (17%)
  matrix products  16.5 us (13%)
  blocking collectives  12.2 us (10%)
  other arithmetic  4.46 us (4%)
  between operations  1.78 us (1%)
    ppermute x10, starting transfers between devices, shift(): return lax.ppermute(value, 'deep', pairs)  18.5 us
    ppermute x8, starting transfers between devices, shift(): return lax.ppermute(value, 'wide', pairs)  13.7 us
    all_to_all x1, blocking collectives, local(): got = lax.all_to_all(back, 'wide', 0, 0, tiled=True)  12.2 us
    ppermute x8, waiting for transfers between devices, shift(): return lax.ppermute(value, 'wide', pairs)  12 us
    ppermute x10, waiting for transfers between devices, shift(): return lax.ppermute(value, 'deep', pairs)  11.1 us
    unnamed x49, local copies, waits for them, and re-layouts  9.69 us
    all_to_all x1, waiting for transfers between devices, local(): got = lax.all_to_all(sent, 'wide', 0, 0, tiled=True)  8.92 us
    all_to_all x1, starting transfers between devices, local(): got = lax.all_to_all(sent, 'wide', 0, 0, tiled=True)  4.05 us
  transfers between devices with their start and end apart: 19, of which 13 were waited for; matrix products, arithmetic and copies ran while one was open for 6% of the time, Pallas kernels for 0%

profile of v4, /device:TPU:7, one launch (start us, length us, event | category | flops | bytes accessed | tf_op | source)
XLA Modules:
  0.0 124.3 jit_solution(18119012726111039934)
XLA Ops:
  0.7 1.2 fusion.99
  2.3 0.6 copy-done.4
  3.5 0.6 copy-done.2
  4.2 1.6 %collective-permute-start.1 = (f32[2,16,256]{2,1,0:T(8,128)S(1)}, f32[2,16,256]{2,1,0:T(8,128)S(1)}, u32[]{:S(2)}, u32[]{:S(2)}) collective-permute-start(f32[2,16,256]{2,1,0:T(8,128)S(1)} %get-tuple-element.18), channel_id=1, source_target_pairs={{248,0},{0,8},{8,16},{16,24},{24,32},{32,40},{40,48},{48,56},{56,6... | collective-permute-start | bytes 98312 | tf_op jit(solution)/shard_map/ppermute | solution.py:71
  5.8 6.5 %collective-permute-start = (f32[2,16,256]{2,1,0:T(8,128)S(1)}, f32[2,16,256]{2,1,0:T(8,128)S(1)}, u32[]{:S(2)}, u32[]{:S(2)}) collective-permute-start(f32[2,16,256]{2,1,0:T(8,128)S(1)} %get-tuple-element.17), channel_id=1, source_target_pairs={{8,0},{16,8},{24,16},{32,24},{40,32},{48,40},{56,48},{64,56},{72,6... | collective-permute-start | bytes 98312 | tf_op jit(solution)/shard_map/ppermute | solution.py:71
  12.3 0.8 slice_bitcast_fusion.9
  13.1 0.7 copy-done.11
  13.9 0.7 copy-done.12
  14.6 0.7 copy-done.18
  15.2 0.7 copy-done.19
  16.3 1.0 collective-permute-start.2
  17.3 2.0 %collective-permute-start.3 = (f32[2,16,256]{2,1,0:T(8,128)S(1)}, f32[2,16,256]{2,1,0:T(8,128)S(1)}, u32[]{:S(2)}, u32[]{:S(2)}) collective-permute-start(f32[2,16,256]{2,1,0:T(8,128)S(1)} %bitcast.353), channel_id=1, source_target_pairs={{7,0},{0,1},{1,2},{2,3},{3,4},{4,5},{5,6},{6,7},{15,8},{8,9},{9,10... | collective-permute-start | bytes 98312 | tf_op jit(solution)/shard_map/ppermute | solution.py:74
  19.3 1.1 concatenate.183
  22.2 0.9 copy-done
  23.8 0.7 copy-done.9
  25.8 0.6 copy-done.6
  27.6 2.5 %collective-permute-start.4 = (f32[16,256]{1,0:T(8,128)S(1)}, f32[16,256]{1,0:T(8,128)S(1)}, u32[]{:S(2)}, u32[]{:S(2)}) collective-permute-start(f32[16,256]{1,0:T(8,128)S(1)} %get-tuple-element.55), channel_id=1, source_target_pairs={{8,0},{16,8},{24,16},{32,24},{40,32},{48,40},{56,48},{64,56},{72,6... | collective-permute-start | bytes 49160 | tf_op jit(solution)/shard_map/ppermute | solution.py:71
  31.5 4.4 %collective-permute-done.5 = f32[16,256]{1,0:T(8,128)S(1)} collective-permute-done((f32[16,256]{1,0:T(8,128)S(1)}, f32[16,256]{1,0:T(8,128)S(1)}, u32[]{:S(2)}, u32[]{:S(2)}) %collective-permute-start.5) | collective-permute-done | bytes 16416 | tf_op jit(solution)/shard_map/ppermute | solution.py:71
  36.1 1.9 %collective-permute-start.6 = (f32[16,256]{1,0:T(8,128)S(1)}, f32[16,256]{1,0:T(8,128)S(1)}, u32[]{:S(2)}, u32[]{:S(2)}) collective-permute-start(f32[16,256]{1,0:T(8,128)S(1)} %bitcast.362), channel_id=1, source_target_pairs={{1,0},{2,1},{3,2},{4,3},{5,4},{6,5},{7,6},{0,7},{9,8},{10,9},{11,1... | collective-permute-start | bytes 49160 | tf_op jit(solution)/shard_map/ppermute | solution.py:74
  38.0 2.4 %collective-permute-start.7 = (f32[16,256]{1,0:T(8,128)S(1)}, f32[16,256]{1,0:T(8,128)S(1)}, u32[]{:S(2)}, u32[]{:S(2)}) collective-permute-start(f32[16,256]{1,0:T(8,128)S(1)} %bitcast.368), channel_id=1, source_target_pairs={{7,0},{0,1},{1,2},{2,3},{3,4},{4,5},{5,6},{6,7},{15,8},{8,9},{9,10... | collective-permute-start | bytes 49160 | tf_op jit(solution)/shard_map/ppermute | solution.py:74
  40.5 0.8 collective-permute-done.7
  44.5 0.6 copy-done.15
  45.7 0.5 copy-done.14
  46.6 3.0 %collective-permute-start.8 = (f32[4,4,64]{2,1,0:T(4,128)S(1)}, f32[4,4,64]{2,1,0:T(4,128)S(1)}, u32[]{:S(2)}, u32[]{:S(2)}) collective-permute-start(f32[4,4,64]{2,1,0:T(4,128)S(1)} %reshape.442), channel_id=1, source_target_pairs={{7,0},{0,1},{1,2},{2,3},{3,4},{4,5},{5,6},{6,7},{15,8},{8,9},{9,10... | collective-permute-start | bytes 12296 | tf_op jit(solution)/shard_map/ppermute | solution.py:74
  49.6 0.8 collective-permute-done.8
  50.4 3.5 %collective-permute-done.9 = f32[4,4,64]{2,1,0:T(4,128)S(1)} collective-permute-done((f32[4,4,64]{2,1,0:T(4,128)S(1)}, f32[4,4,64]{2,1,0:T(4,128)S(1)}, u32[]{:S(2)}, u32[]{:S(2)}) %collective-permute-start.9) | collective-permute-done | bytes 4128 | tf_op jit(solution)/shard_map/ppermute | solution.py:74
  55.0 0.8 copy.122
  55.9 4.0 %all-to-all-start = ((f32[32,3,4,3]{2,1,3,0:T(4,128)}), f32[32,3,4,3]{2,1,3,0:T(4,128)S(1)}, u32[]{:S(2)}, u32[]{:S(2)}) async-start(f32[32,3,4,3]{2,1,3,0:T(4,128)} %copy.122), calls=%async_computation | async-start | bytes 393216 | tf_op jit(solution)/shard_map/all_to_all | solution.py:260
  59.9 0.9 concatenate.184
  60.8 8.9 %all-to-all-done = f32[32,3,4,3]{2,1,3,0:T(4,128)S(1)} async-done(((f32[32,3,4,3]{2,1,3,0:T(4,128)}), f32[32,3,4,3]{2,1,3,0:T(4,128)S(1)}, u32[]{:S(2)}, u32[]{:S(2)}) %all-to-all-start) | async-done | bytes 4640 | tf_op jit(solution)/shard_map/all_to_all | solution.py:260
  70.6 0.7 gather_fusion
  71.7 2.6 %fusion.10 = f32[3,8,1,8,1]{3,2,4,1,0:T(1,128)S(1)} fusion(f32[3,8,8,8,1]{3,4,2,1,0:T(1,128)S(1)} %bitcast.343, f32[1,8,8,8,8]{4,3,2,1,0:T(8,128)} %concatenate.184, f32[2,8,8,8,8]{4,3,2,1,0:T(8,128)S(1)} %copy-done.5), kind=kOutput, calls=%fused_computation.57 | convolution fusion | flops 159744 | bytes 56064 | tf_op jit(solution)/shard_map/yxkij,yxkj,yxk->yxi/dot_general | solution.py:280
  74.4 0.6 gather_fusion.1
  75.3 12.2 %all_to_all.10 = f32[32,3,3]{2,1,0:T(4,128)S(1)} all-to-all(f32[32,3,3]{2,1,0:T(4,128)S(1)} %copy.130), channel_id=1, replica_groups=mesh['wide'=32,'deep'=8] {'wide'}, dimensions={0} | all-to-all | bytes 2304 | tf_op jit(solution)/shard_map/all_to_all | solution.py:286
  88.4 0.6 copy-done.16
  89.8 0.5 copy-done.13
  92.9 0.9 collective-permute-start.10
  93.8 0.7 collective-permute-start.11
  95.9 3.8 %collective-permute-done.11 = f32[16,256]{1,0:T(8,128)S(1)} collective-permute-done((f32[16,256]{1,0:T(8,128)S(1)}, f32[16,256]{1,0:T(8,128)S(1)}, u32[]{:S(2)}, u32[]{:S(2)}) %collective-permute-start.11) | collective-permute-done | bytes 16416 | tf_op jit(solution)/shard_map/ppermute | solution.py:71
  99.8 0.9 collective-permute-start.12
  100.8 3.2 %collective-permute-start.13 = (f32[16,256]{1,0:T(8,128)S(1)}, f32[16,256]{1,0:T(8,128)S(1)}, u32[]{:S(2)}, u32[]{:S(2)}) collective-permute-start(f32[16,256]{1,0:T(8,128)S(1)} %bitcast.367), channel_id=1, source_target_pairs={{7,0},{0,1},{1,2},{2,3},{3,4},{4,5},{5,6},{6,7},{15,8},{8,9},{9,10... | collective-permute-start | bytes 49160 | tf_op jit(solution)/shard_map/ppermute | solution.py:74
  103.9 1.4 %collective-permute-done.12 = f32[16,256]{1,0:T(8,128)S(1)} collective-permute-done((f32[16,256]{1,0:T(8,128)S(1)}, f32[16,256]{1,0:T(8,128)S(1)}, u32[]{:S(2)}, u32[]{:S(2)}) %collective-permute-start.12) | collective-permute-done | bytes 16416 | tf_op jit(solution)/shard_map/ppermute | solution.py:74
  108.3 1.5 %collective-permute-start.15 = (f32[16,256]{1,0:T(8,128)S(1)}, f32[16,256]{1,0:T(8,128)S(1)}, u32[]{:S(2)}, u32[]{:S(2)}) collective-permute-start(f32[16,256]{1,0:T(8,128)S(1)} %get-tuple-element.52), channel_id=1, source_target_pairs={{248,0},{0,8},{8,16},{16,24},{24,32},{32,40},{40,48},{48,56},{56,6... | collective-permute-start | bytes 49160 | tf_op jit(solution)/shard_map/ppermute | solution.py:71
  110.8 3.4 %collective-permute-done.15 = f32[16,256]{1,0:T(8,128)S(1)} collective-permute-done((f32[16,256]{1,0:T(8,128)S(1)}, f32[16,256]{1,0:T(8,128)S(1)}, u32[]{:S(2)}, u32[]{:S(2)}) %collective-permute-start.15) | collective-permute-done | bytes 16416 | tf_op jit(solution)/shard_map/ppermute | solution.py:71
  114.4 4.1 %collective-permute-start.17 = (f32[16,256]{1,0:T(8,128)S(1)}, f32[16,256]{1,0:T(8,128)S(1)}, u32[]{:S(2)}, u32[]{:S(2)}) collective-permute-start(f32[16,256]{1,0:T(8,128)S(1)} %bitcast.363), channel_id=1, source_target_pairs={{7,0},{0,1},{1,2},{2,3},{3,4},{4,5},{5,6},{6,7},{15,8},{8,9},{9,10... | collective-permute-start | bytes 49160 | tf_op jit(solution)/shard_map/ppermute | solution.py:74
  118.5 0.6 reshape.452
  119.4 3.5 %collective-permute-done.16 = f32[16,256]{1,0:T(8,128)S(1)} collective-permute-done((f32[16,256]{1,0:T(8,128)S(1)}, f32[16,256]{1,0:T(8,128)S(1)}, u32[]{:S(2)}, u32[]{:S(2)}) %collective-permute-start.16) | collective-permute-done | bytes 16416 | tf_op jit(solution)/shard_map/ppermute | solution.py:74
  123.3 1.0 fusion.60
  (225 shorter events, 25.0 us)
Async XLA Ops:
  0.6 1.2 %copy-start.7 = (f32[256,256]{1,0:T(8,128)S(1)}, f32[256,256]{1,0:T(8,128)}, u32[]{:S(2)}) copy-start(f32[256,256]{1,0:T(8,128)} %constant.213.clone) | copy-start | bytes 786436
  0.6 1.3 %copy-start.3 = (f32[16,16,256]{2,1,0:T(8,128)S(1)}, f32[16,16,256]{2,1,0:T(8,128)}, u32[]{:S(2)}) copy-start(f32[16,16,256]{2,1,0:T(8,128)} %param.24) | copy-start | bytes 786436
  1.9 0.9 copy-start.4
  3.2 1.0 copy-start.2
  4.2 11.8 %collective-permute-start.1 = (f32[2,16,256]{2,1,0:T(8,128)S(1)}, f32[2,16,256]{2,1,0:T(8,128)S(1)}, u32[]{:S(2)}, u32[]{:S(2)}) collective-permute-start(f32[2,16,256]{2,1,0:T(8,128)S(1)} %get-tuple-element.18), channel_id=1, source_target_pairs={{248,0},{0,8},{8,16},{16,24},{24,32},{32,40},{40,48},{48,56},{56,6... | collective-permute-start | bytes 98312 | tf_op jit(solution)/shard_map/ppermute | solution.py:71
  5.8 10.2 %collective-permute-start = (f32[2,16,256]{2,1,0:T(8,128)S(1)}, f32[2,16,256]{2,1,0:T(8,128)S(1)}, u32[]{:S(2)}, u32[]{:S(2)}) collective-permute-start(f32[2,16,256]{2,1,0:T(8,128)S(1)} %get-tuple-element.17), channel_id=1, source_target_pairs={{8,0},{16,8},{24,16},{32,24},{40,32},{48,40},{56,48},{64,56},{72,6... | collective-permute-start | bytes 98312 | tf_op jit(solution)/shard_map/ppermute | solution.py:71
  13.1 0.8 copy-start.11
  13.9 0.7 copy-start.12
  14.6 0.7 copy-start.18
  15.2 0.7 copy-start.19
  16.3 4.8 %collective-permute-start.2 = (f32[12360]{0:T(1024)S(1)}, f32[12360]{0:T(1024)S(1)}, u32[]{:S(2)}, u32[]{:S(2)}) collective-permute-start(f32[12360]{0:T(1024)S(1)} %concatenate.166), channel_id=1, source_target_pairs={{1,0},{2,1},{3,2},{4,3},{5,4},{6,5},{7,6},{0,7},{9,8},{10,9},{11,1... | collective-permute-start | bytes 148328 | tf_op jit(solution)/shard_map/ppermute | solution.py:74
  17.3 3.3 %collective-permute-start.3 = (f32[2,16,256]{2,1,0:T(8,128)S(1)}, f32[2,16,256]{2,1,0:T(8,128)S(1)}, u32[]{:S(2)}, u32[]{:S(2)}) collective-permute-start(f32[2,16,256]{2,1,0:T(8,128)S(1)} %bitcast.353), channel_id=1, source_target_pairs={{7,0},{0,1},{1,2},{2,3},{3,4},{4,5},{5,6},{6,7},{15,8},{8,9},{9,10... | collective-permute-start | bytes 98312 | tf_op jit(solution)/shard_map/ppermute | solution.py:74
  19.3 1.1 copy-start.17
  22.2 1.0 copy-start
  23.4 1.2 copy-start.1
  23.8 0.7 copy-start.9
  24.9 0.7 copy-start.10
  25.7 0.8 copy-start.6
  26.4 0.7 copy-start.8
  27.6 3.9 %collective-permute-start.4 = (f32[16,256]{1,0:T(8,128)S(1)}, f32[16,256]{1,0:T(8,128)S(1)}, u32[]{:S(2)}, u32[]{:S(2)}) collective-permute-start(f32[16,256]{1,0:T(8,128)S(1)} %get-tuple-element.55), channel_id=1, source_target_pairs={{8,0},{16,8},{24,16},{32,24},{40,32},{48,40},{56,48},{64,56},{72,6... | collective-permute-start | bytes 49160 | tf_op jit(solution)/shard_map/ppermute | solution.py:71
  30.0 5.9 %collective-permute-start.5 = (f32[16,256]{1,0:T(8,128)S(1)}, f32[16,256]{1,0:T(8,128)S(1)}, u32[]{:S(2)}, u32[]{:S(2)}) collective-permute-start(f32[16,256]{1,0:T(8,128)S(1)} %get-tuple-element.56), channel_id=1, source_target_pairs={{248,0},{0,8},{8,16},{16,24},{24,32},{32,40},{40,48},{48,56},{56,6... | collective-permute-start | bytes 49160 | tf_op jit(solution)/shard_map/ppermute | solution.py:71
  36.1 5.7 %collective-permute-start.6 = (f32[16,256]{1,0:T(8,128)S(1)}, f32[16,256]{1,0:T(8,128)S(1)}, u32[]{:S(2)}, u32[]{:S(2)}) collective-permute-start(f32[16,256]{1,0:T(8,128)S(1)} %bitcast.362), channel_id=1, source_target_pairs={{1,0},{2,1},{3,2},{4,3},{5,4},{6,5},{7,6},{0,7},{9,8},{10,9},{11,1... | collective-permute-start | bytes 49160 | tf_op jit(solution)/shard_map/ppermute | solution.py:74
  38.0 3.2 %collective-permute-start.7 = (f32[16,256]{1,0:T(8,128)S(1)}, f32[16,256]{1,0:T(8,128)S(1)}, u32[]{:S(2)}, u32[]{:S(2)}) collective-permute-start(f32[16,256]{1,0:T(8,128)S(1)} %bitcast.368), channel_id=1, source_target_pairs={{7,0},{0,1},{1,2},{2,3},{3,4},{4,5},{5,6},{6,7},{15,8},{8,9},{9,10... | collective-permute-start | bytes 49160 | tf_op jit(solution)/shard_map/ppermute | solution.py:74
  44.5 0.7 copy-start.15
  45.6 0.7 copy-start.14
  46.6 3.8 %collective-permute-start.8 = (f32[4,4,64]{2,1,0:T(4,128)S(1)}, f32[4,4,64]{2,1,0:T(4,128)S(1)}, u32[]{:S(2)}, u32[]{:S(2)}) collective-permute-start(f32[4,4,64]{2,1,0:T(4,128)S(1)} %reshape.442), channel_id=1, source_target_pairs={{7,0},{0,1},{1,2},{2,3},{3,4},{4,5},{5,6},{6,7},{15,8},{8,9},{9,10... | collective-permute-start | bytes 12296 | tf_op jit(solution)/shard_map/ppermute | solution.py:74
  49.6 4.3 %collective-permute-start.9 = (f32[4,4,64]{2,1,0:T(4,128)S(1)}, f32[4,4,64]{2,1,0:T(4,128)S(1)}, u32[]{:S(2)}, u32[]{:S(2)}) collective-permute-start(f32[4,4,64]{2,1,0:T(4,128)S(1)} %reshape.442), channel_id=1, source_target_pairs={{1,0},{2,1},{3,2},{4,3},{5,4},{6,5},{7,6},{0,7},{9,8},{10,9},{11,1... | collective-permute-start | bytes 12296 | tf_op jit(solution)/shard_map/ppermute | solution.py:74
  55.9 13.9 %all-to-all-start = ((f32[32,3,4,3]{2,1,3,0:T(4,128)}), f32[32,3,4,3]{2,1,3,0:T(4,128)S(1)}, u32[]{:S(2)}, u32[]{:S(2)}) async-start(f32[32,3,4,3]{2,1,3,0:T(4,128)} %copy.122), calls=%async_computation | async-start | bytes 393216 | tf_op jit(solution)/shard_map/all_to_all | solution.py:260
  70.6 1.0 copy-start.5
  88.3 0.7 copy-start.16
  89.6 0.7 copy-start.13
  92.9 3.0 %collective-permute-start.10 = (f32[16,256]{1,0:T(8,128)S(1)}, f32[16,256]{1,0:T(8,128)S(1)}, u32[]{:S(2)}, u32[]{:S(2)}) collective-permute-start(f32[16,256]{1,0:T(8,128)S(1)} %get-tuple-element.53), channel_id=1, source_target_pairs={{8,0},{16,8},{24,16},{32,24},{40,32},{48,40},{56,48},{64,56},{72,6... | collective-permute-start | bytes 49160 | tf_op jit(solution)/shard_map/ppermute | solution.py:71
  93.8 5.9 %collective-permute-start.11 = (f32[16,256]{1,0:T(8,128)S(1)}, f32[16,256]{1,0:T(8,128)S(1)}, u32[]{:S(2)}, u32[]{:S(2)}) collective-permute-start(f32[16,256]{1,0:T(8,128)S(1)} %get-tuple-element.54), channel_id=1, source_target_pairs={{248,0},{0,8},{8,16},{16,24},{24,32},{32,40},{40,48},{48,56},{56,6... | collective-permute-start | bytes 49160 | tf_op jit(solution)/shard_map/ppermute | solution.py:71
  99.8 5.5 %collective-permute-start.12 = (f32[16,256]{1,0:T(8,128)S(1)}, f32[16,256]{1,0:T(8,128)S(1)}, u32[]{:S(2)}, u32[]{:S(2)}) collective-permute-start(f32[16,256]{1,0:T(8,128)S(1)} %bitcast.366), channel_id=1, source_target_pairs={{1,0},{2,1},{3,2},{4,3},{5,4},{6,5},{7,6},{0,7},{9,8},{10,9},{11,1... | collective-permute-start | bytes 49160 | tf_op jit(solution)/shard_map/ppermute | solution.py:74
  100.8 4.6 %collective-permute-start.13 = (f32[16,256]{1,0:T(8,128)S(1)}, f32[16,256]{1,0:T(8,128)S(1)}, u32[]{:S(2)}, u32[]{:S(2)}) collective-permute-start(f32[16,256]{1,0:T(8,128)S(1)} %bitcast.367), channel_id=1, source_target_pairs={{7,0},{0,1},{1,2},{2,3},{3,4},{4,5},{5,6},{6,7},{15,8},{8,9},{9,10... | collective-permute-start | bytes 49160 | tf_op jit(solution)/shard_map/ppermute | solution.py:74
  108.2 2.7 %collective-permute-start.14 = (f32[16,256]{1,0:T(8,128)S(1)}, f32[16,256]{1,0:T(8,128)S(1)}, u32[]{:S(2)}, u32[]{:S(2)}) collective-permute-start(f32[16,256]{1,0:T(8,128)S(1)} %get-tuple-element.51), channel_id=1, source_target_pairs={{8,0},{16,8},{24,16},{32,24},{40,32},{48,40},{56,48},{64,56},{72,6... | collective-permute-start | bytes 49160 | tf_op jit(solution)/shard_map/ppermute | solution.py:71
  108.3 6.0 %collective-permute-start.15 = (f32[16,256]{1,0:T(8,128)S(1)}, f32[16,256]{1,0:T(8,128)S(1)}, u32[]{:S(2)}, u32[]{:S(2)}) collective-permute-start(f32[16,256]{1,0:T(8,128)S(1)} %get-tuple-element.52), channel_id=1, source_target_pairs={{248,0},{0,8},{8,16},{16,24},{24,32},{32,40},{40,48},{48,56},{56,6... | collective-permute-start | bytes 49160 | tf_op jit(solution)/shard_map/ppermute | solution.py:71
  114.4 5.0 %collective-permute-start.17 = (f32[16,256]{1,0:T(8,128)S(1)}, f32[16,256]{1,0:T(8,128)S(1)}, u32[]{:S(2)}, u32[]{:S(2)}) collective-permute-start(f32[16,256]{1,0:T(8,128)S(1)} %bitcast.363), channel_id=1, source_target_pairs={{7,0},{0,1},{1,2},{2,3},{3,4},{4,5},{5,6},{6,7},{15,8},{8,9},{9,10... | collective-permute-start | bytes 49160 | tf_op jit(solution)/shard_map/ppermute | solution.py:74
  118.5 4.4 %collective-permute-start.16 = (f32[16,256]{1,0:T(8,128)S(1)}, f32[16,256]{1,0:T(8,128)S(1)}, u32[]{:S(2)}, u32[]{:S(2)}) collective-permute-start(f32[16,256]{1,0:T(8,128)S(1)} %bitcast.365), channel_id=1, source_target_pairs={{1,0},{2,1},{3,2},{4,3},{5,4},{6,5},{7,6},{0,7},{9,8},{10,9},{11,1... | collective-permute-start | bytes 49160 | tf_op jit(solution)/shard_map/ppermute | solution.py:74

commit v5 on v3

--- a/solution.py
+++ b/solution.py
@@ -239,17 +239,20 @@
     layer = cols // (2 * nxb)
     block = cols % (2 * nxb)
     index = (layer * 4 + y_off + block // nxb) * nxb + block % nxb
-    picked = jnp.take(frame_rows, index.reshape(-1), axis=0).reshape(index.shape + (BS,))
+    picked = jnp.take(frame_rows, index.reshape(-1), axis=0, mode="clip").reshape(index.shape + (BS,))
     live = (jnp.arange(K, dtype=jnp.int32)[None, None, :] < lives[:, :, None]).astype(
         jnp.float32
     )
-    values = vals.reshape(vals.shape[:2] + (K, BS, BS))
-    product = jnp.einsum("yxkij,yxkj,yxk->yxi", values, picked, live, precision=highest)
+    values = vals.reshape(vals.shape[:2] + (K, BS, BS)) * live[..., None, None]
+    values = lax.optimization_barrier(values)
+    product = jnp.einsum("yxkij,yxkj->yxi", values, picked, precision=highest)
     product = product.reshape(3, span)
     coarse_product = product[:2].reshape(1, 2, span)
 
-    pick = (2 * np.arange(nw)[:, None] + np.arange(3)[None, :]) % span
-    back = jnp.transpose(product[:, pick], (1, 0, 2))
+    back = jnp.stack(
+        [product[:, 0::2], product[:, 1::2], jnp.roll(product, -2, axis=1)[:, 0::2]], axis=-1
+    )
+    back = jnp.transpose(back, (1, 0, 2))
     got = lax.all_to_all(back, "wide", 0, 0, tiled=True)
     hx = jnp.stack([got[:, :, 0:2], got[:, :, 1:3]], axis=-1).reshape(nw, 3, 4)
     hy = jnp.stack([hx[:, 0:2], hx[:, 1:3]], axis=2).reshape(nw, 4, 4)

time: 122 us -> 128 us (1.049)
  local copies, waits for them, and re-layouts: 18.5 us -> 22.6 us
  starting transfers between devices: 37.9 us -> 39.4 us
    slice x6, local copies, waits for them, and re-layouts: 0.44 us -> 3.09 us  [local(): even = got[:, 0] + jnp.roll(got[:, 2], 1, axis=0)]
    mul x0 -> x1, other arithmetic: none -> 1.31 us  [local(): values = vals.reshape(vals.shape[:2] + (K, BS, BS)) * live[..., None, None]]
  transfers between devices with their start and end apart: 19 -> 19, of which waited for: 13 -> 14; matrix products, arithmetic and copies ran while one was open for 4% -> 4% of each run, Pallas kernels for 0% -> 0%
where the time goes in v5:
time: 128 us; the launch traced here: 127 us
  starting transfers between devices  39.4 us (31%)
  waiting for transfers between devices  31.7 us (25%)
  local copies, waits for them, and re-layouts  22.6 us (18%)
  blocking collectives  12.2 us (10%)
  matrix products  12.1 us (9%)
  other arithmetic  7.44 us (6%)
  between operations  1.64 us (1%)
    ppermute x10, starting transfers between devices, shift(): return lax.ppermute(value, 'deep', pairs)  18.5 us
    ppermute x8, starting transfers between devices, shift(): return lax.ppermute(value, 'wide', pairs)  16.2 us
    ppermute x8, waiting for transfers between devices, shift(): return lax.ppermute(value, 'wide', pairs)  14.4 us
    all_to_all x1, blocking collectives, local(): got = lax.all_to_all(back, 'wide', 0, 0, tiled=True)  12.2 us
    all_to_all x1, waiting for transfers between devices, local(): got = lax.all_to_all(sent, 'wide', 0, 0, tiled=True)  9.22 us
    unnamed x59, local copies, waits for them, and re-layouts  8.55 us
    ppermute x10, waiting for transfers between devices, shift(): return lax.ppermute(value, 'deep', pairs)  8.11 us
    all_to_all x1, starting transfers between devices, local(): got = lax.all_to_all(sent, 'wide', 0, 0, tiled=True)  4.75 us
  transfers between devices with their start and end apart: 19, of which 14 were waited for; matrix products, arithmetic and copies ran while one was open for 4% of the time, Pallas kernels for 0%

profile of v5, /device:TPU:7, one launch (start us, length us, event | category | flops | bytes accessed | tf_op | source)
XLA Modules:
  0.0 127.0 jit_solution(580597282785116785)
XLA Ops:
  0.7 1.2 fusion.67
  3.5 0.6 copy-done.2
  4.2 1.7 %collective-permute-start.1 = (f32[2,16,256]{2,1,0:T(8,128)S(1)}, f32[2,16,256]{2,1,0:T(8,128)S(1)}, u32[]{:S(2)}, u32[]{:S(2)}) collective-permute-start(f32[2,16,256]{2,1,0:T(8,128)S(1)} %get-tuple-element.14), channel_id=1, source_target_pairs={{248,0},{0,8},{8,16},{16,24},{24,32},{32,40},{40,48},{48,56},{56,6... | collective-permute-start | bytes 98312 | tf_op jit(solution)/shard_map/ppermute | solution.py:71
  5.9 6.5 %collective-permute-start = (f32[2,16,256]{2,1,0:T(8,128)S(1)}, f32[2,16,256]{2,1,0:T(8,128)S(1)}, u32[]{:S(2)}, u32[]{:S(2)}) collective-permute-start(f32[2,16,256]{2,1,0:T(8,128)S(1)} %get-tuple-element.13), channel_id=1, source_target_pairs={{8,0},{16,8},{24,16},{32,24},{40,32},{48,40},{56,48},{64,56},{72,6... | collective-permute-start | bytes 98312 | tf_op jit(solution)/shard_map/ppermute | solution.py:71
  12.4 0.7 copy-done.23
  13.9 1.5 %collective-permute-start.2 = (f32[12360]{0:T(1024)S(1)}, f32[12360]{0:T(1024)S(1)}, u32[]{:S(2)}, u32[]{:S(2)}) collective-permute-start(f32[12360]{0:T(1024)S(1)} %concatenate.136), channel_id=1, source_target_pairs={{1,0},{2,1},{3,2},{4,3},{5,4},{6,5},{7,6},{0,7},{9,8},{10,9},{11,1... | collective-permute-start | bytes 148328 | tf_op jit(solution)/shard_map/ppermute | solution.py:74
  15.5 1.4 %collective-permute-start.3 = (f32[2,16,256]{2,1,0:T(8,128)S(1)}, f32[2,16,256]{2,1,0:T(8,128)S(1)}, u32[]{:S(2)}, u32[]{:S(2)}) collective-permute-start(f32[2,16,256]{2,1,0:T(8,128)S(1)} %bitcast.284), channel_id=1, source_target_pairs={{7,0},{0,1},{1,2},{2,3},{3,4},{4,5},{5,6},{6,7},{15,8},{8,9},{9,10... | collective-permute-start | bytes 98312 | tf_op jit(solution)/shard_map/ppermute | solution.py:74
  16.9 1.1 concatenate.147
  19.8 0.9 copy-done
  23.3 0.7 copy-done.6
  24.0 4.9 %collective-permute-start.4 = (f32[16,256]{1,0:T(8,128)S(1)}, f32[16,256]{1,0:T(8,128)S(1)}, u32[]{:S(2)}, u32[]{:S(2)}) collective-permute-start(f32[16,256]{1,0:T(8,128)S(1)} %get-tuple-element.37), channel_id=1, source_target_pairs={{8,0},{16,8},{24,16},{32,24},{40,32},{48,40},{56,48},{64,56},{72,6... | collective-permute-start | bytes 49160 | tf_op jit(solution)/shard_map/ppermute | solution.py:71
  29.3 1.3 %maximum_multiply_fusion = f32[3,8,8,8,8]{4,3,2,1,0:T(8,128)S(1)} fusion(f32[1,8,8,8,8]{4,3,2,1,0:T(8,128)S(1)} %concatenate.148, f32[2,8,8,8,8]{4,3,2,1,0:T(8,128)} %concatenate.147, f32[3,8,8]{2,1,0:T(8,128)S(1)} %fusion.59), kind=kLoop, calls=%fused_computation.32 | loop fusion | flops 24576 | bytes 99072 | tf_op jit(solution)/shard_map/mul | solution.py:246
  30.7 4.2 %collective-permute-done.5 = f32[16,256]{1,0:T(8,128)S(1)} collective-permute-done((f32[16,256]{1,0:T(8,128)S(1)}, f32[16,256]{1,0:T(8,128)S(1)}, u32[]{:S(2)}, u32[]{:S(2)}) %collective-permute-start.5) | collective-permute-done | bytes 16416 | tf_op jit(solution)/shard_map/ppermute | solution.py:71
  34.8 1.4 %fusion.32 = f32[16,16,256]{2,1,0:T(8,128)S(1)} fusion(f32[16,16,256]{2,1,0:T(8,128)} %copy-done.6, f32[1,16,256]{2,1,0:T(8,128)S(1)} %bitcast.289, f32[1,16,256]{2,1,0:T(8,128)S(1)} %bitcast.288, pred[16]{0:T(512)(128)(4,1)S(1)} %get-tuple-element.49, pred[16]{0:T(512)(128)(4,1)S(1)} %get-tuple-element.50), kind=kLoop, calls=%fused_computation.89 | loop fusion | flops 393216 | bytes 557088 | tf_op jit(solution)/shard_map/add | solution.py:99
  36.3 1.9 %collective-permute-start.6 = (f32[16,256]{1,0:T(8,128)S(1)}, f32[16,256]{1,0:T(8,128)S(1)}, u32[]{:S(2)}, u32[]{:S(2)}) collective-permute-start(f32[16,256]{1,0:T(8,128)S(1)} %bitcast.294), channel_id=1, source_target_pairs={{1,0},{2,1},{3,2},{4,3},{5,4},{6,5},{7,6},{0,7},{9,8},{10,9},{11,1... | collective-permute-start | bytes 49160 | tf_op jit(solution)/shard_map/ppermute | solution.py:74
  38.2 2.4 %collective-permute-start.7 = (f32[16,256]{1,0:T(8,128)S(1)}, f32[16,256]{1,0:T(8,128)S(1)}, u32[]{:S(2)}, u32[]{:S(2)}) collective-permute-start(f32[16,256]{1,0:T(8,128)S(1)} %bitcast.300), channel_id=1, source_target_pairs={{7,0},{0,1},{1,2},{2,3},{3,4},{4,5},{5,6},{6,7},{15,8},{8,9},{9,10... | collective-permute-start | bytes 49160 | tf_op jit(solution)/shard_map/ppermute | solution.py:74
  40.6 0.8 collective-permute-done.7
  42.4 0.8 copy-done.5
  47.6 3.0 %collective-permute-start.8 = (f32[4,4,64]{2,1,0:T(4,128)S(1)}, f32[4,4,64]{2,1,0:T(4,128)S(1)}, u32[]{:S(2)}, u32[]{:S(2)}) collective-permute-start(f32[4,4,64]{2,1,0:T(4,128)S(1)} %reshape.401), channel_id=1, source_target_pairs={{7,0},{0,1},{1,2},{2,3},{3,4},{4,5},{5,6},{6,7},{15,8},{8,9},{9,10... | collective-permute-start | bytes 12296 | tf_op jit(solution)/shard_map/ppermute | solution.py:74
  50.7 0.8 collective-permute-done.8
  51.4 3.5 %collective-permute-done.9 = f32[4,4,64]{2,1,0:T(4,128)S(1)} collective-permute-done((f32[4,4,64]{2,1,0:T(4,128)S(1)}, f32[4,4,64]{2,1,0:T(4,128)S(1)}, u32[]{:S(2)}, u32[]{:S(2)}) %collective-permute-start.9) | collective-permute-done | bytes 4128 | tf_op jit(solution)/shard_map/ppermute | solution.py:74
  56.1 0.8 copy.106
  56.9 4.8 %all-to-all-start = ((f32[32,3,4,3]{2,1,3,0:T(4,128)}), f32[32,3,4,3]{2,1,3,0:T(4,128)}, u32[]{:S(2)}, u32[]{:S(2)}) async-start(f32[32,3,4,3]{2,1,3,0:T(4,128)} %copy.106), calls=%async_computation | async-start | bytes 393216 | tf_op jit(solution)/shard_map/all_to_all | solution.py:227
  62.2 9.2 %all-to-all-done = f32[32,3,4,3]{2,1,3,0:T(4,128)} async-done(((f32[32,3,4,3]{2,1,3,0:T(4,128)}), f32[32,3,4,3]{2,1,3,0:T(4,128)}, u32[]{:S(2)}, u32[]{:S(2)}) %all-to-all-start) | async-done | bytes 4640 | tf_op jit(solution)/shard_map/all_to_all | solution.py:227
  71.4 1.1 fusion.80
  72.7 1.0 slice.454
  73.7 0.7 slice.453
  74.7 0.8 copy.111
  75.6 1.0 reshape_reshape.3
  76.6 0.8 gather_fusion
  77.4 1.6 %fusion.83 = f32[3,8,1,8,1]{3,2,4,1,0:T(1,128)S(1)} fusion(f32[3,8,8,8,8]{4,3,2,1,0:T(8,128)S(1)} %maximum_multiply_fusion, f32[3,8,8,8,1]{3,4,2,1,0:T(1,128)S(1)} %bitcast.272), kind=kOutput, calls=%fused_computation.216 | convolution fusion | flops 147456 | bytes 56064 | tf_op jit(solution)/shard_map/yxkij,yxkj->yxi/dot_general | solution.py:248
  79.8 12.2 %all_to_all.10 = f32[32,3,3]{1,2,0:T(4,128)S(1)} all-to-all(f32[32,3,3]{1,2,0:T(4,128)S(1)} %copy.112), channel_id=1, replica_groups=mesh['wide'=32,'deep'=8] {'wide'}, dimensions={0} | all-to-all | bytes 2304 | tf_op jit(solution)/shard_map/all_to_all | solution.py:256
  97.3 0.9 collective-permute-start.10
  98.2 0.7 collective-permute-start.11
  98.8 1.5 %collective-permute-done.10 = f32[16,256]{1,0:T(8,128)S(1)} collective-permute-done((f32[16,256]{1,0:T(8,128)S(1)}, f32[16,256]{1,0:T(8,128)S(1)}, u32[]{:S(2)}, u32[]{:S(2)}) %collective-permute-start.10) | collective-permute-done | bytes 16416 | tf_op jit(solution)/shard_map/ppermute | solution.py:71
  100.3 3.7 %collective-permute-done.11 = f32[16,256]{1,0:T(8,128)S(1)} collective-permute-done((f32[16,256]{1,0:T(8,128)S(1)}, f32[16,256]{1,0:T(8,128)S(1)}, u32[]{:S(2)}, u32[]{:S(2)}) %collective-permute-start.11) | collective-permute-done | bytes 16416 | tf_op jit(solution)/shard_map/ppermute | solution.py:71
  104.1 0.7 copy-done.11
  104.9 0.9 collective-permute-start.12
  105.8 3.2 %collective-permute-start.13 = (f32[16,256]{1,0:T(8,128)S(1)}, f32[16,256]{1,0:T(8,128)S(1)}, u32[]{:S(2)}, u32[]{:S(2)}) collective-permute-start(f32[16,256]{1,0:T(8,128)S(1)} %bitcast.299), channel_id=1, source_target_pairs={{7,0},{0,1},{1,2},{2,3},{3,4},{4,5},{5,6},{6,7},{15,8},{8,9},{9,10... | collective-permute-start | bytes 49160 | tf_op jit(solution)/shard_map/ppermute | solution.py:74
  109.0 1.4 %collective-permute-done.12 = f32[16,256]{1,0:T(8,128)S(1)} collective-permute-done((f32[16,256]{1,0:T(8,128)S(1)}, f32[16,256]{1,0:T(8,128)S(1)}, u32[]{:S(2)}, u32[]{:S(2)}) %collective-permute-start.12) | collective-permute-done | bytes 16416 | tf_op jit(solution)/shard_map/ppermute | solution.py:74
  110.8 0.7 copy-done.18
  113.9 1.5 %collective-permute-start.15 = (f32[16,256]{1,0:T(8,128)S(1)}, f32[16,256]{1,0:T(8,128)S(1)}, u32[]{:S(2)}, u32[]{:S(2)}) collective-permute-start(f32[16,256]{1,0:T(8,128)S(1)} %get-tuple-element.22), channel_id=1, source_target_pairs={{248,0},{0,8},{8,16},{16,24},{24,32},{32,40},{40,48},{48,56},{56,6... | collective-permute-start | bytes 49160 | tf_op jit(solution)/shard_map/ppermute | solution.py:71
  115.4 1.1 collective-permute-done.14
  116.5 3.4 %collective-permute-done.15 = f32[16,256]{1,0:T(8,128)S(1)} collective-permute-done((f32[16,256]{1,0:T(8,128)S(1)}, f32[16,256]{1,0:T(8,128)S(1)}, u32[]{:S(2)}, u32[]{:S(2)}) %collective-permute-start.15) | collective-permute-done | bytes 16416 | tf_op jit(solution)/shard_map/ppermute | solution.py:71
  120.1 4.1 %collective-permute-start.17 = (f32[16,256]{1,0:T(8,128)S(1)}, f32[16,256]{1,0:T(8,128)S(1)}, u32[]{:S(2)}, u32[]{:S(2)}) collective-permute-start(f32[16,256]{1,0:T(8,128)S(1)} %bitcast.297), channel_id=1, source_target_pairs={{7,0},{0,1},{1,2},{2,3},{3,4},{4,5},{5,6},{6,7},{15,8},{8,9},{9,10... | collective-permute-start | bytes 49160 | tf_op jit(solution)/shard_map/ppermute | solution.py:74
  124.2 0.6 reshape.412
  124.9 0.7 collective-permute-done.16
  126.0 1.0 fusion.47
  (211 shorter events, 23.9 us)
Async XLA Ops:
  0.6 1.2 copy-start.8
  0.6 1.3 copy-start.3
  1.9 0.9 copy-start.7
  3.2 1.0 copy-start.2
  4.2 8.2 %copy-start.9 = (f32[1,2,8,512]{3,2,1,0:T(8,128)S(1)}, f32[1,2,8,512]{3,2,1,0:T(8,128)}, u32[]{:S(2)}) copy-start(f32[1,2,8,512]{3,2,1,0:T(8,128)} %param.24) | copy-start | bytes 98308
  4.2 9.4 %collective-permute-start.1 = (f32[2,16,256]{2,1,0:T(8,128)S(1)}, f32[2,16,256]{2,1,0:T(8,128)S(1)}, u32[]{:S(2)}, u32[]{:S(2)}) collective-permute-start(f32[2,16,256]{2,1,0:T(8,128)S(1)} %get-tuple-element.14), channel_id=1, source_target_pairs={{248,0},{0,8},{8,16},{16,24},{24,32},{32,40},{40,48},{48,56},{56,6... | collective-permute-start | bytes 98312 | tf_op jit(solution)/shard_map/ppermute | solution.py:71
  5.9 6.5 %copy-start.14 = (s32[1,2,8,8]{3,2,1,0:T(8,128)S(1)}, s32[1,2,8,8]{3,2,1,0:T(8,128)}, u32[]{:S(2)}) copy-start(s32[1,2,8,8]{3,2,1,0:T(8,128)} %param.22) | copy-start | bytes 1540
  5.9 7.7 %collective-permute-start = (f32[2,16,256]{2,1,0:T(8,128)S(1)}, f32[2,16,256]{2,1,0:T(8,128)S(1)}, u32[]{:S(2)}, u32[]{:S(2)}) collective-permute-start(f32[2,16,256]{2,1,0:T(8,128)S(1)} %get-tuple-element.13), channel_id=1, source_target_pairs={{8,0},{16,8},{24,16},{32,24},{40,32},{48,40},{56,48},{64,56},{72,6... | collective-permute-start | bytes 98312 | tf_op jit(solution)/shard_map/ppermute | solution.py:71
  12.4 0.7 copy-start.23
  13.1 29.2 %copy-start.10 = (pred[16]{0:T(512)(128)(4,1)}, pred[16]{0:T(512)(128)(4,1)S(1)}, u32[]{:S(2)}) copy-start(pred[16]{0:T(512)(128)(4,1)S(1)} %get-tuple-element.49) | copy-start | bytes 52
  13.1 29.2 %copy-start.12 = (pred[16]{0:T(512)(128)(4,1)}, pred[16]{0:T(512)(128)(4,1)S(1)}, u32[]{:S(2)}) copy-start(pred[16]{0:T(512)(128)(4,1)S(1)} %get-tuple-element.50) | copy-start | bytes 52
  13.9 4.8 %collective-permute-start.2 = (f32[12360]{0:T(1024)S(1)}, f32[12360]{0:T(1024)S(1)}, u32[]{:S(2)}, u32[]{:S(2)}) collective-permute-start(f32[12360]{0:T(1024)S(1)} %concatenate.136), channel_id=1, source_target_pairs={{1,0},{2,1},{3,2},{4,3},{5,4},{6,5},{7,6},{0,7},{9,8},{10,9},{11,1... | collective-permute-start | bytes 148328 | tf_op jit(solution)/shard_map/ppermute | solution.py:74
  15.5 2.7 %collective-permute-start.3 = (f32[2,16,256]{2,1,0:T(8,128)S(1)}, f32[2,16,256]{2,1,0:T(8,128)S(1)}, u32[]{:S(2)}, u32[]{:S(2)}) collective-permute-start(f32[2,16,256]{2,1,0:T(8,128)S(1)} %bitcast.284), channel_id=1, source_target_pairs={{7,0},{0,1},{1,2},{2,3},{3,4},{4,5},{5,6},{6,7},{15,8},{8,9},{9,10... | collective-permute-start | bytes 98312 | tf_op jit(solution)/shard_map/ppermute | solution.py:74
  16.9 25.5 %copy-start.17 = (pred[256]{0:T(512)(128)(4,1)}, pred[256]{0:T(512)(128)(4,1)S(1)}, u32[]{:S(2)}) copy-start(pred[256]{0:T(512)(128)(4,1)S(1)} %get-tuple-element.51) | copy-start | bytes 772
  16.9 25.5 %copy-start.19 = (pred[256]{0:T(512)(128)(4,1)}, pred[256]{0:T(512)(128)(4,1)S(1)}, u32[]{:S(2)}) copy-start(pred[256]{0:T(512)(128)(4,1)S(1)} %get-tuple-element.52) | copy-start | bytes 772
  16.9 1.1 copy-start.24
  19.7 1.0 copy-start
  21.0 1.0 copy-start.1
  23.3 0.7 copy-start.6
  24.0 6.6 %collective-permute-start.4 = (f32[16,256]{1,0:T(8,128)S(1)}, f32[16,256]{1,0:T(8,128)S(1)}, u32[]{:S(2)}, u32[]{:S(2)}) collective-permute-start(f32[16,256]{1,0:T(8,128)S(1)} %get-tuple-element.37), channel_id=1, source_target_pairs={{8,0},{16,8},{24,16},{32,24},{40,32},{48,40},{56,48},{64,56},{72,6... | collective-permute-start | bytes 49160 | tf_op jit(solution)/shard_map/ppermute | solution.py:71
  28.9 5.9 %collective-permute-start.5 = (f32[16,256]{1,0:T(8,128)S(1)}, f32[16,256]{1,0:T(8,128)S(1)}, u32[]{:S(2)}, u32[]{:S(2)}) collective-permute-start(f32[16,256]{1,0:T(8,128)S(1)} %get-tuple-element.38), channel_id=1, source_target_pairs={{248,0},{0,8},{8,16},{16,24},{24,32},{32,40},{40,48},{48,56},{56,6... | collective-permute-start | bytes 49160 | tf_op jit(solution)/shard_map/ppermute | solution.py:71
  36.2 5.9 %copy-start.4 = (f32[16,16,256]{2,1,0:T(8,128)}, f32[16,16,256]{2,1,0:T(8,128)S(1)}, u32[]{:S(2)}) copy-start(f32[16,16,256]{2,1,0:T(8,128)S(1)} %fusion.32) | copy-start | bytes 786436
  36.3 5.7 %collective-permute-start.6 = (f32[16,256]{1,0:T(8,128)S(1)}, f32[16,256]{1,0:T(8,128)S(1)}, u32[]{:S(2)}, u32[]{:S(2)}) collective-permute-start(f32[16,256]{1,0:T(8,128)S(1)} %bitcast.294), channel_id=1, source_target_pairs={{1,0},{2,1},{3,2},{4,3},{5,4},{6,5},{7,6},{0,7},{9,8},{10,9},{11,1... | collective-permute-start | bytes 49160 | tf_op jit(solution)/shard_map/ppermute | solution.py:74
  38.2 3.2 %collective-permute-start.7 = (f32[16,256]{1,0:T(8,128)S(1)}, f32[16,256]{1,0:T(8,128)S(1)}, u32[]{:S(2)}, u32[]{:S(2)}) collective-permute-start(f32[16,256]{1,0:T(8,128)S(1)} %bitcast.300), channel_id=1, source_target_pairs={{7,0},{0,1},{1,2},{2,3},{3,4},{4,5},{5,6},{6,7},{15,8},{8,9},{9,10... | collective-permute-start | bytes 49160 | tf_op jit(solution)/shard_map/ppermute | solution.py:74
  42.2 1.0 copy-start.5
  45.5 0.7 copy-start.21
  46.6 0.7 copy-start.16
  47.6 3.8 %collective-permute-start.8 = (f32[4,4,64]{2,1,0:T(4,128)S(1)}, f32[4,4,64]{2,1,0:T(4,128)S(1)}, u32[]{:S(2)}, u32[]{:S(2)}) collective-permute-start(f32[4,4,64]{2,1,0:T(4,128)S(1)} %reshape.401), channel_id=1, source_target_pairs={{7,0},{0,1},{1,2},{2,3},{3,4},{4,5},{5,6},{6,7},{15,8},{8,9},{9,10... | collective-permute-start | bytes 12296 | tf_op jit(solution)/shard_map/ppermute | solution.py:74
  50.6 4.3 %collective-permute-start.9 = (f32[4,4,64]{2,1,0:T(4,128)S(1)}, f32[4,4,64]{2,1,0:T(4,128)S(1)}, u32[]{:S(2)}, u32[]{:S(2)}) collective-permute-start(f32[4,4,64]{2,1,0:T(4,128)S(1)} %reshape.401), channel_id=1, source_target_pairs={{1,0},{2,1},{3,2},{4,3},{5,4},{6,5},{7,6},{0,7},{9,8},{10,9},{11,1... | collective-permute-start | bytes 12296 | tf_op jit(solution)/shard_map/ppermute | solution.py:74
  56.9 14.6 %all-to-all-start = ((f32[32,3,4,3]{2,1,3,0:T(4,128)}), f32[32,3,4,3]{2,1,3,0:T(4,128)}, u32[]{:S(2)}, u32[]{:S(2)}) async-start(f32[32,3,4,3]{2,1,3,0:T(4,128)} %copy.106), calls=%async_computation | async-start | bytes 393216 | tf_op jit(solution)/shard_map/all_to_all | solution.py:227
  92.8 0.7 copy-start.22
  94.0 0.7 copy-start.15
  97.3 3.1 %collective-permute-start.10 = (f32[16,256]{1,0:T(8,128)S(1)}, f32[16,256]{1,0:T(8,128)S(1)}, u32[]{:S(2)}, u32[]{:S(2)}) collective-permute-start(f32[16,256]{1,0:T(8,128)S(1)} %get-tuple-element.29), channel_id=1, source_target_pairs={{8,0},{16,8},{24,16},{32,24},{40,32},{48,40},{56,48},{64,56},{72,6... | collective-permute-start | bytes 49160 | tf_op jit(solution)/shard_map/ppermute | solution.py:71
  98.2 5.9 %collective-permute-start.11 = (f32[16,256]{1,0:T(8,128)S(1)}, f32[16,256]{1,0:T(8,128)S(1)}, u32[]{:S(2)}, u32[]{:S(2)}) collective-permute-start(f32[16,256]{1,0:T(8,128)S(1)} %get-tuple-element.30), channel_id=1, source_target_pairs={{248,0},{0,8},{8,16},{16,24},{24,32},{32,40},{40,48},{48,56},{56,6... | collective-permute-start | bytes 49160 | tf_op jit(solution)/shard_map/ppermute | solution.py:71
  104.1 0.7 copy-start.11
  104.1 0.7 copy-start.13
  104.9 5.5 %collective-permute-start.12 = (f32[16,256]{1,0:T(8,128)S(1)}, f32[16,256]{1,0:T(8,128)S(1)}, u32[]{:S(2)}, u32[]{:S(2)}) collective-permute-start(f32[16,256]{1,0:T(8,128)S(1)} %bitcast.298), channel_id=1, source_target_pairs={{1,0},{2,1},{3,2},{4,3},{5,4},{6,5},{7,6},{0,7},{9,8},{10,9},{11,1... | collective-permute-start | bytes 49160 | tf_op jit(solution)/shard_map/ppermute | solution.py:74
  105.8 4.6 %collective-permute-start.13 = (f32[16,256]{1,0:T(8,128)S(1)}, f32[16,256]{1,0:T(8,128)S(1)}, u32[]{:S(2)}, u32[]{:S(2)}) collective-permute-start(f32[16,256]{1,0:T(8,128)S(1)} %bitcast.299), channel_id=1, source_target_pairs={{7,0},{0,1},{1,2},{2,3},{3,4},{4,5},{5,6},{6,7},{15,8},{8,9},{9,10... | collective-permute-start | bytes 49160 | tf_op jit(solution)/shard_map/ppermute | solution.py:74
  110.8 0.7 copy-start.18
  110.8 0.7 copy-start.20
  113.8 2.7 %collective-permute-start.14 = (f32[16,256]{1,0:T(8,128)S(1)}, f32[16,256]{1,0:T(8,128)S(1)}, u32[]{:S(2)}, u32[]{:S(2)}) collective-permute-start(f32[16,256]{1,0:T(8,128)S(1)} %get-tuple-element.21), channel_id=1, source_target_pairs={{8,0},{16,8},{24,16},{32,24},{40,32},{48,40},{56,48},{64,56},{72,6... | collective-permute-start | bytes 49160 | tf_op jit(solution)/shard_map/ppermute | solution.py:71
  113.9 6.0 %collective-permute-start.15 = (f32[16,256]{1,0:T(8,128)S(1)}, f32[16,256]{1,0:T(8,128)S(1)}, u32[]{:S(2)}, u32[]{:S(2)}) collective-permute-start(f32[16,256]{1,0:T(8,128)S(1)} %get-tuple-element.22), channel_id=1, source_target_pairs={{248,0},{0,8},{8,16},{16,24},{24,32},{32,40},{40,48},{48,56},{56,6... | collective-permute-start | bytes 49160 | tf_op jit(solution)/shard_map/ppermute | solution.py:71
  120.1 5.5 %collective-permute-start.16 = (f32[16,256]{1,0:T(8,128)S(1)}, f32[16,256]{1,0:T(8,128)S(1)}, u32[]{:S(2)}, u32[]{:S(2)}) collective-permute-start(f32[16,256]{1,0:T(8,128)S(1)} %bitcast.295), channel_id=1, source_target_pairs={{1,0},{2,1},{3,2},{4,3},{5,4},{6,5},{7,6},{0,7},{9,8},{10,9},{11,1... | collective-permute-start | bytes 49160 | tf_op jit(solution)/shard_map/ppermute | solution.py:74
  120.1 5.5 %collective-permute-start.17 = (f32[16,256]{1,0:T(8,128)S(1)}, f32[16,256]{1,0:T(8,128)S(1)}, u32[]{:S(2)}, u32[]{:S(2)}) collective-permute-start(f32[16,256]{1,0:T(8,128)S(1)} %bitcast.297), channel_id=1, source_target_pairs={{7,0},{0,1},{1,2},{2,3},{3,4},{4,5},{5,6},{6,7},{15,8},{8,9},{9,10... | collective-permute-start | bytes 49160 | tf_op jit(solution)/shard_map/ppermute | solution.py:74

commit v6 on v3

--- a/solution.py
+++ b/solution.py
@@ -239,7 +239,7 @@
     layer = cols // (2 * nxb)
     block = cols % (2 * nxb)
     index = (layer * 4 + y_off + block // nxb) * nxb + block % nxb
-    picked = jnp.take(frame_rows, index.reshape(-1), axis=0).reshape(index.shape + (BS,))
+    picked = jnp.take(frame_rows, index.reshape(-1), axis=0, mode="clip").reshape(index.shape + (BS,))
     live = (jnp.arange(K, dtype=jnp.int32)[None, None, :] < lives[:, :, None]).astype(
         jnp.float32
     )

time: 122 us -> 122 us (level)
  no operation moved by 1% of the time
where the time goes in v6:
time: 122 us; the launch traced here: 121 us
  starting transfers between devices  37.9 us (31%)
  waiting for transfers between devices  31.8 us (26%)
  local copies, waits for them, and re-layouts  18.6 us (15%)
  blocking collectives  12.2 us (10%)
  matrix products  12.1 us (10%)
  other arithmetic  6.84 us (6%)
  between operations  1.64 us (1%)
    ppermute x10, starting transfers between devices, shift(): return lax.ppermute(value, 'deep', pairs)  18.5 us
    ppermute x8, starting transfers between devices, shift(): return lax.ppermute(value, 'wide', pairs)  15.4 us
    ppermute x8, waiting for transfers between devices, shift(): return lax.ppermute(value, 'wide', pairs)  14.8 us
    all_to_all x1, blocking collectives, local(): got = lax.all_to_all(back, 'wide', 0, 0, tiled=True)  12.2 us
    all_to_all x1, waiting for transfers between devices, local(): got = lax.all_to_all(sent, 'wide', 0, 0, tiled=True)  8.87 us
    unnamed x59, local copies, waits for them, and re-layouts  8.28 us
    ppermute x10, waiting for transfers between devices, shift(): return lax.ppermute(value, 'deep', pairs)  8.11 us
    all_to_all x1, starting transfers between devices, local(): got = lax.all_to_all(sent, 'wide', 0, 0, tiled=True)  4.04 us
  transfers between devices with their start and end apart: 19, of which 13 were waited for; matrix products, arithmetic and copies ran while one was open for 4% of the time, Pallas kernels for 0%

profile of v6, /device:TPU:7, one launch (start us, length us, event | category | flops | bytes accessed | tf_op | source)
XLA Modules:
  0.0 121.1 jit_solution(3839270824280840454)
XLA Ops:
  0.7 1.2 %fusion.72 = (f32[1,16,16,256]{3,2,1,0:T(8,128)S(1)}, f32[1,16,16,256]{3,2,1,0:T(8,128)S(1)}, f32[1,16,16,256]{3,2,1,0:T(8,128)S(1)}) fusion(f32[3,16,16,256]{3,2,1,0:T(8,128)} %param.22), kind=kLoop, calls=%fused_computation.205 | loop fusion | bytes 1572864 | tf_op jit(solution)/shard_map/slice | solution.py:191
  3.5 0.6 copy-done.2
  4.2 1.7 %collective-permute-start.1 = (f32[2,16,256]{2,1,0:T(8,128)S(1)}, f32[2,16,256]{2,1,0:T(8,128)S(1)}, u32[]{:S(2)}, u32[]{:S(2)}) collective-permute-start(f32[2,16,256]{2,1,0:T(8,128)S(1)} %get-tuple-element.14), channel_id=1, source_target_pairs={{248,0},{0,8},{8,16},{16,24},{24,32},{32,40},{40,48},{48,56},{56,6... | collective-permute-start | bytes 98312 | tf_op jit(solution)/shard_map/ppermute | solution.py:71
  5.9 6.5 %collective-permute-start = (f32[2,16,256]{2,1,0:T(8,128)S(1)}, f32[2,16,256]{2,1,0:T(8,128)S(1)}, u32[]{:S(2)}, u32[]{:S(2)}) collective-permute-start(f32[2,16,256]{2,1,0:T(8,128)S(1)} %get-tuple-element.13), channel_id=1, source_target_pairs={{8,0},{16,8},{24,16},{32,24},{40,32},{48,40},{56,48},{64,56},{72,6... | collective-permute-start | bytes 98312 | tf_op jit(solution)/shard_map/ppermute | solution.py:71
  12.4 0.7 copy-done.22
  13.1 0.7 copy-done.24
  13.7 0.6 pad_clamp_fusion
  14.8 1.0 collective-permute-start.2
  15.7 2.0 %collective-permute-start.3 = (f32[2,16,256]{2,1,0:T(8,128)S(1)}, f32[2,16,256]{2,1,0:T(8,128)S(1)}, u32[]{:S(2)}, u32[]{:S(2)}) collective-permute-start(f32[2,16,256]{2,1,0:T(8,128)S(1)} %bitcast.282), channel_id=1, source_target_pairs={{7,0},{0,1},{1,2},{2,3},{3,4},{4,5},{5,6},{6,7},{15,8},{8,9},{9,10... | collective-permute-start | bytes 98312 | tf_op jit(solution)/shard_map/ppermute | solution.py:74
  17.7 1.1 concatenate.143
  20.7 0.9 copy-done
  22.2 0.6 copy-done.1
  24.2 4.1 %collective-permute-start.4 = (f32[16,256]{1,0:T(8,128)S(1)}, f32[16,256]{1,0:T(8,128)S(1)}, u32[]{:S(2)}, u32[]{:S(2)}) collective-permute-start(f32[16,256]{1,0:T(8,128)S(1)} %get-tuple-element.37), channel_id=1, source_target_pairs={{8,0},{16,8},{24,16},{32,24},{40,32},{48,40},{56,48},{64,56},{72,6... | collective-permute-start | bytes 49160 | tf_op jit(solution)/shard_map/ppermute | solution.py:71
  28.4 0.7 fusion.63
  29.2 5.0 %collective-permute-done.5 = f32[16,256]{1,0:T(8,128)S(1)} collective-permute-done((f32[16,256]{1,0:T(8,128)S(1)}, f32[16,256]{1,0:T(8,128)S(1)}, u32[]{:S(2)}, u32[]{:S(2)}) %collective-permute-start.5) | collective-permute-done | bytes 16416 | tf_op jit(solution)/shard_map/ppermute | solution.py:71
  34.4 1.9 %collective-permute-start.6 = (f32[16,256]{1,0:T(8,128)S(1)}, f32[16,256]{1,0:T(8,128)S(1)}, u32[]{:S(2)}, u32[]{:S(2)}) collective-permute-start(f32[16,256]{1,0:T(8,128)S(1)} %bitcast.292), channel_id=1, source_target_pairs={{1,0},{2,1},{3,2},{4,3},{5,4},{6,5},{7,6},{0,7},{9,8},{10,9},{11,1... | collective-permute-start | bytes 49160 | tf_op jit(solution)/shard_map/ppermute | solution.py:74
  36.3 2.4 %collective-permute-start.7 = (f32[16,256]{1,0:T(8,128)S(1)}, f32[16,256]{1,0:T(8,128)S(1)}, u32[]{:S(2)}, u32[]{:S(2)}) collective-permute-start(f32[16,256]{1,0:T(8,128)S(1)} %bitcast.298), channel_id=1, source_target_pairs={{7,0},{0,1},{1,2},{2,3},{3,4},{4,5},{5,6},{6,7},{15,8},{8,9},{9,10... | collective-permute-start | bytes 49160 | tf_op jit(solution)/shard_map/ppermute | solution.py:74
  38.7 0.8 collective-permute-done.7
  42.9 0.6 copy-done.20
  44.9 3.0 %collective-permute-start.8 = (f32[4,4,64]{2,1,0:T(4,128)S(1)}, f32[4,4,64]{2,1,0:T(4,128)S(1)}, u32[]{:S(2)}, u32[]{:S(2)}) collective-permute-start(f32[4,4,64]{2,1,0:T(4,128)S(1)} %reshape.397), channel_id=1, source_target_pairs={{7,0},{0,1},{1,2},{2,3},{3,4},{4,5},{5,6},{6,7},{15,8},{8,9},{9,10... | collective-permute-start | bytes 12296 | tf_op jit(solution)/shard_map/ppermute | solution.py:74
  48.0 0.8 collective-permute-done.8
  48.7 3.5 %collective-permute-done.9 = f32[4,4,64]{2,1,0:T(4,128)S(1)} collective-permute-done((f32[4,4,64]{2,1,0:T(4,128)S(1)}, f32[4,4,64]{2,1,0:T(4,128)S(1)}, u32[]{:S(2)}, u32[]{:S(2)}) %collective-permute-start.9) | collective-permute-done | bytes 4128 | tf_op jit(solution)/shard_map/ppermute | solution.py:74
  53.4 0.8 copy.117
  54.2 4.0 %all-to-all-start = ((f32[32,3,4,3]{2,1,3,0:T(4,128)}), f32[32,3,4,3]{2,1,3,0:T(4,128)S(1)}, u32[]{:S(2)}, u32[]{:S(2)}) async-start(f32[32,3,4,3]{2,1,3,0:T(4,128)} %copy.117), calls=%async_computation | async-start | bytes 393216 | tf_op jit(solution)/shard_map/all_to_all | solution.py:227
  58.2 0.6 pad_clamp_fusion.1
  59.0 8.9 %all-to-all-done = f32[32,3,4,3]{2,1,3,0:T(4,128)S(1)} async-done(((f32[32,3,4,3]{2,1,3,0:T(4,128)}), f32[32,3,4,3]{2,1,3,0:T(4,128)S(1)}, u32[]{:S(2)}, u32[]{:S(2)}) %all-to-all-start) | async-done | bytes 4640 | tf_op jit(solution)/shard_map/all_to_all | solution.py:227
  68.8 1.0 gather_fusion
  69.8 0.8 broadcast_multiply_fusion
  70.6 1.7 %fusion.1 = f32[3,8,1,8,1]{3,2,4,1,0:T(1,128)S(1)} fusion(f32[3,8,8,8,1]{3,4,2,1,0:T(1,128)S(1)} %bitcast.274, f32[1,8,8,8,8]{4,3,2,1,0:T(8,128)S(1)} %concatenate.144, f32[2,8,8,8,8]{4,3,2,1,0:T(8,128)S(1)} %copy-done.5), kind=kOutput, calls=%fused_computation.33 | convolution fusion | flops 159744 | bytes 56064 | tf_op jit(solution)/shard_map/yxkij,yxkj,yxk->yxi/dot_general | solution.py:247
  72.9 0.6 gather_fusion.1
  73.8 12.2 %all_to_all.10 = f32[32,3,3]{2,1,0:T(4,128)S(1)} all-to-all(f32[32,3,3]{2,1,0:T(4,128)S(1)} %copy.125), channel_id=1, replica_groups=mesh['wide'=32,'deep'=8] {'wide'}, dimensions={0} | all-to-all | bytes 2304 | tf_op jit(solution)/shard_map/all_to_all | solution.py:253
  86.9 0.6 copy-done.21
  91.3 0.9 collective-permute-start.10
  92.2 0.7 collective-permute-start.11
  92.8 1.5 %collective-permute-done.10 = f32[16,256]{1,0:T(8,128)S(1)} collective-permute-done((f32[16,256]{1,0:T(8,128)S(1)}, f32[16,256]{1,0:T(8,128)S(1)}, u32[]{:S(2)}, u32[]{:S(2)}) %collective-permute-start.10) | collective-permute-done | bytes 16416 | tf_op jit(solution)/shard_map/ppermute | solution.py:71
  94.3 3.8 %collective-permute-done.11 = f32[16,256]{1,0:T(8,128)S(1)} collective-permute-done((f32[16,256]{1,0:T(8,128)S(1)}, f32[16,256]{1,0:T(8,128)S(1)}, u32[]{:S(2)}, u32[]{:S(2)}) %collective-permute-start.11) | collective-permute-done | bytes 16416 | tf_op jit(solution)/shard_map/ppermute | solution.py:71
  98.1 0.7 copy-done.10
  98.9 0.9 collective-permute-start.12
  99.9 3.2 %collective-permute-start.13 = (f32[16,256]{1,0:T(8,128)S(1)}, f32[16,256]{1,0:T(8,128)S(1)}, u32[]{:S(2)}, u32[]{:S(2)}) collective-permute-start(f32[16,256]{1,0:T(8,128)S(1)} %bitcast.297), channel_id=1, source_target_pairs={{7,0},{0,1},{1,2},{2,3},{3,4},{4,5},{5,6},{6,7},{15,8},{8,9},{9,10... | collective-permute-start | bytes 49160 | tf_op jit(solution)/shard_map/ppermute | solution.py:74
  103.1 1.4 %collective-permute-done.12 = f32[16,256]{1,0:T(8,128)S(1)} collective-permute-done((f32[16,256]{1,0:T(8,128)S(1)}, f32[16,256]{1,0:T(8,128)S(1)}, u32[]{:S(2)}, u32[]{:S(2)}) %collective-permute-start.12) | collective-permute-done | bytes 16416 | tf_op jit(solution)/shard_map/ppermute | solution.py:74
  104.9 0.7 copy-done.17
  108.0 1.5 %collective-permute-start.15 = (f32[16,256]{1,0:T(8,128)S(1)}, f32[16,256]{1,0:T(8,128)S(1)}, u32[]{:S(2)}, u32[]{:S(2)}) collective-permute-start(f32[16,256]{1,0:T(8,128)S(1)} %get-tuple-element.22), channel_id=1, source_target_pairs={{248,0},{0,8},{8,16},{16,24},{24,32},{32,40},{40,48},{48,56},{56,6... | collective-permute-start | bytes 49160 | tf_op jit(solution)/shard_map/ppermute | solution.py:71
  109.4 1.1 collective-permute-done.14
  110.5 3.4 %collective-permute-done.15 = f32[16,256]{1,0:T(8,128)S(1)} collective-permute-done((f32[16,256]{1,0:T(8,128)S(1)}, f32[16,256]{1,0:T(8,128)S(1)}, u32[]{:S(2)}, u32[]{:S(2)}) %collective-permute-start.15) | collective-permute-done | bytes 16416 | tf_op jit(solution)/shard_map/ppermute | solution.py:71
  114.2 4.1 %collective-permute-start.17 = (f32[16,256]{1,0:T(8,128)S(1)}, f32[16,256]{1,0:T(8,128)S(1)}, u32[]{:S(2)}, u32[]{:S(2)}) collective-permute-start(f32[16,256]{1,0:T(8,128)S(1)} %bitcast.295), channel_id=1, source_target_pairs={{7,0},{0,1},{1,2},{2,3},{3,4},{4,5},{5,6},{6,7},{15,8},{8,9},{9,10... | collective-permute-start | bytes 49160 | tf_op jit(solution)/shard_map/ppermute | solution.py:74
  118.3 0.6 reshape.408
  118.9 0.7 collective-permute-done.16
  120.1 1.0 fusion.51
  (209 shorter events, 21.9 us)
Async XLA Ops:
  0.6 1.2 %copy-start.6 = (f32[256,256]{1,0:T(8,128)S(1)}, f32[256,256]{1,0:T(8,128)}, u32[]{:S(2)}) copy-start(f32[256,256]{1,0:T(8,128)} %constant.191.clone) | copy-start | bytes 786436
  0.6 1.3 %copy-start.3 = (f32[16,16,256]{2,1,0:T(8,128)S(1)}, f32[16,16,256]{2,1,0:T(8,128)}, u32[]{:S(2)}) copy-start(f32[16,16,256]{2,1,0:T(8,128)} %param.23) | copy-start | bytes 786436
  1.9 0.9 copy-start.4
  3.2 1.0 copy-start.2
  4.2 8.2 %copy-start.8 = (f32[1,2,8,512]{3,2,1,0:T(8,128)S(1)}, f32[1,2,8,512]{3,2,1,0:T(8,128)}, u32[]{:S(2)}) copy-start(f32[1,2,8,512]{3,2,1,0:T(8,128)} %param.26) | copy-start | bytes 98308
  4.2 10.2 %collective-permute-start.1 = (f32[2,16,256]{2,1,0:T(8,128)S(1)}, f32[2,16,256]{2,1,0:T(8,128)S(1)}, u32[]{:S(2)}, u32[]{:S(2)}) collective-permute-start(f32[2,16,256]{2,1,0:T(8,128)S(1)} %get-tuple-element.14), channel_id=1, source_target_pairs={{248,0},{0,8},{8,16},{16,24},{24,32},{32,40},{40,48},{48,56},{56,6... | collective-permute-start | bytes 98312 | tf_op jit(solution)/shard_map/ppermute | solution.py:71
  5.9 6.5 %copy-start.13 = (s32[1,2,8,8]{3,2,1,0:T(8,128)S(1)}, s32[1,2,8,8]{3,2,1,0:T(8,128)}, u32[]{:S(2)}) copy-start(s32[1,2,8,8]{3,2,1,0:T(8,128)} %param.24) | copy-start | bytes 1540
  5.9 8.5 %collective-permute-start = (f32[2,16,256]{2,1,0:T(8,128)S(1)}, f32[2,16,256]{2,1,0:T(8,128)S(1)}, u32[]{:S(2)}, u32[]{:S(2)}) collective-permute-start(f32[2,16,256]{2,1,0:T(8,128)S(1)} %get-tuple-element.13), channel_id=1, source_target_pairs={{8,0},{16,8},{24,16},{32,24},{40,32},{48,40},{56,48},{64,56},{72,6... | collective-permute-start | bytes 98312 | tf_op jit(solution)/shard_map/ppermute | solution.py:71
  12.4 0.7 copy-start.22
  13.1 0.7 copy-start.24
  14.4 26.1 %copy-start.9 = (pred[16]{0:T(512)(128)(4,1)}, pred[16]{0:T(512)(128)(4,1)S(1)}, u32[]{:S(2)}) copy-start(pred[16]{0:T(512)(128)(4,1)S(1)} %get-tuple-element.49) | copy-start | bytes 52
  14.4 26.1 %copy-start.11 = (pred[16]{0:T(512)(128)(4,1)}, pred[16]{0:T(512)(128)(4,1)S(1)}, u32[]{:S(2)}) copy-start(pred[16]{0:T(512)(128)(4,1)S(1)} %get-tuple-element.50) | copy-start | bytes 52
  14.8 4.8 %collective-permute-start.2 = (f32[12360]{0:T(1024)S(1)}, f32[12360]{0:T(1024)S(1)}, u32[]{:S(2)}, u32[]{:S(2)}) collective-permute-start(f32[12360]{0:T(1024)S(1)} %concatenate.132), channel_id=1, source_target_pairs={{1,0},{2,1},{3,2},{4,3},{5,4},{6,5},{7,6},{0,7},{9,8},{10,9},{11,1... | collective-permute-start | bytes 148328 | tf_op jit(solution)/shard_map/ppermute | solution.py:74
  15.7 3.3 %collective-permute-start.3 = (f32[2,16,256]{2,1,0:T(8,128)S(1)}, f32[2,16,256]{2,1,0:T(8,128)S(1)}, u32[]{:S(2)}, u32[]{:S(2)}) collective-permute-start(f32[2,16,256]{2,1,0:T(8,128)S(1)} %bitcast.282), channel_id=1, source_target_pairs={{7,0},{0,1},{1,2},{2,3},{3,4},{4,5},{5,6},{6,7},{15,8},{8,9},{9,10... | collective-permute-start | bytes 98312 | tf_op jit(solution)/shard_map/ppermute | solution.py:74
  17.7 22.7 %copy-start.16 = (pred[256]{0:T(512)(128)(4,1)}, pred[256]{0:T(512)(128)(4,1)S(1)}, u32[]{:S(2)}) copy-start(pred[256]{0:T(512)(128)(4,1)S(1)} %get-tuple-element.51) | copy-start | bytes 772
  17.7 22.7 %copy-start.18 = (pred[256]{0:T(512)(128)(4,1)}, pred[256]{0:T(512)(128)(4,1)S(1)}, u32[]{:S(2)}) copy-start(pred[256]{0:T(512)(128)(4,1)S(1)} %get-tuple-element.52) | copy-start | bytes 772
  17.7 1.1 copy-start.23
  20.6 1.0 copy-start
  21.8 1.0 copy-start.1
  24.2 5.0 %collective-permute-start.4 = (f32[16,256]{1,0:T(8,128)S(1)}, f32[16,256]{1,0:T(8,128)S(1)}, u32[]{:S(2)}, u32[]{:S(2)}) collective-permute-start(f32[16,256]{1,0:T(8,128)S(1)} %get-tuple-element.37), channel_id=1, source_target_pairs={{8,0},{16,8},{24,16},{32,24},{40,32},{48,40},{56,48},{64,56},{72,6... | collective-permute-start | bytes 49160 | tf_op jit(solution)/shard_map/ppermute | solution.py:71
  28.3 5.9 %collective-permute-start.5 = (f32[16,256]{1,0:T(8,128)S(1)}, f32[16,256]{1,0:T(8,128)S(1)}, u32[]{:S(2)}, u32[]{:S(2)}) collective-permute-start(f32[16,256]{1,0:T(8,128)S(1)} %get-tuple-element.38), channel_id=1, source_target_pairs={{248,0},{0,8},{8,16},{16,24},{24,32},{32,40},{40,48},{48,56},{56,6... | collective-permute-start | bytes 49160 | tf_op jit(solution)/shard_map/ppermute | solution.py:71
  34.4 5.7 %collective-permute-start.6 = (f32[16,256]{1,0:T(8,128)S(1)}, f32[16,256]{1,0:T(8,128)S(1)}, u32[]{:S(2)}, u32[]{:S(2)}) collective-permute-start(f32[16,256]{1,0:T(8,128)S(1)} %bitcast.292), channel_id=1, source_target_pairs={{1,0},{2,1},{3,2},{4,3},{5,4},{6,5},{7,6},{0,7},{9,8},{10,9},{11,1... | collective-permute-start | bytes 49160 | tf_op jit(solution)/shard_map/ppermute | solution.py:74
  36.3 3.2 %collective-permute-start.7 = (f32[16,256]{1,0:T(8,128)S(1)}, f32[16,256]{1,0:T(8,128)S(1)}, u32[]{:S(2)}, u32[]{:S(2)}) collective-permute-start(f32[16,256]{1,0:T(8,128)S(1)} %bitcast.298), channel_id=1, source_target_pairs={{7,0},{0,1},{1,2},{2,3},{3,4},{4,5},{5,6},{6,7},{15,8},{8,9},{9,10... | collective-permute-start | bytes 49160 | tf_op jit(solution)/shard_map/ppermute | solution.py:74
  42.8 0.7 copy-start.20
  43.9 0.7 copy-start.15
  44.9 3.8 %collective-permute-start.8 = (f32[4,4,64]{2,1,0:T(4,128)S(1)}, f32[4,4,64]{2,1,0:T(4,128)S(1)}, u32[]{:S(2)}, u32[]{:S(2)}) collective-permute-start(f32[4,4,64]{2,1,0:T(4,128)S(1)} %reshape.397), channel_id=1, source_target_pairs={{7,0},{0,1},{1,2},{2,3},{3,4},{4,5},{5,6},{6,7},{15,8},{8,9},{9,10... | collective-permute-start | bytes 12296 | tf_op jit(solution)/shard_map/ppermute | solution.py:74
  47.9 4.3 %collective-permute-start.9 = (f32[4,4,64]{2,1,0:T(4,128)S(1)}, f32[4,4,64]{2,1,0:T(4,128)S(1)}, u32[]{:S(2)}, u32[]{:S(2)}) collective-permute-start(f32[4,4,64]{2,1,0:T(4,128)S(1)} %reshape.397), channel_id=1, source_target_pairs={{1,0},{2,1},{3,2},{4,3},{5,4},{6,5},{7,6},{0,7},{9,8},{10,9},{11,1... | collective-permute-start | bytes 12296 | tf_op jit(solution)/shard_map/ppermute | solution.py:74
  54.2 13.7 %all-to-all-start = ((f32[32,3,4,3]{2,1,3,0:T(4,128)}), f32[32,3,4,3]{2,1,3,0:T(4,128)S(1)}, u32[]{:S(2)}, u32[]{:S(2)}) async-start(f32[32,3,4,3]{2,1,3,0:T(4,128)} %copy.117), calls=%async_computation | async-start | bytes 393216 | tf_op jit(solution)/shard_map/all_to_all | solution.py:227
  68.8 1.8 %copy-start.5 = (f32[2,8,8,8,8]{4,3,2,1,0:T(8,128)S(1)}, f32[2,8,8,8,8]{4,3,2,1,0:T(8,128)}, u32[]{:S(2)}) copy-start(f32[2,8,8,8,8]{4,3,2,1,0:T(8,128)} %concatenate.143) | copy-start | bytes 98308
  72.2 0.7 copy-start.7
  86.8 0.7 copy-start.21
  88.1 0.7 copy-start.14
  91.3 3.0 %collective-permute-start.10 = (f32[16,256]{1,0:T(8,128)S(1)}, f32[16,256]{1,0:T(8,128)S(1)}, u32[]{:S(2)}, u32[]{:S(2)}) collective-permute-start(f32[16,256]{1,0:T(8,128)S(1)} %get-tuple-element.29), channel_id=1, source_target_pairs={{8,0},{16,8},{24,16},{32,24},{40,32},{48,40},{56,48},{64,56},{72,6... | collective-permute-start | bytes 49160 | tf_op jit(solution)/shard_map/ppermute | solution.py:71
  92.2 5.9 %collective-permute-start.11 = (f32[16,256]{1,0:T(8,128)S(1)}, f32[16,256]{1,0:T(8,128)S(1)}, u32[]{:S(2)}, u32[]{:S(2)}) collective-permute-start(f32[16,256]{1,0:T(8,128)S(1)} %get-tuple-element.30), channel_id=1, source_target_pairs={{248,0},{0,8},{8,16},{16,24},{24,32},{32,40},{40,48},{48,56},{56,6... | collective-permute-start | bytes 49160 | tf_op jit(solution)/shard_map/ppermute | solution.py:71
  98.1 0.7 copy-start.10
  98.1 0.7 copy-start.12
  98.9 5.5 %collective-permute-start.12 = (f32[16,256]{1,0:T(8,128)S(1)}, f32[16,256]{1,0:T(8,128)S(1)}, u32[]{:S(2)}, u32[]{:S(2)}) collective-permute-start(f32[16,256]{1,0:T(8,128)S(1)} %bitcast.296), channel_id=1, source_target_pairs={{1,0},{2,1},{3,2},{4,3},{5,4},{6,5},{7,6},{0,7},{9,8},{10,9},{11,1... | collective-permute-start | bytes 49160 | tf_op jit(solution)/shard_map/ppermute | solution.py:74
  99.9 4.6 %collective-permute-start.13 = (f32[16,256]{1,0:T(8,128)S(1)}, f32[16,256]{1,0:T(8,128)S(1)}, u32[]{:S(2)}, u32[]{:S(2)}) collective-permute-start(f32[16,256]{1,0:T(8,128)S(1)} %bitcast.297), channel_id=1, source_target_pairs={{7,0},{0,1},{1,2},{2,3},{3,4},{4,5},{5,6},{6,7},{15,8},{8,9},{9,10... | collective-permute-start | bytes 49160 | tf_op jit(solution)/shard_map/ppermute | solution.py:74
  104.9 0.7 copy-start.17
  104.9 0.7 copy-start.19
  107.9 2.7 %collective-permute-start.14 = (f32[16,256]{1,0:T(8,128)S(1)}, f32[16,256]{1,0:T(8,128)S(1)}, u32[]{:S(2)}, u32[]{:S(2)}) collective-permute-start(f32[16,256]{1,0:T(8,128)S(1)} %get-tuple-element.21), channel_id=1, source_target_pairs={{8,0},{16,8},{24,16},{32,24},{40,32},{48,40},{56,48},{64,56},{72,6... | collective-permute-start | bytes 49160 | tf_op jit(solution)/shard_map/ppermute | solution.py:71
  108.0 6.0 %collective-permute-start.15 = (f32[16,256]{1,0:T(8,128)S(1)}, f32[16,256]{1,0:T(8,128)S(1)}, u32[]{:S(2)}, u32[]{:S(2)}) collective-permute-start(f32[16,256]{1,0:T(8,128)S(1)} %get-tuple-element.22), channel_id=1, source_target_pairs={{248,0},{0,8},{8,16},{16,24},{24,32},{32,40},{40,48},{48,56},{56,6... | collective-permute-start | bytes 49160 | tf_op jit(solution)/shard_map/ppermute | solution.py:71
  114.1 5.5 %collective-permute-start.16 = (f32[16,256]{1,0:T(8,128)S(1)}, f32[16,256]{1,0:T(8,128)S(1)}, u32[]{:S(2)}, u32[]{:S(2)}) collective-permute-start(f32[16,256]{1,0:T(8,128)S(1)} %bitcast.293), channel_id=1, source_target_pairs={{1,0},{2,1},{3,2},{4,3},{5,4},{6,5},{7,6},{0,7},{9,8},{10,9},{11,1... | collective-permute-start | bytes 49160 | tf_op jit(solution)/shard_map/ppermute | solution.py:74
  114.2 5.5 %collective-permute-start.17 = (f32[16,256]{1,0:T(8,128)S(1)}, f32[16,256]{1,0:T(8,128)S(1)}, u32[]{:S(2)}, u32[]{:S(2)}) collective-permute-start(f32[16,256]{1,0:T(8,128)S(1)} %bitcast.295), channel_id=1, source_target_pairs={{7,0},{0,1},{1,2},{2,3},{3,4},{4,5},{5,6},{6,7},{15,8},{8,9},{9,10... | collective-permute-start | bytes 49160 | tf_op jit(solution)/shard_map/ppermute | solution.py:74

commit v7 on v3

--- a/solution.py
+++ b/solution.py
@@ -53,13 +53,13 @@
 
 def contract(field, table, axis):
     if axis == 0:
-        return jnp.einsum("mi,iyz->myz", table, field, precision=highest)
+        return jnp.einsum("mi,iyz->myz", table, field, precision=fast)
     if axis == 1:
-        return jnp.einsum("mj,xjz->xmz", table, field, precision=highest)
+        return jnp.einsum("mj,xjz->xmz", table, field, precision=fast)
     shape = field.shape
     blocked = table.shape[1]
     grid = field.reshape(shape[0], shape[1], shape[2] // blocked, blocked)
-    result = jnp.einsum("mk,xynk->xynm", table, grid, precision=highest)
+    result = jnp.einsum("mk,xynk->xynm", table, grid, precision=fast)
     return result.reshape(shape[0], shape[1], -1)
 
 

time: 122 us -> 122 us (level)
  no operation moved by 1% of the time
where the time goes in v7:
time: 122 us; the launch traced here: 121 us
  starting transfers between devices  37.9 us (31%)
  waiting for transfers between devices  31.2 us (26%)
  local copies, waits for them, and re-layouts  18.6 us (15%)
  blocking collectives  12.2 us (10%)
  matrix products  11.8 us (10%)
  other arithmetic  7.55 us (6%)
  between operations  1.63 us (1%)
    ppermute x10, starting transfers between devices, shift(): return lax.ppermute(value, 'deep', pairs)  18.5 us
    ppermute x8, starting transfers between devices, shift(): return lax.ppermute(value, 'wide', pairs)  15.4 us
    ppermute x8, waiting for transfers between devices, shift(): return lax.ppermute(value, 'wide', pairs)  14.2 us
    all_to_all x1, blocking collectives, local(): got = lax.all_to_all(back, 'wide', 0, 0, tiled=True)  12.2 us
    all_to_all x1, waiting for transfers between devices, local(): got = lax.all_to_all(sent, 'wide', 0, 0, tiled=True)  8.87 us
    unnamed x59, local copies, waits for them, and re-layouts  8.27 us
    ppermute x10, waiting for transfers between devices, shift(): return lax.ppermute(value, 'deep', pairs)  8.11 us
    all_to_all x1, starting transfers between devices, local(): got = lax.all_to_all(sent, 'wide', 0, 0, tiled=True)  4.05 us
  transfers between devices with their start and end apart: 19, of which 13 were waited for; matrix products, arithmetic and copies ran while one was open for 4% of the time, Pallas kernels for 0%

profile of v7, /device:TPU:7, one launch (start us, length us, event | category | flops | bytes accessed | tf_op | source)
XLA Modules:
  0.0 120.8 jit_solution(13967012140046471354)
XLA Ops:
  0.7 1.2 %fusion.83 = (f32[1,16,16,256]{3,2,1,0:T(8,128)S(1)}, f32[1,16,16,256]{3,2,1,0:T(8,128)S(1)}, f32[1,16,16,256]{3,2,1,0:T(8,128)S(1)}) fusion(f32[3,16,16,256]{3,2,1,0:T(8,128)} %param.22), kind=kLoop, calls=%fused_computation.231 | loop fusion | bytes 1572864 | tf_op jit(solution)/shard_map/slice | solution.py:191
  3.5 0.6 copy-done.2
  4.2 1.7 %collective-permute-start.1 = (f32[2,16,256]{2,1,0:T(8,128)S(1)}, f32[2,16,256]{2,1,0:T(8,128)S(1)}, u32[]{:S(2)}, u32[]{:S(2)}) collective-permute-start(f32[2,16,256]{2,1,0:T(8,128)S(1)} %get-tuple-element.14), channel_id=1, source_target_pairs={{248,0},{0,8},{8,16},{16,24},{24,32},{32,40},{40,48},{48,56},{56,6... | collective-permute-start | bytes 98312 | tf_op jit(solution)/shard_map/ppermute | solution.py:71
  5.9 6.5 %collective-permute-start = (f32[2,16,256]{2,1,0:T(8,128)S(1)}, f32[2,16,256]{2,1,0:T(8,128)S(1)}, u32[]{:S(2)}, u32[]{:S(2)}) collective-permute-start(f32[2,16,256]{2,1,0:T(8,128)S(1)} %get-tuple-element.13), channel_id=1, source_target_pairs={{8,0},{16,8},{24,16},{32,24},{40,32},{48,40},{56,48},{64,56},{72,6... | collective-permute-start | bytes 98312 | tf_op jit(solution)/shard_map/ppermute | solution.py:71
  12.4 0.7 copy-done.23
  13.1 0.7 copy-done.24
  13.7 0.6 pad_clamp_fusion
  14.8 1.0 collective-permute-start.2
  15.7 2.0 %collective-permute-start.3 = (f32[2,16,256]{2,1,0:T(8,128)S(1)}, f32[2,16,256]{2,1,0:T(8,128)S(1)}, u32[]{:S(2)}, u32[]{:S(2)}) collective-permute-start(f32[2,16,256]{2,1,0:T(8,128)S(1)} %bitcast.284), channel_id=1, source_target_pairs={{7,0},{0,1},{1,2},{2,3},{3,4},{4,5},{5,6},{6,7},{15,8},{8,9},{9,10... | collective-permute-start | bytes 98312 | tf_op jit(solution)/shard_map/ppermute | solution.py:74
  17.7 1.1 concatenate.143
  20.7 0.9 copy-done
  22.2 0.6 copy-done.1
  24.2 4.1 %collective-permute-start.4 = (f32[16,256]{1,0:T(8,128)S(1)}, f32[16,256]{1,0:T(8,128)S(1)}, u32[]{:S(2)}, u32[]{:S(2)}) collective-permute-start(f32[16,256]{1,0:T(8,128)S(1)} %get-tuple-element.37), channel_id=1, source_target_pairs={{8,0},{16,8},{24,16},{32,24},{40,32},{48,40},{56,48},{64,56},{72,6... | collective-permute-start | bytes 49160 | tf_op jit(solution)/shard_map/ppermute | solution.py:71
  28.5 0.7 fusion.73
  29.2 0.7 compare_and_fusion
  29.8 4.4 %collective-permute-done.5 = f32[16,256]{1,0:T(8,128)S(1)} collective-permute-done((f32[16,256]{1,0:T(8,128)S(1)}, f32[16,256]{1,0:T(8,128)S(1)}, u32[]{:S(2)}, u32[]{:S(2)}) %collective-permute-start.5) | collective-permute-done | bytes 16416 | tf_op jit(solution)/shard_map/ppermute | solution.py:71
  34.4 1.9 %collective-permute-start.6 = (f32[16,256]{1,0:T(8,128)S(1)}, f32[16,256]{1,0:T(8,128)S(1)}, u32[]{:S(2)}, u32[]{:S(2)}) collective-permute-start(f32[16,256]{1,0:T(8,128)S(1)} %bitcast.293), channel_id=1, source_target_pairs={{1,0},{2,1},{3,2},{4,3},{5,4},{6,5},{7,6},{0,7},{9,8},{10,9},{11,1... | collective-permute-start | bytes 49160 | tf_op jit(solution)/shard_map/ppermute | solution.py:74
  36.3 2.4 %collective-permute-start.7 = (f32[16,256]{1,0:T(8,128)S(1)}, f32[16,256]{1,0:T(8,128)S(1)}, u32[]{:S(2)}, u32[]{:S(2)}) collective-permute-start(f32[16,256]{1,0:T(8,128)S(1)} %bitcast.299), channel_id=1, source_target_pairs={{7,0},{0,1},{1,2},{2,3},{3,4},{4,5},{5,6},{6,7},{15,8},{8,9},{9,10... | collective-permute-start | bytes 49160 | tf_op jit(solution)/shard_map/ppermute | solution.py:74
  38.8 0.8 collective-permute-done.7
  42.9 0.6 copy-done.20
  44.8 3.0 %collective-permute-start.8 = (f32[4,4,64]{2,1,0:T(4,128)S(1)}, f32[4,4,64]{2,1,0:T(4,128)S(1)}, u32[]{:S(2)}, u32[]{:S(2)}) collective-permute-start(f32[4,4,64]{2,1,0:T(4,128)S(1)} %reshape.416), channel_id=1, source_target_pairs={{7,0},{0,1},{1,2},{2,3},{3,4},{4,5},{5,6},{6,7},{15,8},{8,9},{9,10... | collective-permute-start | bytes 12296 | tf_op jit(solution)/shard_map/ppermute | solution.py:74
  47.9 0.8 collective-permute-done.8
  48.6 3.5 %collective-permute-done.9 = f32[4,4,64]{2,1,0:T(4,128)S(1)} collective-permute-done((f32[4,4,64]{2,1,0:T(4,128)S(1)}, f32[4,4,64]{2,1,0:T(4,128)S(1)}, u32[]{:S(2)}, u32[]{:S(2)}) %collective-permute-start.9) | collective-permute-done | bytes 4128 | tf_op jit(solution)/shard_map/ppermute | solution.py:74
  53.3 0.8 copy.117
  54.1 4.0 %all-to-all-start = ((f32[32,3,4,3]{2,1,3,0:T(4,128)}), f32[32,3,4,3]{2,1,3,0:T(4,128)S(1)}, u32[]{:S(2)}, u32[]{:S(2)}) async-start(f32[32,3,4,3]{2,1,3,0:T(4,128)} %copy.117), calls=%async_computation | async-start | bytes 393216 | tf_op jit(solution)/shard_map/all_to_all | solution.py:227
  58.1 0.6 pad_clamp_fusion.1
  58.9 8.9 %all-to-all-done = f32[32,3,4,3]{2,1,3,0:T(4,128)S(1)} async-done(((f32[32,3,4,3]{2,1,3,0:T(4,128)}), f32[32,3,4,3]{2,1,3,0:T(4,128)S(1)}, u32[]{:S(2)}, u32[]{:S(2)}) %all-to-all-start) | async-done | bytes 4640 | tf_op jit(solution)/shard_map/all_to_all | solution.py:227
  68.7 1.0 gather_fusion
  69.7 0.8 select_multiply_fusion
  70.5 1.7 %fusion.1 = f32[3,8,1,8,1]{3,2,4,1,0:T(1,128)S(1)} fusion(f32[3,8,8,8,1]{3,4,2,1,0:T(1,128)S(1)} %bitcast.274, f32[1,8,8,8,8]{4,3,2,1,0:T(8,128)S(1)} %concatenate.144, f32[2,8,8,8,8]{4,3,2,1,0:T(8,128)S(1)} %copy-done.5), kind=kOutput, calls=%fused_computation.33 | convolution fusion | flops 159744 | bytes 56064 | tf_op jit(solution)/shard_map/yxkij,yxkj,yxk->yxi/dot_general | solution.py:247
  72.8 0.6 gather_fusion.1
  73.7 12.2 %all_to_all.10 = f32[32,3,3]{2,1,0:T(4,128)S(1)} all-to-all(f32[32,3,3]{2,1,0:T(4,128)S(1)} %copy.125), channel_id=1, replica_groups=mesh['wide'=32,'deep'=8] {'wide'}, dimensions={0} | all-to-all | bytes 2304 | tf_op jit(solution)/shard_map/all_to_all | solution.py:253
  86.9 0.6 copy-done.21
  91.0 0.9 collective-permute-start.10
  91.9 0.7 collective-permute-start.11
  92.6 1.5 %collective-permute-done.10 = f32[16,256]{1,0:T(8,128)S(1)} collective-permute-done((f32[16,256]{1,0:T(8,128)S(1)}, f32[16,256]{1,0:T(8,128)S(1)}, u32[]{:S(2)}, u32[]{:S(2)}) %collective-permute-start.10) | collective-permute-done | bytes 16416 | tf_op jit(solution)/shard_map/ppermute | solution.py:71
  94.1 3.7 %collective-permute-done.11 = f32[16,256]{1,0:T(8,128)S(1)} collective-permute-done((f32[16,256]{1,0:T(8,128)S(1)}, f32[16,256]{1,0:T(8,128)S(1)}, u32[]{:S(2)}, u32[]{:S(2)}) %collective-permute-start.11) | collective-permute-done | bytes 16416 | tf_op jit(solution)/shard_map/ppermute | solution.py:71
  97.8 0.7 copy-done.10
  98.7 0.9 collective-permute-start.12
  99.6 3.2 %collective-permute-start.13 = (f32[16,256]{1,0:T(8,128)S(1)}, f32[16,256]{1,0:T(8,128)S(1)}, u32[]{:S(2)}, u32[]{:S(2)}) collective-permute-start(f32[16,256]{1,0:T(8,128)S(1)} %bitcast.298), channel_id=1, source_target_pairs={{7,0},{0,1},{1,2},{2,3},{3,4},{4,5},{5,6},{6,7},{15,8},{8,9},{9,10... | collective-permute-start | bytes 49160 | tf_op jit(solution)/shard_map/ppermute | solution.py:74
  102.8 1.4 %collective-permute-done.12 = f32[16,256]{1,0:T(8,128)S(1)} collective-permute-done((f32[16,256]{1,0:T(8,128)S(1)}, f32[16,256]{1,0:T(8,128)S(1)}, u32[]{:S(2)}, u32[]{:S(2)}) %collective-permute-start.12) | collective-permute-done | bytes 16416 | tf_op jit(solution)/shard_map/ppermute | solution.py:74
  107.7 1.5 %collective-permute-start.15 = (f32[16,256]{1,0:T(8,128)S(1)}, f32[16,256]{1,0:T(8,128)S(1)}, u32[]{:S(2)}, u32[]{:S(2)}) collective-permute-start(f32[16,256]{1,0:T(8,128)S(1)} %get-tuple-element.22), channel_id=1, source_target_pairs={{248,0},{0,8},{8,16},{16,24},{24,32},{32,40},{40,48},{48,56},{56,6... | collective-permute-start | bytes 49160 | tf_op jit(solution)/shard_map/ppermute | solution.py:71
  109.1 1.1 collective-permute-done.14
  110.2 3.4 %collective-permute-done.15 = f32[16,256]{1,0:T(8,128)S(1)} collective-permute-done((f32[16,256]{1,0:T(8,128)S(1)}, f32[16,256]{1,0:T(8,128)S(1)}, u32[]{:S(2)}, u32[]{:S(2)}) %collective-permute-start.15) | collective-permute-done | bytes 16416 | tf_op jit(solution)/shard_map/ppermute | solution.py:71
  113.9 4.1 %collective-permute-start.17 = (f32[16,256]{1,0:T(8,128)S(1)}, f32[16,256]{1,0:T(8,128)S(1)}, u32[]{:S(2)}, u32[]{:S(2)}) collective-permute-start(f32[16,256]{1,0:T(8,128)S(1)} %bitcast.296), channel_id=1, source_target_pairs={{7,0},{0,1},{1,2},{2,3},{3,4},{4,5},{5,6},{6,7},{15,8},{8,9},{9,10... | collective-permute-start | bytes 49160 | tf_op jit(solution)/shard_map/ppermute | solution.py:74
  118.0 0.6 reshape.426
  118.6 0.7 collective-permute-done.16
  119.8 1.0 fusion.51
  (210 shorter events, 22.2 us)
Async XLA Ops:
  0.6 1.2 %copy-start.6 = (f32[256,256]{1,0:T(8,128)S(1)}, f32[256,256]{1,0:T(8,128)}, u32[]{:S(2)}) copy-start(f32[256,256]{1,0:T(8,128)} %constant.210.clone) | copy-start | bytes 786436
  0.6 1.3 %copy-start.3 = (f32[16,16,256]{2,1,0:T(8,128)S(1)}, f32[16,16,256]{2,1,0:T(8,128)}, u32[]{:S(2)}) copy-start(f32[16,16,256]{2,1,0:T(8,128)} %param.23) | copy-start | bytes 786436
  1.9 0.9 copy-start.4
  3.2 1.0 copy-start.2
  4.2 8.2 %copy-start.8 = (f32[1,2,8,512]{3,2,1,0:T(8,128)S(1)}, f32[1,2,8,512]{3,2,1,0:T(8,128)}, u32[]{:S(2)}) copy-start(f32[1,2,8,512]{3,2,1,0:T(8,128)} %param.26) | copy-start | bytes 98308
  4.2 10.2 %collective-permute-start.1 = (f32[2,16,256]{2,1,0:T(8,128)S(1)}, f32[2,16,256]{2,1,0:T(8,128)S(1)}, u32[]{:S(2)}, u32[]{:S(2)}) collective-permute-start(f32[2,16,256]{2,1,0:T(8,128)S(1)} %get-tuple-element.14), channel_id=1, source_target_pairs={{248,0},{0,8},{8,16},{16,24},{24,32},{32,40},{40,48},{48,56},{56,6... | collective-permute-start | bytes 98312 | tf_op jit(solution)/shard_map/ppermute | solution.py:71
  5.9 6.5 %copy-start.13 = (s32[1,2,8,8]{3,2,1,0:T(8,128)S(1)}, s32[1,2,8,8]{3,2,1,0:T(8,128)}, u32[]{:S(2)}) copy-start(s32[1,2,8,8]{3,2,1,0:T(8,128)} %param.24) | copy-start | bytes 1540
  5.9 8.5 %collective-permute-start = (f32[2,16,256]{2,1,0:T(8,128)S(1)}, f32[2,16,256]{2,1,0:T(8,128)S(1)}, u32[]{:S(2)}, u32[]{:S(2)}) collective-permute-start(f32[2,16,256]{2,1,0:T(8,128)S(1)} %get-tuple-element.13), channel_id=1, source_target_pairs={{8,0},{16,8},{24,16},{32,24},{40,32},{48,40},{56,48},{64,56},{72,6... | collective-permute-start | bytes 98312 | tf_op jit(solution)/shard_map/ppermute | solution.py:71
  12.4 0.7 copy-start.23
  13.1 0.7 copy-start.24
  14.4 26.1 %copy-start.9 = (pred[16]{0:T(512)(128)(4,1)}, pred[16]{0:T(512)(128)(4,1)S(1)}, u32[]{:S(2)}) copy-start(pred[16]{0:T(512)(128)(4,1)S(1)} %get-tuple-element.49) | copy-start | bytes 52
  14.4 26.1 %copy-start.11 = (pred[16]{0:T(512)(128)(4,1)}, pred[16]{0:T(512)(128)(4,1)S(1)}, u32[]{:S(2)}) copy-start(pred[16]{0:T(512)(128)(4,1)S(1)} %get-tuple-element.50) | copy-start | bytes 52
  14.8 4.8 %collective-permute-start.2 = (f32[12360]{0:T(1024)S(1)}, f32[12360]{0:T(1024)S(1)}, u32[]{:S(2)}, u32[]{:S(2)}) collective-permute-start(f32[12360]{0:T(1024)S(1)} %concatenate.132), channel_id=1, source_target_pairs={{1,0},{2,1},{3,2},{4,3},{5,4},{6,5},{7,6},{0,7},{9,8},{10,9},{11,1... | collective-permute-start | bytes 148328 | tf_op jit(solution)/shard_map/ppermute | solution.py:74
  15.7 3.3 %collective-permute-start.3 = (f32[2,16,256]{2,1,0:T(8,128)S(1)}, f32[2,16,256]{2,1,0:T(8,128)S(1)}, u32[]{:S(2)}, u32[]{:S(2)}) collective-permute-start(f32[2,16,256]{2,1,0:T(8,128)S(1)} %bitcast.284), channel_id=1, source_target_pairs={{7,0},{0,1},{1,2},{2,3},{3,4},{4,5},{5,6},{6,7},{15,8},{8,9},{9,10... | collective-permute-start | bytes 98312 | tf_op jit(solution)/shard_map/ppermute | solution.py:74
  17.7 22.7 %copy-start.16 = (pred[256]{0:T(512)(128)(4,1)}, pred[256]{0:T(512)(128)(4,1)S(1)}, u32[]{:S(2)}) copy-start(pred[256]{0:T(512)(128)(4,1)S(1)} %get-tuple-element.51) | copy-start | bytes 772
  17.7 22.7 %copy-start.18 = (pred[256]{0:T(512)(128)(4,1)}, pred[256]{0:T(512)(128)(4,1)S(1)}, u32[]{:S(2)}) copy-start(pred[256]{0:T(512)(128)(4,1)S(1)} %get-tuple-element.52) | copy-start | bytes 772
  17.7 1.1 copy-start.22
  20.6 1.0 copy-start
  21.8 1.0 copy-start.1
  24.2 5.6 %collective-permute-start.4 = (f32[16,256]{1,0:T(8,128)S(1)}, f32[16,256]{1,0:T(8,128)S(1)}, u32[]{:S(2)}, u32[]{:S(2)}) collective-permute-start(f32[16,256]{1,0:T(8,128)S(1)} %get-tuple-element.37), channel_id=1, source_target_pairs={{8,0},{16,8},{24,16},{32,24},{40,32},{48,40},{56,48},{64,56},{72,6... | collective-permute-start | bytes 49160 | tf_op jit(solution)/shard_map/ppermute | solution.py:71
  28.3 5.9 %collective-permute-start.5 = (f32[16,256]{1,0:T(8,128)S(1)}, f32[16,256]{1,0:T(8,128)S(1)}, u32[]{:S(2)}, u32[]{:S(2)}) collective-permute-start(f32[16,256]{1,0:T(8,128)S(1)} %get-tuple-element.38), channel_id=1, source_target_pairs={{248,0},{0,8},{8,16},{16,24},{24,32},{32,40},{40,48},{48,56},{56,6... | collective-permute-start | bytes 49160 | tf_op jit(solution)/shard_map/ppermute | solution.py:71
  34.4 5.7 %collective-permute-start.6 = (f32[16,256]{1,0:T(8,128)S(1)}, f32[16,256]{1,0:T(8,128)S(1)}, u32[]{:S(2)}, u32[]{:S(2)}) collective-permute-start(f32[16,256]{1,0:T(8,128)S(1)} %bitcast.293), channel_id=1, source_target_pairs={{1,0},{2,1},{3,2},{4,3},{5,4},{6,5},{7,6},{0,7},{9,8},{10,9},{11,1... | collective-permute-start | bytes 49160 | tf_op jit(solution)/shard_map/ppermute | solution.py:74
  36.3 3.2 %collective-permute-start.7 = (f32[16,256]{1,0:T(8,128)S(1)}, f32[16,256]{1,0:T(8,128)S(1)}, u32[]{:S(2)}, u32[]{:S(2)}) collective-permute-start(f32[16,256]{1,0:T(8,128)S(1)} %bitcast.299), channel_id=1, source_target_pairs={{7,0},{0,1},{1,2},{2,3},{3,4},{4,5},{5,6},{6,7},{15,8},{8,9},{9,10... | collective-permute-start | bytes 49160 | tf_op jit(solution)/shard_map/ppermute | solution.py:74
  42.8 0.7 copy-start.20
  43.8 0.7 copy-start.15
  44.8 3.8 %collective-permute-start.8 = (f32[4,4,64]{2,1,0:T(4,128)S(1)}, f32[4,4,64]{2,1,0:T(4,128)S(1)}, u32[]{:S(2)}, u32[]{:S(2)}) collective-permute-start(f32[4,4,64]{2,1,0:T(4,128)S(1)} %reshape.416), channel_id=1, source_target_pairs={{7,0},{0,1},{1,2},{2,3},{3,4},{4,5},{5,6},{6,7},{15,8},{8,9},{9,10... | collective-permute-start | bytes 12296 | tf_op jit(solution)/shard_map/ppermute | solution.py:74
  47.8 4.3 %collective-permute-start.9 = (f32[4,4,64]{2,1,0:T(4,128)S(1)}, f32[4,4,64]{2,1,0:T(4,128)S(1)}, u32[]{:S(2)}, u32[]{:S(2)}) collective-permute-start(f32[4,4,64]{2,1,0:T(4,128)S(1)} %reshape.416), channel_id=1, source_target_pairs={{1,0},{2,1},{3,2},{4,3},{5,4},{6,5},{7,6},{0,7},{9,8},{10,9},{11,1... | collective-permute-start | bytes 12296 | tf_op jit(solution)/shard_map/ppermute | solution.py:74
  54.1 13.7 %all-to-all-start = ((f32[32,3,4,3]{2,1,3,0:T(4,128)}), f32[32,3,4,3]{2,1,3,0:T(4,128)S(1)}, u32[]{:S(2)}, u32[]{:S(2)}) async-start(f32[32,3,4,3]{2,1,3,0:T(4,128)} %copy.117), calls=%async_computation | async-start | bytes 393216 | tf_op jit(solution)/shard_map/all_to_all | solution.py:227
  68.7 1.8 %copy-start.5 = (f32[2,8,8,8,8]{4,3,2,1,0:T(8,128)S(1)}, f32[2,8,8,8,8]{4,3,2,1,0:T(8,128)}, u32[]{:S(2)}) copy-start(f32[2,8,8,8,8]{4,3,2,1,0:T(8,128)} %concatenate.143) | copy-start | bytes 98308
  72.1 0.7 copy-start.7
  86.8 0.7 copy-start.21
  87.9 0.7 copy-start.14
  91.0 3.1 %collective-permute-start.10 = (f32[16,256]{1,0:T(8,128)S(1)}, f32[16,256]{1,0:T(8,128)S(1)}, u32[]{:S(2)}, u32[]{:S(2)}) collective-permute-start(f32[16,256]{1,0:T(8,128)S(1)} %get-tuple-element.29), channel_id=1, source_target_pairs={{8,0},{16,8},{24,16},{32,24},{40,32},{48,40},{56,48},{64,56},{72,6... | collective-permute-start | bytes 49160 | tf_op jit(solution)/shard_map/ppermute | solution.py:71
  91.9 5.9 %collective-permute-start.11 = (f32[16,256]{1,0:T(8,128)S(1)}, f32[16,256]{1,0:T(8,128)S(1)}, u32[]{:S(2)}, u32[]{:S(2)}) collective-permute-start(f32[16,256]{1,0:T(8,128)S(1)} %get-tuple-element.30), channel_id=1, source_target_pairs={{248,0},{0,8},{8,16},{16,24},{24,32},{32,40},{40,48},{48,56},{56,6... | collective-permute-start | bytes 49160 | tf_op jit(solution)/shard_map/ppermute | solution.py:71
  97.8 0.7 copy-start.10
  97.8 0.7 copy-start.12
  98.7 5.5 %collective-permute-start.12 = (f32[16,256]{1,0:T(8,128)S(1)}, f32[16,256]{1,0:T(8,128)S(1)}, u32[]{:S(2)}, u32[]{:S(2)}) collective-permute-start(f32[16,256]{1,0:T(8,128)S(1)} %bitcast.297), channel_id=1, source_target_pairs={{1,0},{2,1},{3,2},{4,3},{5,4},{6,5},{7,6},{0,7},{9,8},{10,9},{11,1... | collective-permute-start | bytes 49160 | tf_op jit(solution)/shard_map/ppermute | solution.py:74
  99.6 4.6 %collective-permute-start.13 = (f32[16,256]{1,0:T(8,128)S(1)}, f32[16,256]{1,0:T(8,128)S(1)}, u32[]{:S(2)}, u32[]{:S(2)}) collective-permute-start(f32[16,256]{1,0:T(8,128)S(1)} %bitcast.298), channel_id=1, source_target_pairs={{7,0},{0,1},{1,2},{2,3},{3,4},{4,5},{5,6},{6,7},{15,8},{8,9},{9,10... | collective-permute-start | bytes 49160 | tf_op jit(solution)/shard_map/ppermute | solution.py:74
  104.6 0.6 copy-start.17
  104.6 0.6 copy-start.19
  107.6 2.7 %collective-permute-start.14 = (f32[16,256]{1,0:T(8,128)S(1)}, f32[16,256]{1,0:T(8,128)S(1)}, u32[]{:S(2)}, u32[]{:S(2)}) collective-permute-start(f32[16,256]{1,0:T(8,128)S(1)} %get-tuple-element.21), channel_id=1, source_target_pairs={{8,0},{16,8},{24,16},{32,24},{40,32},{48,40},{56,48},{64,56},{72,6... | collective-permute-start | bytes 49160 | tf_op jit(solution)/shard_map/ppermute | solution.py:71
  107.7 6.0 %collective-permute-start.15 = (f32[16,256]{1,0:T(8,128)S(1)}, f32[16,256]{1,0:T(8,128)S(1)}, u32[]{:S(2)}, u32[]{:S(2)}) collective-permute-start(f32[16,256]{1,0:T(8,128)S(1)} %get-tuple-element.22), channel_id=1, source_target_pairs={{248,0},{0,8},{8,16},{16,24},{24,32},{32,40},{40,48},{48,56},{56,6... | collective-permute-start | bytes 49160 | tf_op jit(solution)/shard_map/ppermute | solution.py:71
  113.8 5.5 %collective-permute-start.16 = (f32[16,256]{1,0:T(8,128)S(1)}, f32[16,256]{1,0:T(8,128)S(1)}, u32[]{:S(2)}, u32[]{:S(2)}) collective-permute-start(f32[16,256]{1,0:T(8,128)S(1)} %bitcast.294), channel_id=1, source_target_pairs={{1,0},{2,1},{3,2},{4,3},{5,4},{6,5},{7,6},{0,7},{9,8},{10,9},{11,1... | collective-permute-start | bytes 49160 | tf_op jit(solution)/shard_map/ppermute | solution.py:74
  113.9 5.5 %collective-permute-start.17 = (f32[16,256]{1,0:T(8,128)S(1)}, f32[16,256]{1,0:T(8,128)S(1)}, u32[]{:S(2)}, u32[]{:S(2)}) collective-permute-start(f32[16,256]{1,0:T(8,128)S(1)} %bitcast.296), channel_id=1, source_target_pairs={{7,0},{0,1},{1,2},{2,3},{3,4},{4,5},{5,6},{6,7},{15,8},{8,9},{9,10... | collective-permute-start | bytes 49160 | tf_op jit(solution)/shard_map/ppermute | solution.py:74

commit v8 on v3

--- a/solution.py
+++ b/solution.py
@@ -248,8 +248,10 @@
     product = product.reshape(3, span)
     coarse_product = product[:2].reshape(1, 2, span)
 
-    pick = (2 * np.arange(nw)[:, None] + np.arange(3)[None, :]) % span
-    back = jnp.transpose(product[:, pick], (1, 0, 2))
+    back = jnp.stack(
+        [product[:, 0::2], product[:, 1::2], jnp.roll(product, -2, axis=1)[:, 0::2]], axis=-1
+    )
+    back = jnp.transpose(back, (1, 0, 2))
     got = lax.all_to_all(back, "wide", 0, 0, tiled=True)
     hx = jnp.stack([got[:, :, 0:2], got[:, :, 1:3]], axis=-1).reshape(nw, 3, 4)
     hy = jnp.stack([hx[:, 0:2], hx[:, 1:3]], axis=2).reshape(nw, 4, 4)

time: 122 us -> 121 us (level)
  local copies, waits for them, and re-layouts: 18.5 us -> 17 us
    unnamed x59 -> x55, local copies, waits for them, and re-layouts: 8.25 us -> 7.07 us
  transfers between devices with their start and end apart: 19 -> 19, of which waited for: 13 -> 14; matrix products, arithmetic and copies ran while one was open for 4% -> 4% of each run, Pallas kernels for 0% -> 0%
where the time goes in v8:
time: 121 us; the launch traced here: 120 us
  starting transfers between devices  38.8 us (32%)
  waiting for transfers between devices  31.5 us (26%)
  local copies, waits for them, and re-layouts  17 us (14%)
  blocking collectives  12.2 us (10%)
  matrix products  12.1 us (10%)
  other arithmetic  7.02 us (6%)
  between operations  1.64 us (1%)
    ppermute x10, starting transfers between devices, shift(): return lax.ppermute(value, 'deep', pairs)  18.5 us
    ppermute x8, starting transfers between devices, shift(): return lax.ppermute(value, 'wide', pairs)  16.2 us
    ppermute x8, waiting for transfers between devices, shift(): return lax.ppermute(value, 'wide', pairs)  14.6 us
    all_to_all x1, blocking collectives, local(): got = lax.all_to_all(back, 'wide', 0, 0, tiled=True)  12.2 us
    all_to_all x1, waiting for transfers between devices, local(): got = lax.all_to_all(sent, 'wide', 0, 0, tiled=True)  8.87 us
    ppermute x10, waiting for transfers between devices, shift(): return lax.ppermute(value, 'deep', pairs)  8.11 us
    unnamed x55, local copies, waits for them, and re-layouts  7.07 us
    all_to_all x1, starting transfers between devices, local(): got = lax.all_to_all(sent, 'wide', 0, 0, tiled=True)  4.04 us
  transfers between devices with their start and end apart: 19, of which 14 were waited for; matrix products, arithmetic and copies ran while one was open for 4% of the time, Pallas kernels for 0%

profile of v8, /device:TPU:7, one launch (start us, length us, event | category | flops | bytes accessed | tf_op | source)
XLA Modules:
  0.0 120.2 jit_solution(18170065240701994194)
XLA Ops:
  0.7 1.2 %fusion.83 = (f32[1,16,16,256]{3,2,1,0:T(8,128)S(1)}, f32[1,16,16,256]{3,2,1,0:T(8,128)S(1)}, f32[1,16,16,256]{3,2,1,0:T(8,128)S(1)}) fusion(f32[3,16,16,256]{3,2,1,0:T(8,128)} %param.20), kind=kLoop, calls=%fused_computation.231 | loop fusion | bytes 1572864 | tf_op jit(solution)/shard_map/slice | solution.py:191
  2.3 0.6 copy-done.4
  3.5 0.6 copy-done.2
  4.2 1.7 %collective-permute-start.1 = (f32[2,16,256]{2,1,0:T(8,128)S(1)}, f32[2,16,256]{2,1,0:T(8,128)S(1)}, u32[]{:S(2)}, u32[]{:S(2)}) collective-permute-start(f32[2,16,256]{2,1,0:T(8,128)S(1)} %get-tuple-element.14), channel_id=1, source_target_pairs={{248,0},{0,8},{8,16},{16,24},{24,32},{32,40},{40,48},{48,56},{56,6... | collective-permute-start | bytes 98312 | tf_op jit(solution)/shard_map/ppermute | solution.py:71
  5.9 6.5 %collective-permute-start = (f32[2,16,256]{2,1,0:T(8,128)S(1)}, f32[2,16,256]{2,1,0:T(8,128)S(1)}, u32[]{:S(2)}, u32[]{:S(2)}) collective-permute-start(f32[2,16,256]{2,1,0:T(8,128)S(1)} %get-tuple-element.13), channel_id=1, source_target_pairs={{8,0},{16,8},{24,16},{32,24},{40,32},{48,40},{56,48},{64,56},{72,6... | collective-permute-start | bytes 98312 | tf_op jit(solution)/shard_map/ppermute | solution.py:71
  12.4 0.7 copy-done.22
  13.9 1.5 %collective-permute-start.2 = (f32[12360]{0:T(1024)S(1)}, f32[12360]{0:T(1024)S(1)}, u32[]{:S(2)}, u32[]{:S(2)}) collective-permute-start(f32[12360]{0:T(1024)S(1)} %concatenate.136), channel_id=1, source_target_pairs={{1,0},{2,1},{3,2},{4,3},{5,4},{6,5},{7,6},{0,7},{9,8},{10,9},{11,1... | collective-permute-start | bytes 148328 | tf_op jit(solution)/shard_map/ppermute | solution.py:74
  15.5 1.4 %collective-permute-start.3 = (f32[2,16,256]{2,1,0:T(8,128)S(1)}, f32[2,16,256]{2,1,0:T(8,128)S(1)}, u32[]{:S(2)}, u32[]{:S(2)}) collective-permute-start(f32[2,16,256]{2,1,0:T(8,128)S(1)} %bitcast.285), channel_id=1, source_target_pairs={{7,0},{0,1},{1,2},{2,3},{3,4},{4,5},{5,6},{6,7},{15,8},{8,9},{9,10... | collective-permute-start | bytes 98312 | tf_op jit(solution)/shard_map/ppermute | solution.py:74
  16.9 1.1 concatenate.147
  19.8 0.9 copy-done
  21.4 0.6 copy-done.1
  23.4 5.0 %collective-permute-start.4 = (f32[16,256]{1,0:T(8,128)S(1)}, f32[16,256]{1,0:T(8,128)S(1)}, u32[]{:S(2)}, u32[]{:S(2)}) collective-permute-start(f32[16,256]{1,0:T(8,128)S(1)} %get-tuple-element.37), channel_id=1, source_target_pairs={{8,0},{16,8},{24,16},{32,24},{40,32},{48,40},{56,48},{64,56},{72,6... | collective-permute-start | bytes 49160 | tf_op jit(solution)/shard_map/ppermute | solution.py:71
  28.5 0.7 fusion.73
  29.2 0.7 compare_and_fusion
  29.8 4.4 %collective-permute-done.5 = f32[16,256]{1,0:T(8,128)S(1)} collective-permute-done((f32[16,256]{1,0:T(8,128)S(1)}, f32[16,256]{1,0:T(8,128)S(1)}, u32[]{:S(2)}, u32[]{:S(2)}) %collective-permute-start.5) | collective-permute-done | bytes 16416 | tf_op jit(solution)/shard_map/ppermute | solution.py:71
  34.4 1.9 %collective-permute-start.6 = (f32[16,256]{1,0:T(8,128)S(1)}, f32[16,256]{1,0:T(8,128)S(1)}, u32[]{:S(2)}, u32[]{:S(2)}) collective-permute-start(f32[16,256]{1,0:T(8,128)S(1)} %bitcast.294), channel_id=1, source_target_pairs={{1,0},{2,1},{3,2},{4,3},{5,4},{6,5},{7,6},{0,7},{9,8},{10,9},{11,1... | collective-permute-start | bytes 49160 | tf_op jit(solution)/shard_map/ppermute | solution.py:74
  36.3 2.4 %collective-permute-start.7 = (f32[16,256]{1,0:T(8,128)S(1)}, f32[16,256]{1,0:T(8,128)S(1)}, u32[]{:S(2)}, u32[]{:S(2)}) collective-permute-start(f32[16,256]{1,0:T(8,128)S(1)} %bitcast.300), channel_id=1, source_target_pairs={{7,0},{0,1},{1,2},{2,3},{3,4},{4,5},{5,6},{6,7},{15,8},{8,9},{9,10... | collective-permute-start | bytes 49160 | tf_op jit(solution)/shard_map/ppermute | solution.py:74
  38.8 0.8 collective-permute-done.7
  42.9 0.6 copy-done.19
  44.1 0.5 copy-done.14
  44.9 3.0 %collective-permute-start.8 = (f32[4,4,64]{2,1,0:T(4,128)S(1)}, f32[4,4,64]{2,1,0:T(4,128)S(1)}, u32[]{:S(2)}, u32[]{:S(2)}) collective-permute-start(f32[4,4,64]{2,1,0:T(4,128)S(1)} %reshape.416), channel_id=1, source_target_pairs={{7,0},{0,1},{1,2},{2,3},{3,4},{4,5},{5,6},{6,7},{15,8},{8,9},{9,10... | collective-permute-start | bytes 12296 | tf_op jit(solution)/shard_map/ppermute | solution.py:74
  48.0 0.8 collective-permute-done.8
  48.7 3.5 %collective-permute-done.9 = f32[4,4,64]{2,1,0:T(4,128)S(1)} collective-permute-done((f32[4,4,64]{2,1,0:T(4,128)S(1)}, f32[4,4,64]{2,1,0:T(4,128)S(1)}, u32[]{:S(2)}, u32[]{:S(2)}) %collective-permute-start.9) | collective-permute-done | bytes 4128 | tf_op jit(solution)/shard_map/ppermute | solution.py:74
  53.4 0.8 copy.106
  54.2 4.0 %all-to-all-start = ((f32[32,3,4,3]{2,1,3,0:T(4,128)}), f32[32,3,4,3]{2,1,3,0:T(4,128)S(1)}, u32[]{:S(2)}, u32[]{:S(2)}) async-start(f32[32,3,4,3]{2,1,3,0:T(4,128)} %copy.106), calls=%async_computation | async-start | bytes 393216 | tf_op jit(solution)/shard_map/all_to_all | solution.py:227
  58.3 0.6 pad_clamp_fusion
  59.0 8.9 %all-to-all-done = f32[32,3,4,3]{2,1,3,0:T(4,128)S(1)} async-done(((f32[32,3,4,3]{2,1,3,0:T(4,128)}), f32[32,3,4,3]{2,1,3,0:T(4,128)S(1)}, u32[]{:S(2)}, u32[]{:S(2)}) %all-to-all-start) | async-done | bytes 4640 | tf_op jit(solution)/shard_map/all_to_all | solution.py:227
  68.8 1.0 gather_fusion
  69.8 0.8 select_multiply_fusion
  70.6 1.7 %fusion.1 = f32[3,8,1,8,1]{3,2,4,1,0:T(1,128)S(1)} fusion(f32[3,8,8,8,1]{3,4,2,1,0:T(1,128)S(1)} %bitcast.274, f32[1,8,8,8,8]{4,3,2,1,0:T(8,128)S(1)} %concatenate.148, f32[2,8,8,8,8]{4,3,2,1,0:T(8,128)S(1)} %copy-done.5), kind=kOutput, calls=%fused_computation.32 | convolution fusion | flops 159744 | bytes 56064 | tf_op jit(solution)/shard_map/yxkij,yxkj,yxk->yxi/dot_general | solution.py:247
  73.0 12.2 %all_to_all.10 = f32[32,3,3]{1,2,0:T(4,128)S(1)} all-to-all(f32[32,3,3]{1,2,0:T(4,128)S(1)} %copy.112), channel_id=1, replica_groups=mesh['wide'=32,'deep'=8] {'wide'}, dimensions={0} | all-to-all | bytes 2304 | tf_op jit(solution)/shard_map/all_to_all | solution.py:255
  86.1 0.6 copy-done.20
  90.4 0.9 collective-permute-start.10
  91.3 0.7 collective-permute-start.11
  92.0 1.5 %collective-permute-done.10 = f32[16,256]{1,0:T(8,128)S(1)} collective-permute-done((f32[16,256]{1,0:T(8,128)S(1)}, f32[16,256]{1,0:T(8,128)S(1)}, u32[]{:S(2)}, u32[]{:S(2)}) %collective-permute-start.10) | collective-permute-done | bytes 16416 | tf_op jit(solution)/shard_map/ppermute | solution.py:71
  93.5 3.7 %collective-permute-done.11 = f32[16,256]{1,0:T(8,128)S(1)} collective-permute-done((f32[16,256]{1,0:T(8,128)S(1)}, f32[16,256]{1,0:T(8,128)S(1)}, u32[]{:S(2)}, u32[]{:S(2)}) %collective-permute-start.11) | collective-permute-done | bytes 16416 | tf_op jit(solution)/shard_map/ppermute | solution.py:71
  97.2 0.7 copy-done.9
  98.1 1.0 collective-permute-start.12
  99.0 3.2 %collective-permute-start.13 = (f32[16,256]{1,0:T(8,128)S(1)}, f32[16,256]{1,0:T(8,128)S(1)}, u32[]{:S(2)}, u32[]{:S(2)}) collective-permute-start(f32[16,256]{1,0:T(8,128)S(1)} %bitcast.299), channel_id=1, source_target_pairs={{7,0},{0,1},{1,2},{2,3},{3,4},{4,5},{5,6},{6,7},{15,8},{8,9},{9,10... | collective-permute-start | bytes 49160 | tf_op jit(solution)/shard_map/ppermute | solution.py:74
  102.2 1.4 %collective-permute-done.12 = f32[16,256]{1,0:T(8,128)S(1)} collective-permute-done((f32[16,256]{1,0:T(8,128)S(1)}, f32[16,256]{1,0:T(8,128)S(1)}, u32[]{:S(2)}, u32[]{:S(2)}) %collective-permute-start.12) | collective-permute-done | bytes 16416 | tf_op jit(solution)/shard_map/ppermute | solution.py:74
  104.0 0.6 copy-done.16
  107.1 1.5 %collective-permute-start.15 = (f32[16,256]{1,0:T(8,128)S(1)}, f32[16,256]{1,0:T(8,128)S(1)}, u32[]{:S(2)}, u32[]{:S(2)}) collective-permute-start(f32[16,256]{1,0:T(8,128)S(1)} %get-tuple-element.22), channel_id=1, source_target_pairs={{248,0},{0,8},{8,16},{16,24},{24,32},{32,40},{40,48},{48,56},{56,6... | collective-permute-start | bytes 49160 | tf_op jit(solution)/shard_map/ppermute | solution.py:71
  108.6 1.1 collective-permute-done.14
  109.7 3.4 %collective-permute-done.15 = f32[16,256]{1,0:T(8,128)S(1)} collective-permute-done((f32[16,256]{1,0:T(8,128)S(1)}, f32[16,256]{1,0:T(8,128)S(1)}, u32[]{:S(2)}, u32[]{:S(2)}) %collective-permute-start.15) | collective-permute-done | bytes 16416 | tf_op jit(solution)/shard_map/ppermute | solution.py:71
  113.3 4.1 %collective-permute-start.17 = (f32[16,256]{1,0:T(8,128)S(1)}, f32[16,256]{1,0:T(8,128)S(1)}, u32[]{:S(2)}, u32[]{:S(2)}) collective-permute-start(f32[16,256]{1,0:T(8,128)S(1)} %bitcast.297), channel_id=1, source_target_pairs={{7,0},{0,1},{1,2},{2,3},{3,4},{4,5},{5,6},{6,7},{15,8},{8,9},{9,10... | collective-permute-start | bytes 49160 | tf_op jit(solution)/shard_map/ppermute | solution.py:74
  117.4 0.6 reshape.426
  118.1 0.7 collective-permute-done.16
  119.2 1.0 fusion.51
  (208 shorter events, 21.0 us)
Async XLA Ops:
  0.6 1.2 %copy-start.6 = (f32[256,256]{1,0:T(8,128)S(1)}, f32[256,256]{1,0:T(8,128)}, u32[]{:S(2)}) copy-start(f32[256,256]{1,0:T(8,128)} %constant.204.clone) | copy-start | bytes 786436
  0.6 1.3 %copy-start.3 = (f32[16,16,256]{2,1,0:T(8,128)S(1)}, f32[16,16,256]{2,1,0:T(8,128)}, u32[]{:S(2)}) copy-start(f32[16,16,256]{2,1,0:T(8,128)} %param.21) | copy-start | bytes 786436
  1.9 0.9 copy-start.4
  3.2 1.0 copy-start.2
  4.2 8.2 %copy-start.7 = (f32[1,2,8,512]{3,2,1,0:T(8,128)S(1)}, f32[1,2,8,512]{3,2,1,0:T(8,128)}, u32[]{:S(2)}) copy-start(f32[1,2,8,512]{3,2,1,0:T(8,128)} %param.24) | copy-start | bytes 98308
  4.2 9.4 %collective-permute-start.1 = (f32[2,16,256]{2,1,0:T(8,128)S(1)}, f32[2,16,256]{2,1,0:T(8,128)S(1)}, u32[]{:S(2)}, u32[]{:S(2)}) collective-permute-start(f32[2,16,256]{2,1,0:T(8,128)S(1)} %get-tuple-element.14), channel_id=1, source_target_pairs={{248,0},{0,8},{8,16},{16,24},{24,32},{32,40},{40,48},{48,56},{56,6... | collective-permute-start | bytes 98312 | tf_op jit(solution)/shard_map/ppermute | solution.py:71
  5.9 6.5 %copy-start.12 = (s32[1,2,8,8]{3,2,1,0:T(8,128)S(1)}, s32[1,2,8,8]{3,2,1,0:T(8,128)}, u32[]{:S(2)}) copy-start(s32[1,2,8,8]{3,2,1,0:T(8,128)} %param.22) | copy-start | bytes 1540
  5.9 7.7 %collective-permute-start = (f32[2,16,256]{2,1,0:T(8,128)S(1)}, f32[2,16,256]{2,1,0:T(8,128)S(1)}, u32[]{:S(2)}, u32[]{:S(2)}) collective-permute-start(f32[2,16,256]{2,1,0:T(8,128)S(1)} %get-tuple-element.13), channel_id=1, source_target_pairs={{8,0},{16,8},{24,16},{32,24},{40,32},{48,40},{56,48},{64,56},{72,6... | collective-permute-start | bytes 98312 | tf_op jit(solution)/shard_map/ppermute | solution.py:71
  12.4 0.7 copy-start.22
  13.1 27.3 %copy-start.8 = (pred[16]{0:T(512)(128)(4,1)}, pred[16]{0:T(512)(128)(4,1)S(1)}, u32[]{:S(2)}) copy-start(pred[16]{0:T(512)(128)(4,1)S(1)} %get-tuple-element.49) | copy-start | bytes 52
  13.1 27.3 %copy-start.10 = (pred[16]{0:T(512)(128)(4,1)}, pred[16]{0:T(512)(128)(4,1)S(1)}, u32[]{:S(2)}) copy-start(pred[16]{0:T(512)(128)(4,1)S(1)} %get-tuple-element.50) | copy-start | bytes 52
  13.9 4.8 %collective-permute-start.2 = (f32[12360]{0:T(1024)S(1)}, f32[12360]{0:T(1024)S(1)}, u32[]{:S(2)}, u32[]{:S(2)}) collective-permute-start(f32[12360]{0:T(1024)S(1)} %concatenate.136), channel_id=1, source_target_pairs={{1,0},{2,1},{3,2},{4,3},{5,4},{6,5},{7,6},{0,7},{9,8},{10,9},{11,1... | collective-permute-start | bytes 148328 | tf_op jit(solution)/shard_map/ppermute | solution.py:74
  15.5 2.7 %collective-permute-start.3 = (f32[2,16,256]{2,1,0:T(8,128)S(1)}, f32[2,16,256]{2,1,0:T(8,128)S(1)}, u32[]{:S(2)}, u32[]{:S(2)}) collective-permute-start(f32[2,16,256]{2,1,0:T(8,128)S(1)} %bitcast.285), channel_id=1, source_target_pairs={{7,0},{0,1},{1,2},{2,3},{3,4},{4,5},{5,6},{6,7},{15,8},{8,9},{9,10... | collective-permute-start | bytes 98312 | tf_op jit(solution)/shard_map/ppermute | solution.py:74
  16.9 23.6 %copy-start.15 = (pred[256]{0:T(512)(128)(4,1)}, pred[256]{0:T(512)(128)(4,1)S(1)}, u32[]{:S(2)}) copy-start(pred[256]{0:T(512)(128)(4,1)S(1)} %get-tuple-element.51) | copy-start | bytes 772
  16.9 23.6 %copy-start.17 = (pred[256]{0:T(512)(128)(4,1)}, pred[256]{0:T(512)(128)(4,1)S(1)}, u32[]{:S(2)}) copy-start(pred[256]{0:T(512)(128)(4,1)S(1)} %get-tuple-element.52) | copy-start | bytes 772
  16.9 1.1 copy-start.21
  19.8 1.0 copy-start
  21.0 1.0 copy-start.1
  23.4 6.5 %collective-permute-start.4 = (f32[16,256]{1,0:T(8,128)S(1)}, f32[16,256]{1,0:T(8,128)S(1)}, u32[]{:S(2)}, u32[]{:S(2)}) collective-permute-start(f32[16,256]{1,0:T(8,128)S(1)} %get-tuple-element.37), channel_id=1, source_target_pairs={{8,0},{16,8},{24,16},{32,24},{40,32},{48,40},{56,48},{64,56},{72,6... | collective-permute-start | bytes 49160 | tf_op jit(solution)/shard_map/ppermute | solution.py:71
  28.3 5.9 %collective-permute-start.5 = (f32[16,256]{1,0:T(8,128)S(1)}, f32[16,256]{1,0:T(8,128)S(1)}, u32[]{:S(2)}, u32[]{:S(2)}) collective-permute-start(f32[16,256]{1,0:T(8,128)S(1)} %get-tuple-element.38), channel_id=1, source_target_pairs={{248,0},{0,8},{8,16},{16,24},{24,32},{32,40},{40,48},{48,56},{56,6... | collective-permute-start | bytes 49160 | tf_op jit(solution)/shard_map/ppermute | solution.py:71
  34.4 5.7 %collective-permute-start.6 = (f32[16,256]{1,0:T(8,128)S(1)}, f32[16,256]{1,0:T(8,128)S(1)}, u32[]{:S(2)}, u32[]{:S(2)}) collective-permute-start(f32[16,256]{1,0:T(8,128)S(1)} %bitcast.294), channel_id=1, source_target_pairs={{1,0},{2,1},{3,2},{4,3},{5,4},{6,5},{7,6},{0,7},{9,8},{10,9},{11,1... | collective-permute-start | bytes 49160 | tf_op jit(solution)/shard_map/ppermute | solution.py:74
  36.3 3.2 %collective-permute-start.7 = (f32[16,256]{1,0:T(8,128)S(1)}, f32[16,256]{1,0:T(8,128)S(1)}, u32[]{:S(2)}, u32[]{:S(2)}) collective-permute-start(f32[16,256]{1,0:T(8,128)S(1)} %bitcast.300), channel_id=1, source_target_pairs={{7,0},{0,1},{1,2},{2,3},{3,4},{4,5},{5,6},{6,7},{15,8},{8,9},{9,10... | collective-permute-start | bytes 49160 | tf_op jit(solution)/shard_map/ppermute | solution.py:74
  42.8 0.7 copy-start.19
  43.9 0.7 copy-start.14
  44.9 3.8 %collective-permute-start.8 = (f32[4,4,64]{2,1,0:T(4,128)S(1)}, f32[4,4,64]{2,1,0:T(4,128)S(1)}, u32[]{:S(2)}, u32[]{:S(2)}) collective-permute-start(f32[4,4,64]{2,1,0:T(4,128)S(1)} %reshape.416), channel_id=1, source_target_pairs={{7,0},{0,1},{1,2},{2,3},{3,4},{4,5},{5,6},{6,7},{15,8},{8,9},{9,10... | collective-permute-start | bytes 12296 | tf_op jit(solution)/shard_map/ppermute | solution.py:74
  47.9 4.3 %collective-permute-start.9 = (f32[4,4,64]{2,1,0:T(4,128)S(1)}, f32[4,4,64]{2,1,0:T(4,128)S(1)}, u32[]{:S(2)}, u32[]{:S(2)}) collective-permute-start(f32[4,4,64]{2,1,0:T(4,128)S(1)} %reshape.416), channel_id=1, source_target_pairs={{1,0},{2,1},{3,2},{4,3},{5,4},{6,5},{7,6},{0,7},{9,8},{10,9},{11,1... | collective-permute-start | bytes 12296 | tf_op jit(solution)/shard_map/ppermute | solution.py:74
  54.2 13.7 %all-to-all-start = ((f32[32,3,4,3]{2,1,3,0:T(4,128)}), f32[32,3,4,3]{2,1,3,0:T(4,128)S(1)}, u32[]{:S(2)}, u32[]{:S(2)}) async-start(f32[32,3,4,3]{2,1,3,0:T(4,128)} %copy.106), calls=%async_computation | async-start | bytes 393216 | tf_op jit(solution)/shard_map/all_to_all | solution.py:227
  68.8 1.8 %copy-start.5 = (f32[2,8,8,8,8]{4,3,2,1,0:T(8,128)S(1)}, f32[2,8,8,8,8]{4,3,2,1,0:T(8,128)}, u32[]{:S(2)}) copy-start(f32[2,8,8,8,8]{4,3,2,1,0:T(8,128)} %concatenate.147) | copy-start | bytes 98308
  86.0 0.7 copy-start.20
  87.2 0.7 copy-start.13
  90.4 3.1 %collective-permute-start.10 = (f32[16,256]{1,0:T(8,128)S(1)}, f32[16,256]{1,0:T(8,128)S(1)}, u32[]{:S(2)}, u32[]{:S(2)}) collective-permute-start(f32[16,256]{1,0:T(8,128)S(1)} %get-tuple-element.29), channel_id=1, source_target_pairs={{8,0},{16,8},{24,16},{32,24},{40,32},{48,40},{56,48},{64,56},{72,6... | collective-permute-start | bytes 49160 | tf_op jit(solution)/shard_map/ppermute | solution.py:71
  91.3 5.9 %collective-permute-start.11 = (f32[16,256]{1,0:T(8,128)S(1)}, f32[16,256]{1,0:T(8,128)S(1)}, u32[]{:S(2)}, u32[]{:S(2)}) collective-permute-start(f32[16,256]{1,0:T(8,128)S(1)} %get-tuple-element.30), channel_id=1, source_target_pairs={{248,0},{0,8},{8,16},{16,24},{24,32},{32,40},{40,48},{48,56},{56,6... | collective-permute-start | bytes 49160 | tf_op jit(solution)/shard_map/ppermute | solution.py:71
  97.2 0.7 copy-start.9
  97.2 0.7 copy-start.11
  98.1 5.5 %collective-permute-start.12 = (f32[16,256]{1,0:T(8,128)S(1)}, f32[16,256]{1,0:T(8,128)S(1)}, u32[]{:S(2)}, u32[]{:S(2)}) collective-permute-start(f32[16,256]{1,0:T(8,128)S(1)} %bitcast.298), channel_id=1, source_target_pairs={{1,0},{2,1},{3,2},{4,3},{5,4},{6,5},{7,6},{0,7},{9,8},{10,9},{11,1... | collective-permute-start | bytes 49160 | tf_op jit(solution)/shard_map/ppermute | solution.py:74
  99.0 4.6 %collective-permute-start.13 = (f32[16,256]{1,0:T(8,128)S(1)}, f32[16,256]{1,0:T(8,128)S(1)}, u32[]{:S(2)}, u32[]{:S(2)}) collective-permute-start(f32[16,256]{1,0:T(8,128)S(1)} %bitcast.299), channel_id=1, source_target_pairs={{7,0},{0,1},{1,2},{2,3},{3,4},{4,5},{5,6},{6,7},{15,8},{8,9},{9,10... | collective-permute-start | bytes 49160 | tf_op jit(solution)/shard_map/ppermute | solution.py:74
  104.0 0.6 copy-start.16
  104.0 0.7 copy-start.18
  107.0 2.7 %collective-permute-start.14 = (f32[16,256]{1,0:T(8,128)S(1)}, f32[16,256]{1,0:T(8,128)S(1)}, u32[]{:S(2)}, u32[]{:S(2)}) collective-permute-start(f32[16,256]{1,0:T(8,128)S(1)} %get-tuple-element.21), channel_id=1, source_target_pairs={{8,0},{16,8},{24,16},{32,24},{40,32},{48,40},{56,48},{64,56},{72,6... | collective-permute-start | bytes 49160 | tf_op jit(solution)/shard_map/ppermute | solution.py:71
  107.1 6.0 %collective-permute-start.15 = (f32[16,256]{1,0:T(8,128)S(1)}, f32[16,256]{1,0:T(8,128)S(1)}, u32[]{:S(2)}, u32[]{:S(2)}) collective-permute-start(f32[16,256]{1,0:T(8,128)S(1)} %get-tuple-element.22), channel_id=1, source_target_pairs={{248,0},{0,8},{8,16},{16,24},{24,32},{32,40},{40,48},{48,56},{56,6... | collective-permute-start | bytes 49160 | tf_op jit(solution)/shard_map/ppermute | solution.py:71
  113.3 5.5 %collective-permute-start.16 = (f32[16,256]{1,0:T(8,128)S(1)}, f32[16,256]{1,0:T(8,128)S(1)}, u32[]{:S(2)}, u32[]{:S(2)}) collective-permute-start(f32[16,256]{1,0:T(8,128)S(1)} %bitcast.295), channel_id=1, source_target_pairs={{1,0},{2,1},{3,2},{4,3},{5,4},{6,5},{7,6},{0,7},{9,8},{10,9},{11,1... | collective-permute-start | bytes 49160 | tf_op jit(solution)/shard_map/ppermute | solution.py:74
  113.3 5.5 %collective-permute-start.17 = (f32[16,256]{1,0:T(8,128)S(1)}, f32[16,256]{1,0:T(8,128)S(1)}, u32[]{:S(2)}, u32[]{:S(2)}) collective-permute-start(f32[16,256]{1,0:T(8,128)S(1)} %bitcast.297), channel_id=1, source_target_pairs={{7,0},{0,1},{1,2},{2,3},{3,4},{4,5},{5,6},{6,7},{15,8},{8,9},{9,10... | collective-permute-start | bytes 49160 | tf_op jit(solution)/shard_map/ppermute | solution.py:74

commit v9 on v8

--- a/solution.py
+++ b/solution.py
@@ -239,7 +239,7 @@
     layer = cols // (2 * nxb)
     block = cols % (2 * nxb)
     index = (layer * 4 + y_off + block // nxb) * nxb + block % nxb
-    picked = jnp.take(frame_rows, index.reshape(-1), axis=0).reshape(index.shape + (BS,))
+    picked = jnp.take(frame_rows, index.reshape(-1), axis=0, mode="clip").reshape(index.shape + (BS,))
     live = (jnp.arange(K, dtype=jnp.int32)[None, None, :] < lives[:, :, None]).astype(
         jnp.float32
     )

time: 121 us -> 121 us (level)
  transfers between devices with their start and end apart: 19 -> 19, of which waited for: 14 -> 14; matrix products, arithmetic and copies ran while one was open for 4% -> 3% of each run, Pallas kernels for 0% -> 0%
where the time goes in v9:
time: 121 us; the launch traced here: 120 us
  starting transfers between devices  38.8 us (32%)
  waiting for transfers between devices  32.2 us (27%)
  local copies, waits for them, and re-layouts  17 us (14%)
  blocking collectives  12.2 us (10%)
  matrix products  12.1 us (10%)
  other arithmetic  6.28 us (5%)
  between operations  1.65 us (1%)
    ppermute x10, starting transfers between devices, shift(): return lax.ppermute(value, 'deep', pairs)  18.5 us
    ppermute x8, starting transfers between devices, shift(): return lax.ppermute(value, 'wide', pairs)  16.2 us
    ppermute x8, waiting for transfers between devices, shift(): return lax.ppermute(value, 'wide', pairs)  15.3 us
    all_to_all x1, blocking collectives, local(): got = lax.all_to_all(back, 'wide', 0, 0, tiled=True)  12.2 us
    all_to_all x1, waiting for transfers between devices, local(): got = lax.all_to_all(sent, 'wide', 0, 0, tiled=True)  8.87 us
    ppermute x10, waiting for transfers between devices, shift(): return lax.ppermute(value, 'deep', pairs)  8.11 us
    unnamed x55, local copies, waits for them, and re-layouts  7.04 us
    all_to_all x1, starting transfers between devices, local(): got = lax.all_to_all(sent, 'wide', 0, 0, tiled=True)  4.05 us
  transfers between devices with their start and end apart: 19, of which 14 were waited for; matrix products, arithmetic and copies ran while one was open for 3% of the time, Pallas kernels for 0%

profile of v9, /device:TPU:7, one launch (start us, length us, event | category | flops | bytes accessed | tf_op | source)
XLA Modules:
  0.0 120.2 jit_solution(14172106385230754280)
XLA Ops:
  0.7 1.2 %fusion.72 = (f32[1,16,16,256]{3,2,1,0:T(8,128)S(1)}, f32[1,16,16,256]{3,2,1,0:T(8,128)S(1)}, f32[1,16,16,256]{3,2,1,0:T(8,128)S(1)}) fusion(f32[3,16,16,256]{3,2,1,0:T(8,128)} %param.20), kind=kLoop, calls=%fused_computation.205 | loop fusion | bytes 1572864 | tf_op jit(solution)/shard_map/slice | solution.py:191
  2.3 0.6 copy-done.4
  3.5 0.6 copy-done.2
  4.2 1.7 %collective-permute-start.1 = (f32[2,16,256]{2,1,0:T(8,128)S(1)}, f32[2,16,256]{2,1,0:T(8,128)S(1)}, u32[]{:S(2)}, u32[]{:S(2)}) collective-permute-start(f32[2,16,256]{2,1,0:T(8,128)S(1)} %get-tuple-element.14), channel_id=1, source_target_pairs={{248,0},{0,8},{8,16},{16,24},{24,32},{32,40},{40,48},{48,56},{56,6... | collective-permute-start | bytes 98312 | tf_op jit(solution)/shard_map/ppermute | solution.py:71
  5.9 6.5 %collective-permute-start = (f32[2,16,256]{2,1,0:T(8,128)S(1)}, f32[2,16,256]{2,1,0:T(8,128)S(1)}, u32[]{:S(2)}, u32[]{:S(2)}) collective-permute-start(f32[2,16,256]{2,1,0:T(8,128)S(1)} %get-tuple-element.13), channel_id=1, source_target_pairs={{8,0},{16,8},{24,16},{32,24},{40,32},{48,40},{56,48},{64,56},{72,6... | collective-permute-start | bytes 98312 | tf_op jit(solution)/shard_map/ppermute | solution.py:71
  12.4 0.7 copy-done.21
  13.9 1.5 %collective-permute-start.2 = (f32[12360]{0:T(1024)S(1)}, f32[12360]{0:T(1024)S(1)}, u32[]{:S(2)}, u32[]{:S(2)}) collective-permute-start(f32[12360]{0:T(1024)S(1)} %concatenate.136), channel_id=1, source_target_pairs={{1,0},{2,1},{3,2},{4,3},{5,4},{6,5},{7,6},{0,7},{9,8},{10,9},{11,1... | collective-permute-start | bytes 148328 | tf_op jit(solution)/shard_map/ppermute | solution.py:74
  15.5 1.4 %collective-permute-start.3 = (f32[2,16,256]{2,1,0:T(8,128)S(1)}, f32[2,16,256]{2,1,0:T(8,128)S(1)}, u32[]{:S(2)}, u32[]{:S(2)}) collective-permute-start(f32[2,16,256]{2,1,0:T(8,128)S(1)} %bitcast.283), channel_id=1, source_target_pairs={{7,0},{0,1},{1,2},{2,3},{3,4},{4,5},{5,6},{6,7},{15,8},{8,9},{9,10... | collective-permute-start | bytes 98312 | tf_op jit(solution)/shard_map/ppermute | solution.py:74
  16.9 1.1 concatenate.147
  19.8 0.9 copy-done
  21.3 0.6 copy-done.1
  23.3 5.0 %collective-permute-start.4 = (f32[16,256]{1,0:T(8,128)S(1)}, f32[16,256]{1,0:T(8,128)S(1)}, u32[]{:S(2)}, u32[]{:S(2)}) collective-permute-start(f32[16,256]{1,0:T(8,128)S(1)} %get-tuple-element.37), channel_id=1, source_target_pairs={{8,0},{16,8},{24,16},{32,24},{40,32},{48,40},{56,48},{64,56},{72,6... | collective-permute-start | bytes 49160 | tf_op jit(solution)/shard_map/ppermute | solution.py:71
  28.4 0.7 fusion.63
  29.2 5.0 %collective-permute-done.5 = f32[16,256]{1,0:T(8,128)S(1)} collective-permute-done((f32[16,256]{1,0:T(8,128)S(1)}, f32[16,256]{1,0:T(8,128)S(1)}, u32[]{:S(2)}, u32[]{:S(2)}) %collective-permute-start.5) | collective-permute-done | bytes 16416 | tf_op jit(solution)/shard_map/ppermute | solution.py:71
  34.4 1.9 %collective-permute-start.6 = (f32[16,256]{1,0:T(8,128)S(1)}, f32[16,256]{1,0:T(8,128)S(1)}, u32[]{:S(2)}, u32[]{:S(2)}) collective-permute-start(f32[16,256]{1,0:T(8,128)S(1)} %bitcast.293), channel_id=1, source_target_pairs={{1,0},{2,1},{3,2},{4,3},{5,4},{6,5},{7,6},{0,7},{9,8},{10,9},{11,1... | collective-permute-start | bytes 49160 | tf_op jit(solution)/shard_map/ppermute | solution.py:74
  36.3 2.4 %collective-permute-start.7 = (f32[16,256]{1,0:T(8,128)S(1)}, f32[16,256]{1,0:T(8,128)S(1)}, u32[]{:S(2)}, u32[]{:S(2)}) collective-permute-start(f32[16,256]{1,0:T(8,128)S(1)} %bitcast.299), channel_id=1, source_target_pairs={{7,0},{0,1},{1,2},{2,3},{3,4},{4,5},{5,6},{6,7},{15,8},{8,9},{9,10... | collective-permute-start | bytes 49160 | tf_op jit(solution)/shard_map/ppermute | solution.py:74
  38.7 0.8 collective-permute-done.7
  42.8 0.6 copy-done.19
  44.1 0.5 copy-done.14
  44.9 3.0 %collective-permute-start.8 = (f32[4,4,64]{2,1,0:T(4,128)S(1)}, f32[4,4,64]{2,1,0:T(4,128)S(1)}, u32[]{:S(2)}, u32[]{:S(2)}) collective-permute-start(f32[4,4,64]{2,1,0:T(4,128)S(1)} %reshape.397), channel_id=1, source_target_pairs={{7,0},{0,1},{1,2},{2,3},{3,4},{4,5},{5,6},{6,7},{15,8},{8,9},{9,10... | collective-permute-start | bytes 12296 | tf_op jit(solution)/shard_map/ppermute | solution.py:74
  47.9 0.8 collective-permute-done.8
  48.7 3.5 %collective-permute-done.9 = f32[4,4,64]{2,1,0:T(4,128)S(1)} collective-permute-done((f32[4,4,64]{2,1,0:T(4,128)S(1)}, f32[4,4,64]{2,1,0:T(4,128)S(1)}, u32[]{:S(2)}, u32[]{:S(2)}) %collective-permute-start.9) | collective-permute-done | bytes 4128 | tf_op jit(solution)/shard_map/ppermute | solution.py:74
  53.3 0.8 copy.106
  54.2 4.0 %all-to-all-start = ((f32[32,3,4,3]{2,1,3,0:T(4,128)}), f32[32,3,4,3]{2,1,3,0:T(4,128)S(1)}, u32[]{:S(2)}, u32[]{:S(2)}) async-start(f32[32,3,4,3]{2,1,3,0:T(4,128)} %copy.106), calls=%async_computation | async-start | bytes 393216 | tf_op jit(solution)/shard_map/all_to_all | solution.py:227
  58.2 0.6 pad_clamp_fusion
  59.0 8.9 %all-to-all-done = f32[32,3,4,3]{2,1,3,0:T(4,128)S(1)} async-done(((f32[32,3,4,3]{2,1,3,0:T(4,128)}), f32[32,3,4,3]{2,1,3,0:T(4,128)S(1)}, u32[]{:S(2)}, u32[]{:S(2)}) %all-to-all-start) | async-done | bytes 4640 | tf_op jit(solution)/shard_map/all_to_all | solution.py:227
  68.8 1.0 gather_fusion
  69.7 0.8 broadcast_multiply_fusion
  70.5 1.7 %fusion.1 = f32[3,8,1,8,1]{3,2,4,1,0:T(1,128)S(1)} fusion(f32[3,8,8,8,1]{3,4,2,1,0:T(1,128)S(1)} %bitcast.274, f32[1,8,8,8,8]{4,3,2,1,0:T(8,128)S(1)} %concatenate.148, f32[2,8,8,8,8]{4,3,2,1,0:T(8,128)S(1)} %copy-done.5), kind=kOutput, calls=%fused_computation.32 | convolution fusion | flops 159744 | bytes 56064 | tf_op jit(solution)/shard_map/yxkij,yxkj,yxk->yxi/dot_general | solution.py:247
  72.9 12.2 %all_to_all.10 = f32[32,3,3]{1,2,0:T(4,128)S(1)} all-to-all(f32[32,3,3]{1,2,0:T(4,128)S(1)} %copy.112), channel_id=1, replica_groups=mesh['wide'=32,'deep'=8] {'wide'}, dimensions={0} | all-to-all | bytes 2304 | tf_op jit(solution)/shard_map/all_to_all | solution.py:255
  86.0 0.6 copy-done.20
  87.4 0.5 copy-done.13
  90.4 0.9 collective-permute-start.10
  91.3 0.7 collective-permute-start.11
  91.9 1.5 %collective-permute-done.10 = f32[16,256]{1,0:T(8,128)S(1)} collective-permute-done((f32[16,256]{1,0:T(8,128)S(1)}, f32[16,256]{1,0:T(8,128)S(1)}, u32[]{:S(2)}, u32[]{:S(2)}) %collective-permute-start.10) | collective-permute-done | bytes 16416 | tf_op jit(solution)/shard_map/ppermute | solution.py:71
  93.4 3.7 %collective-permute-done.11 = f32[16,256]{1,0:T(8,128)S(1)} collective-permute-done((f32[16,256]{1,0:T(8,128)S(1)}, f32[16,256]{1,0:T(8,128)S(1)}, u32[]{:S(2)}, u32[]{:S(2)}) %collective-permute-start.11) | collective-permute-done | bytes 16416 | tf_op jit(solution)/shard_map/ppermute | solution.py:71
  97.2 0.7 copy-done.9
  98.0 0.9 collective-permute-start.12
  98.9 3.2 %collective-permute-start.13 = (f32[16,256]{1,0:T(8,128)S(1)}, f32[16,256]{1,0:T(8,128)S(1)}, u32[]{:S(2)}, u32[]{:S(2)}) collective-permute-start(f32[16,256]{1,0:T(8,128)S(1)} %bitcast.298), channel_id=1, source_target_pairs={{7,0},{0,1},{1,2},{2,3},{3,4},{4,5},{5,6},{6,7},{15,8},{8,9},{9,10... | collective-permute-start | bytes 49160 | tf_op jit(solution)/shard_map/ppermute | solution.py:74
  102.1 1.4 %collective-permute-done.12 = f32[16,256]{1,0:T(8,128)S(1)} collective-permute-done((f32[16,256]{1,0:T(8,128)S(1)}, f32[16,256]{1,0:T(8,128)S(1)}, u32[]{:S(2)}, u32[]{:S(2)}) %collective-permute-start.12) | collective-permute-done | bytes 16416 | tf_op jit(solution)/shard_map/ppermute | solution.py:74
  104.0 0.7 copy-done.16
  107.0 1.5 %collective-permute-start.15 = (f32[16,256]{1,0:T(8,128)S(1)}, f32[16,256]{1,0:T(8,128)S(1)}, u32[]{:S(2)}, u32[]{:S(2)}) collective-permute-start(f32[16,256]{1,0:T(8,128)S(1)} %get-tuple-element.22), channel_id=1, source_target_pairs={{248,0},{0,8},{8,16},{16,24},{24,32},{32,40},{40,48},{48,56},{56,6... | collective-permute-start | bytes 49160 | tf_op jit(solution)/shard_map/ppermute | solution.py:71
  108.5 1.1 collective-permute-done.14
  109.6 3.4 %collective-permute-done.15 = f32[16,256]{1,0:T(8,128)S(1)} collective-permute-done((f32[16,256]{1,0:T(8,128)S(1)}, f32[16,256]{1,0:T(8,128)S(1)}, u32[]{:S(2)}, u32[]{:S(2)}) %collective-permute-start.15) | collective-permute-done | bytes 16416 | tf_op jit(solution)/shard_map/ppermute | solution.py:71
  113.2 4.1 %collective-permute-start.17 = (f32[16,256]{1,0:T(8,128)S(1)}, f32[16,256]{1,0:T(8,128)S(1)}, u32[]{:S(2)}, u32[]{:S(2)}) collective-permute-start(f32[16,256]{1,0:T(8,128)S(1)} %bitcast.296), channel_id=1, source_target_pairs={{7,0},{0,1},{1,2},{2,3},{3,4},{4,5},{5,6},{6,7},{15,8},{8,9},{9,10... | collective-permute-start | bytes 49160 | tf_op jit(solution)/shard_map/ppermute | solution.py:74
  117.3 0.6 reshape.408
  118.0 0.7 collective-permute-done.16
  119.2 1.0 fusion.51
  (207 shorter events, 20.4 us)
Async XLA Ops:
  0.6 1.2 %copy-start.6 = (f32[256,256]{1,0:T(8,128)S(1)}, f32[256,256]{1,0:T(8,128)}, u32[]{:S(2)}) copy-start(f32[256,256]{1,0:T(8,128)} %constant.185.clone) | copy-start | bytes 786436
  0.6 1.3 %copy-start.3 = (f32[16,16,256]{2,1,0:T(8,128)S(1)}, f32[16,16,256]{2,1,0:T(8,128)}, u32[]{:S(2)}) copy-start(f32[16,16,256]{2,1,0:T(8,128)} %param.21) | copy-start | bytes 786436
  1.9 0.9 copy-start.4
  3.2 1.0 copy-start.2
  4.2 8.2 %copy-start.7 = (f32[1,2,8,512]{3,2,1,0:T(8,128)S(1)}, f32[1,2,8,512]{3,2,1,0:T(8,128)}, u32[]{:S(2)}) copy-start(f32[1,2,8,512]{3,2,1,0:T(8,128)} %param.24) | copy-start | bytes 98308
  4.2 9.4 %collective-permute-start.1 = (f32[2,16,256]{2,1,0:T(8,128)S(1)}, f32[2,16,256]{2,1,0:T(8,128)S(1)}, u32[]{:S(2)}, u32[]{:S(2)}) collective-permute-start(f32[2,16,256]{2,1,0:T(8,128)S(1)} %get-tuple-element.14), channel_id=1, source_target_pairs={{248,0},{0,8},{8,16},{16,24},{24,32},{32,40},{40,48},{48,56},{56,6... | collective-permute-start | bytes 98312 | tf_op jit(solution)/shard_map/ppermute | solution.py:71
  5.9 6.5 %copy-start.12 = (s32[1,2,8,8]{3,2,1,0:T(8,128)S(1)}, s32[1,2,8,8]{3,2,1,0:T(8,128)}, u32[]{:S(2)}) copy-start(s32[1,2,8,8]{3,2,1,0:T(8,128)} %param.22) | copy-start | bytes 1540
  5.9 7.7 %collective-permute-start = (f32[2,16,256]{2,1,0:T(8,128)S(1)}, f32[2,16,256]{2,1,0:T(8,128)S(1)}, u32[]{:S(2)}, u32[]{:S(2)}) collective-permute-start(f32[2,16,256]{2,1,0:T(8,128)S(1)} %get-tuple-element.13), channel_id=1, source_target_pairs={{8,0},{16,8},{24,16},{32,24},{40,32},{48,40},{56,48},{64,56},{72,6... | collective-permute-start | bytes 98312 | tf_op jit(solution)/shard_map/ppermute | solution.py:71
  12.4 0.7 copy-start.21
  13.1 27.3 %copy-start.8 = (pred[16]{0:T(512)(128)(4,1)}, pred[16]{0:T(512)(128)(4,1)S(1)}, u32[]{:S(2)}) copy-start(pred[16]{0:T(512)(128)(4,1)S(1)} %get-tuple-element.49) | copy-start | bytes 52
  13.1 27.3 %copy-start.10 = (pred[16]{0:T(512)(128)(4,1)}, pred[16]{0:T(512)(128)(4,1)S(1)}, u32[]{:S(2)}) copy-start(pred[16]{0:T(512)(128)(4,1)S(1)} %get-tuple-element.50) | copy-start | bytes 52
  13.9 4.8 %collective-permute-start.2 = (f32[12360]{0:T(1024)S(1)}, f32[12360]{0:T(1024)S(1)}, u32[]{:S(2)}, u32[]{:S(2)}) collective-permute-start(f32[12360]{0:T(1024)S(1)} %concatenate.136), channel_id=1, source_target_pairs={{1,0},{2,1},{3,2},{4,3},{5,4},{6,5},{7,6},{0,7},{9,8},{10,9},{11,1... | collective-permute-start | bytes 148328 | tf_op jit(solution)/shard_map/ppermute | solution.py:74
  15.5 2.7 %collective-permute-start.3 = (f32[2,16,256]{2,1,0:T(8,128)S(1)}, f32[2,16,256]{2,1,0:T(8,128)S(1)}, u32[]{:S(2)}, u32[]{:S(2)}) collective-permute-start(f32[2,16,256]{2,1,0:T(8,128)S(1)} %bitcast.283), channel_id=1, source_target_pairs={{7,0},{0,1},{1,2},{2,3},{3,4},{4,5},{5,6},{6,7},{15,8},{8,9},{9,10... | collective-permute-start | bytes 98312 | tf_op jit(solution)/shard_map/ppermute | solution.py:74
  16.9 23.6 %copy-start.15 = (pred[256]{0:T(512)(128)(4,1)}, pred[256]{0:T(512)(128)(4,1)S(1)}, u32[]{:S(2)}) copy-start(pred[256]{0:T(512)(128)(4,1)S(1)} %get-tuple-element.51) | copy-start | bytes 772
  16.9 23.6 %copy-start.17 = (pred[256]{0:T(512)(128)(4,1)}, pred[256]{0:T(512)(128)(4,1)S(1)}, u32[]{:S(2)}) copy-start(pred[256]{0:T(512)(128)(4,1)S(1)} %get-tuple-element.52) | copy-start | bytes 772
  16.9 1.1 copy-start.22
  19.7 1.0 copy-start
  21.0 1.0 copy-start.1
  23.3 5.8 %collective-permute-start.4 = (f32[16,256]{1,0:T(8,128)S(1)}, f32[16,256]{1,0:T(8,128)S(1)}, u32[]{:S(2)}, u32[]{:S(2)}) collective-permute-start(f32[16,256]{1,0:T(8,128)S(1)} %get-tuple-element.37), channel_id=1, source_target_pairs={{8,0},{16,8},{24,16},{32,24},{40,32},{48,40},{56,48},{64,56},{72,6... | collective-permute-start | bytes 49160 | tf_op jit(solution)/shard_map/ppermute | solution.py:71
  28.3 5.9 %collective-permute-start.5 = (f32[16,256]{1,0:T(8,128)S(1)}, f32[16,256]{1,0:T(8,128)S(1)}, u32[]{:S(2)}, u32[]{:S(2)}) collective-permute-start(f32[16,256]{1,0:T(8,128)S(1)} %get-tuple-element.38), channel_id=1, source_target_pairs={{248,0},{0,8},{8,16},{16,24},{24,32},{32,40},{40,48},{48,56},{56,6... | collective-permute-start | bytes 49160 | tf_op jit(solution)/shard_map/ppermute | solution.py:71
  34.4 5.7 %collective-permute-start.6 = (f32[16,256]{1,0:T(8,128)S(1)}, f32[16,256]{1,0:T(8,128)S(1)}, u32[]{:S(2)}, u32[]{:S(2)}) collective-permute-start(f32[16,256]{1,0:T(8,128)S(1)} %bitcast.293), channel_id=1, source_target_pairs={{1,0},{2,1},{3,2},{4,3},{5,4},{6,5},{7,6},{0,7},{9,8},{10,9},{11,1... | collective-permute-start | bytes 49160 | tf_op jit(solution)/shard_map/ppermute | solution.py:74
  36.3 3.2 %collective-permute-start.7 = (f32[16,256]{1,0:T(8,128)S(1)}, f32[16,256]{1,0:T(8,128)S(1)}, u32[]{:S(2)}, u32[]{:S(2)}) collective-permute-start(f32[16,256]{1,0:T(8,128)S(1)} %bitcast.299), channel_id=1, source_target_pairs={{7,0},{0,1},{1,2},{2,3},{3,4},{4,5},{5,6},{6,7},{15,8},{8,9},{9,10... | collective-permute-start | bytes 49160 | tf_op jit(solution)/shard_map/ppermute | solution.py:74
  42.8 0.7 copy-start.19
  43.9 0.7 copy-start.14
  44.9 3.8 %collective-permute-start.8 = (f32[4,4,64]{2,1,0:T(4,128)S(1)}, f32[4,4,64]{2,1,0:T(4,128)S(1)}, u32[]{:S(2)}, u32[]{:S(2)}) collective-permute-start(f32[4,4,64]{2,1,0:T(4,128)S(1)} %reshape.397), channel_id=1, source_target_pairs={{7,0},{0,1},{1,2},{2,3},{3,4},{4,5},{5,6},{6,7},{15,8},{8,9},{9,10... | collective-permute-start | bytes 12296 | tf_op jit(solution)/shard_map/ppermute | solution.py:74
  47.9 4.3 %collective-permute-start.9 = (f32[4,4,64]{2,1,0:T(4,128)S(1)}, f32[4,4,64]{2,1,0:T(4,128)S(1)}, u32[]{:S(2)}, u32[]{:S(2)}) collective-permute-start(f32[4,4,64]{2,1,0:T(4,128)S(1)} %reshape.397), channel_id=1, source_target_pairs={{1,0},{2,1},{3,2},{4,3},{5,4},{6,5},{7,6},{0,7},{9,8},{10,9},{11,1... | collective-permute-start | bytes 12296 | tf_op jit(solution)/shard_map/ppermute | solution.py:74
  54.2 13.7 %all-to-all-start = ((f32[32,3,4,3]{2,1,3,0:T(4,128)}), f32[32,3,4,3]{2,1,3,0:T(4,128)S(1)}, u32[]{:S(2)}, u32[]{:S(2)}) async-start(f32[32,3,4,3]{2,1,3,0:T(4,128)} %copy.106), calls=%async_computation | async-start | bytes 393216 | tf_op jit(solution)/shard_map/all_to_all | solution.py:227
  68.8 1.8 %copy-start.5 = (f32[2,8,8,8,8]{4,3,2,1,0:T(8,128)S(1)}, f32[2,8,8,8,8]{4,3,2,1,0:T(8,128)}, u32[]{:S(2)}) copy-start(f32[2,8,8,8,8]{4,3,2,1,0:T(8,128)} %concatenate.147) | copy-start | bytes 98308
  85.9 0.7 copy-start.20
  87.2 0.7 copy-start.13
  90.4 3.1 %collective-permute-start.10 = (f32[16,256]{1,0:T(8,128)S(1)}, f32[16,256]{1,0:T(8,128)S(1)}, u32[]{:S(2)}, u32[]{:S(2)}) collective-permute-start(f32[16,256]{1,0:T(8,128)S(1)} %get-tuple-element.29), channel_id=1, source_target_pairs={{8,0},{16,8},{24,16},{32,24},{40,32},{48,40},{56,48},{64,56},{72,6... | collective-permute-start | bytes 49160 | tf_op jit(solution)/shard_map/ppermute | solution.py:71
  91.3 5.9 %collective-permute-start.11 = (f32[16,256]{1,0:T(8,128)S(1)}, f32[16,256]{1,0:T(8,128)S(1)}, u32[]{:S(2)}, u32[]{:S(2)}) collective-permute-start(f32[16,256]{1,0:T(8,128)S(1)} %get-tuple-element.30), channel_id=1, source_target_pairs={{248,0},{0,8},{8,16},{16,24},{24,32},{32,40},{40,48},{48,56},{56,6... | collective-permute-start | bytes 49160 | tf_op jit(solution)/shard_map/ppermute | solution.py:71
  97.2 0.7 copy-start.9
  97.2 0.7 copy-start.11
  98.0 5.5 %collective-permute-start.12 = (f32[16,256]{1,0:T(8,128)S(1)}, f32[16,256]{1,0:T(8,128)S(1)}, u32[]{:S(2)}, u32[]{:S(2)}) collective-permute-start(f32[16,256]{1,0:T(8,128)S(1)} %bitcast.297), channel_id=1, source_target_pairs={{1,0},{2,1},{3,2},{4,3},{5,4},{6,5},{7,6},{0,7},{9,8},{10,9},{11,1... | collective-permute-start | bytes 49160 | tf_op jit(solution)/shard_map/ppermute | solution.py:74
  98.9 4.6 %collective-permute-start.13 = (f32[16,256]{1,0:T(8,128)S(1)}, f32[16,256]{1,0:T(8,128)S(1)}, u32[]{:S(2)}, u32[]{:S(2)}) collective-permute-start(f32[16,256]{1,0:T(8,128)S(1)} %bitcast.298), channel_id=1, source_target_pairs={{7,0},{0,1},{1,2},{2,3},{3,4},{4,5},{5,6},{6,7},{15,8},{8,9},{9,10... | collective-permute-start | bytes 49160 | tf_op jit(solution)/shard_map/ppermute | solution.py:74
  103.9 0.7 copy-start.16
  103.9 0.7 copy-start.18
  107.0 2.7 %collective-permute-start.14 = (f32[16,256]{1,0:T(8,128)S(1)}, f32[16,256]{1,0:T(8,128)S(1)}, u32[]{:S(2)}, u32[]{:S(2)}) collective-permute-start(f32[16,256]{1,0:T(8,128)S(1)} %get-tuple-element.21), channel_id=1, source_target_pairs={{8,0},{16,8},{24,16},{32,24},{40,32},{48,40},{56,48},{64,56},{72,6... | collective-permute-start | bytes 49160 | tf_op jit(solution)/shard_map/ppermute | solution.py:71
  107.0 6.0 %collective-permute-start.15 = (f32[16,256]{1,0:T(8,128)S(1)}, f32[16,256]{1,0:T(8,128)S(1)}, u32[]{:S(2)}, u32[]{:S(2)}) collective-permute-start(f32[16,256]{1,0:T(8,128)S(1)} %get-tuple-element.22), channel_id=1, source_target_pairs={{248,0},{0,8},{8,16},{16,24},{24,32},{32,40},{40,48},{48,56},{56,6... | collective-permute-start | bytes 49160 | tf_op jit(solution)/shard_map/ppermute | solution.py:71
  113.2 5.5 %collective-permute-start.16 = (f32[16,256]{1,0:T(8,128)S(1)}, f32[16,256]{1,0:T(8,128)S(1)}, u32[]{:S(2)}, u32[]{:S(2)}) collective-permute-start(f32[16,256]{1,0:T(8,128)S(1)} %bitcast.294), channel_id=1, source_target_pairs={{1,0},{2,1},{3,2},{4,3},{5,4},{6,5},{7,6},{0,7},{9,8},{10,9},{11,1... | collective-permute-start | bytes 49160 | tf_op jit(solution)/shard_map/ppermute | solution.py:74
  113.2 5.5 %collective-permute-start.17 = (f32[16,256]{1,0:T(8,128)S(1)}, f32[16,256]{1,0:T(8,128)S(1)}, u32[]{:S(2)}, u32[]{:S(2)}) collective-permute-start(f32[16,256]{1,0:T(8,128)S(1)} %bitcast.296), channel_id=1, source_target_pairs={{7,0},{0,1},{1,2},{2,3},{3,4},{4,5},{5,6},{6,7},{15,8},{8,9},{9,10... | collective-permute-start | bytes 49160 | tf_op jit(solution)/shard_map/ppermute | solution.py:74
